TPU v7x, 512 devices: a whole 4x8x8 slice. The times are simulated.
512 devices in a mesh: blk: 32 (over y, z_hi), kv: 16 (over z_lo, x, core).
Axes of the slice: x: 4, y: 8, z: 8 (z_hi: 4, z_lo: 2; z = z_hi * 2 + z_lo), core: 2. Of those that a mesh axis runs over, the one named last changes fastest.
Arguments:
- cache_entries: bfloat16 [65536, 8, 256], P(('kv', 'blk'))
- recompute_input: bfloat16 [4096, 4096], P('kv', 'blk'), may hold values from -6 to 6
- norm_gain: bfloat16 [4096], replicated, may hold values from 0.099609375 to 1.8984375
- w_query: bfloat16 [4096, 4096], P(None, 'blk'), may hold values from -0.25 to 0.25
- w_keyval: bfloat16 [4096, 2048], P('blk'), may hold values from -0.09375 to 0.09375
- w_out: bfloat16 [4096, 4096], P('blk'), may hold values from -0.09375 to 0.09375
- rotate_offsets: int32 [64], replicated, may hold values from 0 to 65535
- span_order: int32 [64], replicated, may hold values from 0 to 63, as said below
- tenant_of_span: int32 [64], replicated, may hold values from 0 to 3, never falling along the last dimension, each value on 1 to 32 neighbouring positions
- recompute_pos: int32 [4096], replicated, may hold values from 0 to 4095, as said below
- recompute_count: int32 [16], replicated, may hold values from 1 to 256, as said below
Outputs:
- attention_out: bfloat16 [4096, 4096], P('kv', 'blk')
Inputs may be any that keep to these rules, and one draw needn't show every extreme that they name: `span_order`: each aligned block of 4 entries is a permutation of the block slots of that same block. `tenant_of_span`: tenants never fall along the block slots; there are 4 tenants, one of exactly 32 blocks. `recompute_pos`: the 256 entries of each shard are distinct. `recompute_count`: at least one shard has all 256 slots live.
All inputs are finite; a program needn't handle non-finite values.
Results may differ from a plain program's by a relative error of at most 0.035.
Values may be sent and summed in bfloat16 or wider, within the bound.
No kernel may reach another device: no remote copies, remote signals or barrier semaphores. Data moves between devices by JAX's collectives and lax.ppermute only.
A program may use at most 64 MiB of HBM per device.

v0:
```python
import math

import jax
import jax.numpy as jnp
import numpy as np
from jax import lax
from jax.sharding import PartitionSpec as P

QH = 32
KVH = 8
HEAD_DIM = 128
WINDOW = 4096
SPAN = 1024


NEG_FILL = -1e30
ROPE_BASE = 10000.0
NORM_EPS = 1e-05


def shifted(shard, axis, by):
    devices = lax.axis_size(axis)
    pairs = [(i, i + by) for i in range(devices) if 0 <= i + by < devices]
    return lax.ppermute(shard, axis, pairs)


def rotate_half(values, positions):
    half = values.shape[-1] // 2
    inverse = ROPE_BASE ** (-(jnp.arange(half, dtype=jnp.float32) * 2.0 / values.shape[-1]))
    angles = positions.astype(jnp.float32)[:, None] * inverse[None, :]
    shape = (positions.shape[0],) + (1,) * (values.ndim - 2) + (half,)
    cosine = jnp.cos(angles).reshape(shape)
    sine = jnp.sin(angles).reshape(shape)
    first = values[..., :half]
    second = values[..., half:]
    return jnp.concatenate(
        [first * cosine - second * sine, second * cosine + first * sine], axis=-1
    )


def tenant_lookup(positions, tenant_of_span):
    span_ids = positions // SPAN
    table_index = jnp.arange(tenant_of_span.shape[0], dtype=jnp.int32)
    match = span_ids[:, None] == table_index[None, :]
    return jnp.sum(jnp.where(match, tenant_of_span[None, :], 0), axis=1)


def attend_part(queries, query_pos, query_tenant, keys, values, key_pos, key_tenant):
    scale = 1.0 / math.sqrt(keys.shape[-1])
    scores = jnp.einsum("cgh,sh->gcs", queries, keys, preferred_element_type=jnp.float32) * scale
    gap = query_pos[:, None] - key_pos[None, :]
    allowed = (
        (query_tenant[:, None] == key_tenant[None, :])
        & (gap >= 0)
        & (gap < WINDOW)
        & (key_pos[None, :] >= 0)
    )
    masked = jnp.where(allowed[None], scores, NEG_FILL)
    row_max = jnp.max(masked, axis=2)
    weights = jnp.where(allowed[None], jnp.exp(masked - row_max[..., None]), 0.0)
    totals = jnp.sum(weights, axis=2)
    summed = jnp.einsum(
        "gcs,sh->gch", weights.astype(jnp.bfloat16), values, preferred_element_type=jnp.float32
    )
    return (row_max, totals, summed)


def combine_parts(first, second):
    top = jnp.maximum(first[0], second[0])
    scale_one = jnp.exp(first[0] - top)
    scale_two = jnp.exp(second[0] - top)
    totals = first[1] * scale_one + second[1] * scale_two
    summed = first[2] * scale_one[..., None] + second[2] * scale_two[..., None]
    return summed / totals[..., None]


def local(
    cache_entries,
    recompute_input,
    norm_gain,
    w_query,
    w_keyval,
    w_out,
    rotate_offsets,
    span_order,
    tenant_of_span,
    recompute_pos,
    recompute_count,
):
    blk_count = lax.axis_size("blk")
    kv_index = lax.axis_index("kv")
    blk_index = lax.axis_index("blk")
    block_rows = cache_entries.shape[0]
    shard_len = block_rows * blk_count
    slots = recompute_input.shape[0]
    own_cols = recompute_input.shape[1]
    width = norm_gain.shape[0]
    local_heads = w_query.shape[1] // HEAD_DIM
    spans_here = shard_len // SPAN
    own_group = blk_index * local_heads // (QH // KVH)
    targets = np.arange(blk_count) * local_heads // (QH // KVH)
    wide = lax.all_gather(recompute_input, "blk", axis=1, tiled=True).astype(jnp.float32)
    gains = norm_gain.astype(jnp.float32)
    scaled = (wide * gains[None, :]).astype(jnp.bfloat16)
    query_acc = jnp.dot(scaled, w_query, preferred_element_type=jnp.float32)
    square_acc = jnp.sum(wide * wide, axis=1)
    own_gain = lax.dynamic_slice_in_dim(norm_gain, blk_index * own_cols, own_cols, 0).astype(
        jnp.float32
    )
    own_scaled = (recompute_input.astype(jnp.float32) * own_gain[None, :]).astype(jnp.bfloat16)
    pair_term = jnp.dot(own_scaled, w_keyval, preferred_element_type=jnp.float32)
    pair_sum = lax.psum(pair_term.astype(jnp.bfloat16), "blk").astype(jnp.float32)
    inv_rms = lax.rsqrt(square_acc / width + NORM_EPS)
    pair_heads = (pair_sum * inv_rms[:, None]).reshape(slots, KVH, 2 * HEAD_DIM)
    own_pair = lax.dynamic_index_in_dim(pair_heads, own_group, 1, keepdims=False)
    own_pos = lax.dynamic_slice_in_dim(recompute_pos, kv_index * slots, slots, 0)
    own_count = lax.dynamic_index_in_dim(recompute_count, kv_index, 0, keepdims=False)
    live = jnp.arange(slots, dtype=jnp.int32) < own_count
    query_pos = kv_index * shard_len + own_pos
    fresh_keys = rotate_half(own_pair[:, :HEAD_DIM], query_pos).astype(jnp.bfloat16)
    fresh_values = own_pair[:, HEAD_DIM:].astype(jnp.bfloat16)
    queries = rotate_half(
        (query_acc * inv_rms[:, None]).reshape(slots, local_heads, HEAD_DIM), query_pos
    ).astype(jnp.bfloat16)
    arrived = lax.all_to_all(
        jnp.take(cache_entries, targets, axis=1), "blk", split_axis=1, concat_axis=0, tiled=True
    )
    stored = arrived.reshape(shard_len, 2 * HEAD_DIM)
    offsets_here = lax.dynamic_slice_in_dim(rotate_offsets, kv_index * spans_here, spans_here, 0)
    row_shifts = jnp.repeat(offsets_here, SPAN, total_repeat_length=shard_len)
    turned_rows = rotate_half(stored[:, :HEAD_DIM].astype(jnp.float32), row_shifts).astype(
        jnp.bfloat16
    )
    stored = jnp.concatenate([turned_rows, stored[:, HEAD_DIM:]], axis=-1)
    local_order = (
        lax.dynamic_slice_in_dim(span_order, kv_index * spans_here, spans_here, 0)
        - kv_index * spans_here
    )
    ordered = jnp.take(stored.reshape(spans_here, SPAN, 2 * HEAD_DIM), local_order, axis=0).reshape(
        shard_len, 2 * HEAD_DIM
    )
    place = jnp.where(live, own_pos, shard_len)
    merged = ordered.at[place].set(jnp.concatenate([fresh_keys, fresh_values], axis=1), mode="drop")
    key_pos = kv_index * shard_len + jnp.arange(shard_len, dtype=jnp.int32)
    key_tenant = tenant_lookup(key_pos, tenant_of_span)
    query_tenant = tenant_lookup(query_pos, tenant_of_span)
    own_part = attend_part(
        queries,
        query_pos,
        query_tenant,
        merged[:, :HEAD_DIM],
        merged[:, HEAD_DIM:],
        key_pos,
        key_tenant,
    )
    prior = shifted(merged, "kv", 1)
    prior_pos = key_pos - shard_len
    prior_part = attend_part(
        queries,
        query_pos,
        query_tenant,
        prior[:, :HEAD_DIM],
        prior[:, HEAD_DIM:],
        prior_pos,
        tenant_lookup(prior_pos, tenant_of_span),
    )
    heads_out = combine_parts(own_part, prior_part).astype(jnp.bfloat16)
    out_rows = w_out.reshape(local_heads, HEAD_DIM, width)
    term = jnp.einsum("gch,ghd->cd", heads_out, out_rows, preferred_element_type=jnp.float32)
    summed_out = lax.psum_scatter(
        term.astype(jnp.bfloat16), "blk", scatter_dimension=1, tiled=True
    ).astype(jnp.float32)
    return jnp.where(live[:, None], summed_out, 0.0).astype(jnp.bfloat16)


def solution(mesh):
    placed = (
        P(("kv", "blk"), None, None),
        P("kv", "blk"),
        P(),
        P(None, "blk"),
        P("blk", None),
        P("blk", None),
        P(),
        P(),
        P(),
        P(),
        P(),
    )
    return jax.shard_map(
        local, mesh=mesh, in_specs=placed, out_specs=P("kv", "blk"), check_vma=False
    )
```

profile of v0, /device:TPU:6, one launch (start us, length us, event | category | flops | bytes accessed | tf_op | source)
XLA Modules:
  0.0 771.2 jit_solution(2034141246028215434)
XLA Ops:
  7.9 6.6 gather_fusion
  14.5 2.5 copy.21
  17.0 16.1 %all-to-all-start = ((bf16[128,32,256]{2,0,1:T(8,128)(2,1)}), bf16[128,32,256]{2,0,1:T(8,128)(2,1)S(1)}, u32[]{:S(2)}, u32[]{:S(2)}) async-start(bf16[128,32,256]{2,0,1:T(8,128)(2,1)} %copy.21), calls=%async_computation | async-start | bytes 4194304 | tf_op jit(solution)/shard_map/all_to_all | solution.py:125
  33.3 2.4 convolution_convert_fusion.1
  36.7 1.4 and_select_fusion
  39.0 2.6 select_convert_fusion.1
  41.5 101.7 %all-gather.2.cloned.1.call-done = bf16[256,4096]{1,0:T(8,128)(2,1)} async-done(((bf16[256,128]{1,0:T(8,128)(2,1)}), bf16[256,4096]{1,0:T(8,128)(2,1)}) %all-gather.2.cloned.1.call-update) | async-done | bytes 2097168 | tf_op jit(solution)/shard_map/all_gather | solution.py:102
  143.2 2.1 fusion.4
  145.3 315.9 %all-reduce.2.cloned.1.call-done = bf16[256,2048]{1,0:T(8,128)(2,1)} async-done(((bf16[256,2048]{1,0:T(8,128)(2,1)}), bf16[256,2048]{1,0:T(8,128)(2,1)}) %all-reduce.2.cloned.1.call-update) | async-done | bytes 1048592 | tf_op jit(solution)/shard_map/psum | solution.py:112
  461.2 2.8 convert_multiply_fusion.2
  464.0 2.9 copy.27
  466.9 1.0 dynamic-slice_bitcast_fusion
  468.3 1.5 fusion.107
  469.8 1.5 copy.30
  471.5 5.4 fusion.57
  477.3 1.5 copy.24
  478.9 3.5 pad_maximum_fusion
  482.3 2.3 gather_fusion.1
  484.6 1.9 bitcast_select_fusion
  486.5 4.8 scatter_fusion
  491.3 2.1 collective-permute-start
  494.0 2.7 fusion.36
  497.0 3.5 fusion.109
  500.6 18.3 %collective-permute-done = bf16[4096,256]{1,0:T(8,128)(2,1)S(1)} collective-permute-done((bf16[4096,256]{1,0:T(8,128)(2,1)}, bf16[4096,256]{1,0:T(8,128)(2,1)S(1)}, u32[]{:S(2)}, u32[]{:S(2)}) %collective-permute-start) | collective-permute-done | bytes 2097184 | tf_op jit(solution)/shard_map/ppermute | solution.py:24
  518.9 1.8 fusion.110
  520.7 5.8 fusion.12
  526.5 3.0 fusion.39
  529.5 5.8 convolution_convert_fusion
  535.3 2.5 copy.28
  538.5 224.5 %reduce-scatter.4.cloned.1.call-done = bf16[128,256]{1,0:T(8,128)(2,1)} async-done(((bf16[4096,256]{1,0:T(8,128)(2,1)}), bf16[128,256]{1,0:T(8,128)(2,1)}) %reduce-scatter.4.cloned.1.call-update) | async-done | bytes 65552
  763.0 0.9 copy.29
  763.9 0.7 select_convert_fusion
  (60 shorter events, 6.0 us)
Async XLA Ops:
  6.5 523.0 %copy-start = (bf16[128,4096]{1,0:T(8,128)(2,1)S(1)}, bf16[128,4096]{1,0:T(8,128)(2,1)}, u32[]{:S(2)}) copy-start(bf16[128,4096]{1,0:T(8,128)(2,1)} %param.19) | copy-start | bytes 3145732
  6.5 136.7 %all-gather.2.cloned.1.call-start = ((), (), s32[]{:S(2)}) async-start(), calls=%async_computation.3 | async-start | bytes 2162688 | tf_op jit(solution)/shard_map/all_gather | solution.py:102
  14.5 18.7 %copy-start.4 = (bf16[4096]{0:T(1024)(128)(2,1)S(1)}, bf16[4096]{0:T(1024)(128)(2,1)}, u32[]{:S(2)}) copy-start(bf16[4096]{0:T(1024)(128)(2,1)} %param.16) | copy-start | bytes 24580
  14.5 18.8 %copy-start.3 = (bf16[256,128]{1,0:T(8,128)(2,1)S(1)}, bf16[256,128]{1,0:T(8,128)(2,1)}, u32[]{:S(2)}) copy-start(bf16[256,128]{1,0:T(8,128)(2,1)} %param.15) | copy-start | bytes 196612
  17.0 19.0 %copy-start.11 = (s32[16]{0:T(128)S(1)}, s32[16]{0:T(128)}, u32[]{:S(2)}) copy-start(s32[16]{0:T(128)} %param.24) | copy-start | bytes 196
  17.0 19.6 %copy-start.9 = (s32[64]{0:T(128)S(1)}, s32[64]{0:T(128)}, u32[]{:S(2)}) copy-start(s32[64]{0:T(128)} %param.21) | copy-start | bytes 772
  17.0 21.2 %copy-start.12 = (s32[64]{0:T(128)S(1)}, s32[64]{0:T(128)}, u32[]{:S(2)}) copy-start(s32[64]{0:T(128)} %param.20) | copy-start | bytes 772
  17.0 21.9 %copy-start.5 = (pred[4096]{0:T(1024)(128)(4,1)S(1)}, pred[4096]{0:T(1024)(128)(4,1)}, u32[]{:S(2)}) copy-start(pred[4096]{0:T(1024)(128)(4,1)} %constant.245) | copy-start | bytes 12292
  17.0 21.9 %copy-start.6 = (pred[4096]{0:T(1024)(128)(4,1)S(1)}, pred[4096]{0:T(1024)(128)(4,1)}, u32[]{:S(2)}) copy-start(pred[4096]{0:T(1024)(128)(4,1)} %constant.244) | copy-start | bytes 12292
  17.0 21.9 %copy-start.7 = (pred[4096]{0:T(1024)(128)(4,1)S(1)}, pred[4096]{0:T(1024)(128)(4,1)}, u32[]{:S(2)}) copy-start(pred[4096]{0:T(1024)(128)(4,1)} %constant.243) | copy-start | bytes 12292
  17.0 451.3 %all-to-all-start = ((bf16[128,32,256]{2,0,1:T(8,128)(2,1)}), bf16[128,32,256]{2,0,1:T(8,128)(2,1)S(1)}, u32[]{:S(2)}, u32[]{:S(2)}) async-start(bf16[128,32,256]{2,0,1:T(8,128)(2,1)} %copy.21), calls=%async_computation | async-start | bytes 4194304 | tf_op jit(solution)/shard_map/all_to_all | solution.py:125
  33.1 428.1 %all-reduce.2.cloned.1.call-start = ((), (), s32[]{:S(2)}) async-start(), calls=%async_computation.2 | async-start | bytes 2097152 | tf_op jit(solution)/shard_map/psum | solution.py:112
  35.7 727.2 %reduce-scatter.4.cloned.1.call-start = ((), (), s32[]{:S(2)}) async-start(), calls=%async_computation.4 | async-start | bytes 2162688
  484.6 8.9 %copy-start.8 = (s32[64]{0:T(128)S(1)}, s32[64]{0:T(128)}, u32[]{:S(2)}) copy-start(s32[64]{0:T(128)} %param.22) | copy-start | bytes 772
  491.3 27.6 %collective-permute-start = (bf16[4096,256]{1,0:T(8,128)(2,1)}, bf16[4096,256]{1,0:T(8,128)(2,1)S(1)}, u32[]{:S(2)}, u32[]{:S(2)}) collective-permute-start(bf16[4096,256]{1,0:T(8,128)(2,1)} %scatter_fusion), channel_id=1, source_target_pairs={{0,1},{1,2},{2,3},{3,4},{4,5},{5,6},{6,7},{7,8},{8,9},{9,10},{10,1... | collective-permute-start | bytes 6291464 | tf_op jit(solution)/shard_map/ppermute | solution.py:24
  518.9 1.8 copy-start.10
  520.6 5.8 copy-start.2
  520.6 5.8 copy-start.1
Sparse Core Ops, SparseCore 0:
  10.4 132.7 all-gather.1
  146.1 315.0 all-reduce.1
  537.9 225.0 reduce-scatter.3
where the time goes:
time: 772 us; the launch traced here: 771 us
  waiting for transfers between devices  661 us (86%)
  local copies, waits for them, and re-layouts  29.9 us (4%)
  other arithmetic  29 us (4%)
  matrix products  19.2 us (2%)
  starting transfers between devices  18.5 us (2%)
  between operations  13.5 us (2%)
    psum x1, waiting for transfers between devices, local(): lax.psum(pair_term.astype(jnp.bfloat16), 'blk').astype(jnp.float32)  316 us
    unnamed x4, waiting for transfers between devices  225 us
    all_gather x1, waiting for transfers between devices, local(): lax.all_gather(recompute_input, 'blk', axis=1, tiled=True)  102 us
    ppermute x1, waiting for transfers between devices, shifted(): return lax.ppermute(shard, axis, pairs)  18.3 us
    all_to_all x1, starting transfers between devices, local(): lax.all_to_all(jnp.take(cache_entries, targets, axis=1), 'blk', split_axi...  16.1 us
  transfers between devices with their start and end apart: 5, of which 4 were waited for; matrix products, arithmetic and copies ran while one was open for 4% of the time, Pallas kernels for 0%

commit v1 on v0

--- a/solution.py
+++ b/solution.py
@@ -22,6 +22,19 @@
     devices = lax.axis_size(axis)
     pairs = [(i, i + by) for i in range(devices) if 0 <= i + by < devices]
     return lax.ppermute(shard, axis, pairs)
+
+
+def group_gather(piece, axis, size):
+    devices = lax.axis_size(axis)
+    place = lax.axis_index(axis) % size
+    pieces = [piece]
+    for step in range(1, size):
+        pairs = [(i, i - i % size + (i % size + step) % size) for i in range(devices)]
+        pieces.append(lax.ppermute(piece, axis, pairs))
+    stacked = jnp.stack(pieces)
+    order = (place - jnp.arange(size, dtype=jnp.int32)) % size
+    picked = jnp.take(stacked, order, axis=0)
+    return jnp.concatenate([picked[c] for c in range(size)], axis=-1)
 
 
 def rotate_half(values, positions):
@@ -99,20 +112,22 @@
     spans_here = shard_len // SPAN
     own_group = blk_index * local_heads // (QH // KVH)
     targets = np.arange(blk_count) * local_heads // (QH // KVH)
-    wide = lax.all_gather(recompute_input, "blk", axis=1, tiled=True).astype(jnp.float32)
+    spread = jnp.broadcast_to(recompute_input[:, None, :], (slots, blk_count, own_cols))
+    wide = (
+        lax.all_to_all(spread, "blk", 1, 1, tiled=True).reshape(slots, width).astype(jnp.float32)
+    )
     gains = norm_gain.astype(jnp.float32)
     scaled = (wide * gains[None, :]).astype(jnp.bfloat16)
     query_acc = jnp.dot(scaled, w_query, preferred_element_type=jnp.float32)
     square_acc = jnp.sum(wide * wide, axis=1)
-    own_gain = lax.dynamic_slice_in_dim(norm_gain, blk_index * own_cols, own_cols, 0).astype(
-        jnp.float32
-    )
-    own_scaled = (recompute_input.astype(jnp.float32) * own_gain[None, :]).astype(jnp.bfloat16)
-    pair_term = jnp.dot(own_scaled, w_keyval, preferred_element_type=jnp.float32)
-    pair_sum = lax.psum(pair_term.astype(jnp.bfloat16), "blk").astype(jnp.float32)
+    pair_cols = w_keyval.shape[1] // blk_count
+    group_size = 2 * HEAD_DIM // pair_cols
+    kv_cols = lax.all_to_all(
+        w_keyval.reshape(own_cols, blk_count, pair_cols), "blk", 1, 0, tiled=True
+    ).reshape(width, pair_cols)
     inv_rms = lax.rsqrt(square_acc / width + NORM_EPS)
-    pair_heads = (pair_sum * inv_rms[:, None]).reshape(slots, KVH, 2 * HEAD_DIM)
-    own_pair = lax.dynamic_index_in_dim(pair_heads, own_group, 1, keepdims=False)
+    pair_piece = jnp.dot(scaled, kv_cols, preferred_element_type=jnp.float32) * inv_rms[:, None]
+    own_pair = group_gather(pair_piece, "blk", group_size)
     own_pos = lax.dynamic_slice_in_dim(recompute_pos, kv_index * slots, slots, 0)
     own_count = lax.dynamic_index_in_dim(recompute_count, kv_index, 0, keepdims=False)
     live = jnp.arange(slots, dtype=jnp.int32) < own_count
@@ -167,9 +182,9 @@
     heads_out = combine_parts(own_part, prior_part).astype(jnp.bfloat16)
     out_rows = w_out.reshape(local_heads, HEAD_DIM, width)
     term = jnp.einsum("gch,ghd->cd", heads_out, out_rows, preferred_element_type=jnp.float32)
-    summed_out = lax.psum_scatter(
-        term.astype(jnp.bfloat16), "blk", scatter_dimension=1, tiled=True
-    ).astype(jnp.float32)
+    term_blocks = term.astype(jnp.bfloat16).reshape(slots, blk_count, own_cols)
+    arrived_terms = lax.all_to_all(term_blocks, "blk", 1, 1, tiled=True)
+    summed_out = jnp.sum(arrived_terms.astype(jnp.float32), axis=1)
     return jnp.where(live[:, None], summed_out, 0.0).astype(jnp.bfloat16)
 
 

time: 772 us -> 321 us (0.42)
  the two profiles are of different devices: /device:TPU:6 before, /device:TPU:7 now
where the time goes in v1:
time: 321 us; the launch traced here: 320 us
  waiting for transfers between devices  140 us (44%)
  starting transfers between devices  54.8 us (17%)
  local copies, waits for them, and re-layouts  45.4 us (14%)
  other arithmetic  33.3 us (10%)
  blocking collectives  32.5 us (10%)
  matrix products  13.3 us (4%)
    all_to_all x1, waiting for transfers between devices, local(): arrived_terms = lax.all_to_all(term_blocks, 'blk', 1, 1, tiled=True)  58 us
    all_to_all x1, waiting for transfers between devices, local(): lax.all_to_all(spread, 'blk', 1, 1, tiled=True).reshape(slots, width)  37.9 us
    all_to_all x1, blocking collectives, local(): lax.all_to_all(w_keyval.reshape(own_cols, blk_count, pair_cols), 'blk', 1...  32.5 us
    all_to_all x1, waiting for transfers between devices, local(): lax.all_to_all(jnp.take(cache_entries, targets, axis=1), 'blk', split_axi...  24.8 us
    ppermute x1, waiting for transfers between devices, shifted(): return lax.ppermute(shard, axis, pairs)  19 us
    all_to_all x1, starting transfers between devices, local(): lax.all_to_all(jnp.take(cache_entries, targets, axis=1), 'blk', split_axi...  17.2 us
    ppermute x3, starting transfers between devices, group_gather(): pieces.append(lax.ppermute(piece, axis, pairs))  13.3 us
    gather x2, local copies, waits for them, and re-layouts, local(): jnp.take(cache_entries, targets, axis=1)  12.1 us
  transfers between devices with their start and end apart: 7, of which 4 were waited for; matrix products, arithmetic and copies ran while one was open for 18% of the time, Pallas kernels for 0%

profile of v1, /device:TPU:7, one launch (start us, length us, event | category | flops | bytes accessed | tf_op | source)
XLA Modules:
  0.0 319.6 jit_solution(15136996718779272314)
XLA Ops:
  1.4 32.5 %all_to_all.40 = bf16[128,32,64]{0,2,1:T(8,128)(2,1)S(1)} all-to-all(bf16[128,32,64]{0,2,1:T(8,128)(2,1)S(1)} %bitcast.111), channel_id=1, replica_groups=mesh['blk'=32,'kv'=16] {'blk'}, dimensions={1} | all-to-all | bytes 1048576 | tf_op jit(solution)/shard_map/all_to_all | solution.py:125
  34.0 2.6 broadcast_in_dim.160
  36.6 7.4 %all-to-all-start.1 = ((bf16[256,32,128]{2,0,1:T(8,128)(2,1)}), bf16[256,32,128]{2,0,1:T(8,128)(2,1)}, u32[]{:S(2)}, u32[]{:S(2)}) async-start(bf16[256,32,128]{2,0,1:T(8,128)(2,1)} %broadcast_in_dim.160), calls=%async_computation.1 | async-start | bytes 4194304 | tf_op jit(solution)/shard_map/all_to_all | solution.py:117
  44.1 7.9 %gather_fusion = bf16[32,128,256]{2,0,1:T(8,128)(2,1)} fusion(bf16[128,8,256]{2,1,0:T(8,128)(2,1)S(1)} %copy-done.1, s32[1024]{0:T(1024)S(1)} %pad_clamp_fusion.2), kind=kCustom, calls=%fused_computation | custom fusion | bytes 4194432 | tf_op jit(solution)/shard_map/jit(_take)/gather | solution.py:141
  52.1 4.1 %copy.34 = bf16[128,32,256]{2,0,1:T(8,128)(2,1)} copy(bf16[128,32,256]{2,1,0:T(8,128)(2,1)} %bitcast.108) | data formatting | bytes 4194304 | tf_op jit(solution)/shard_map/jit(_take)/gather | solution.py:141
  56.3 37.9 %all-to-all-done.1 = bf16[256,32,128]{2,0,1:T(8,128)(2,1)} async-done(((bf16[256,32,128]{2,0,1:T(8,128)(2,1)}), bf16[256,32,128]{2,0,1:T(8,128)(2,1)}, u32[]{:S(2)}, u32[]{:S(2)}) %all-to-all-start.1) | async-done | bytes 2097184 | tf_op jit(solution)/shard_map/all_to_all | solution.py:117
  94.1 17.2 %all-to-all-start = ((bf16[128,32,256]{2,0,1:T(8,128)(2,1)}), bf16[128,32,256]{2,0,1:T(8,128)(2,1)}, u32[]{:S(2)}, u32[]{:S(2)}) async-start(bf16[128,32,256]{2,0,1:T(8,128)(2,1)} %copy.34), calls=%async_computation | async-start | bytes 4194304 | tf_op jit(solution)/shard_map/all_to_all | solution.py:140
  112.1 2.0 and_select_fusion.2
  117.8 2.6 select_convert_fusion.1
  121.6 3.3 %copy.38 = bf16[256,32,128]{0,2,1:T(8,128)(2,1)S(1)} copy(bf16[256,32,128]{2,0,1:T(8,128)(2,1)} %all-to-all-done.1) | data formatting | bytes 4194304 | tf_op jit(solution)/shard_map/all_to_all | solution.py:117
  126.3 5.2 %collective-permute-start.2 = (f32[256,64]{0,1:T(8,128)S(1)}, f32[256,64]{0,1:T(8,128)S(1)}, u32[]{:S(2)}, u32[]{:S(2)}) collective-permute-start(f32[256,64]{0,1:T(8,128)S(1)} %convolution_multiply_fusion.3), channel_id=1, source_target_pairs={{0,48},{16,0},{32,16},{48,32},{64,112},{80,64},{96,80},{112,96},{1... | collective-permute-start | bytes 196616 | tf_op jit(solution)/shard_map/ppermute | solution.py:33
  131.5 4.0 %collective-permute-start.1 = (f32[256,64]{0,1:T(8,128)S(1)}, f32[256,64]{0,1:T(8,128)S(1)}, u32[]{:S(2)}, u32[]{:S(2)}) collective-permute-start(f32[256,64]{0,1:T(8,128)S(1)} %convolution_multiply_fusion.3), channel_id=1, source_target_pairs={{0,32},{16,48},{32,0},{48,16},{64,96},{80,112},{96,64},{112,80},{1... | collective-permute-start | bytes 196616 | tf_op jit(solution)/shard_map/ppermute | solution.py:33
  135.5 4.2 %collective-permute-start = (f32[256,64]{0,1:T(8,128)S(1)}, f32[256,64]{0,1:T(8,128)S(1)}, u32[]{:S(2)}, u32[]{:S(2)}) collective-permute-start(f32[256,64]{0,1:T(8,128)S(1)} %convolution_multiply_fusion.3), channel_id=1, source_target_pairs={{0,16},{16,32},{32,48},{48,0},{64,80},{80,96},{96,112},{112,64},{1... | collective-permute-start | bytes 196616 | tf_op jit(solution)/shard_map/ppermute | solution.py:33
  139.7 24.8 %all-to-all-done = bf16[128,32,256]{2,0,1:T(8,128)(2,1)} async-done(((bf16[128,32,256]{2,0,1:T(8,128)(2,1)}), bf16[128,32,256]{2,0,1:T(8,128)(2,1)}, u32[]{:S(2)}, u32[]{:S(2)}) %all-to-all-start) | async-done | bytes 2097184 | tf_op jit(solution)/shard_map/all_to_all | solution.py:140
  164.5 3.0 fusion.105
  167.5 2.3 copy.43
  171.2 5.0 %fusion.47 = (bf16[4096,64]{0,1:T(8,128)(2,1)}, bf16[4096,64]{0,1:T(8,128)(2,1)}) fusion(f32[4096,128]{0,1:T(8,128)S(1)} %convert_element_type.62, f32[64]{0:T(128)S(1)} %negate_power_fusion, f32[4096]{0:T(1024)S(1)} %select_convert_fusion.1), kind=kLoop, calls=%fused_computation.59 | loop fusion | flops 2359296 | bytes 3162368 | tf_op jit(solution)/shard_map/convert.13
  176.2 2.3 copy.36
  178.5 2.4 copy.37
  180.9 4.1 %pad_maximum_fusion = bf16[4096,256]{1,0:T(8,128)(2,1)} fusion(bf16[4096,128]{1,0:T(8,128)(2,1)} %get-tuple-element.35, bf16[4096,64]{1,0:T(8,128)(2,1)} %copy.37, bf16[4096,64]{1,0:T(8,128)(2,1)} %copy.36), kind=kLoop, calls=%fused_computation.37 | loop fusion | flops 6291456 | bytes 4194304 | tf_op jit(solution)/shard_map/concatenate | solution.py:149
  185.1 3.6 %gather_fusion.1 = bf16[4,1024,256]{2,1,0:T(8,128)(2,1)} fusion(bf16[4,1024,256]{2,1,0:T(8,128)(2,1)} %bitcast.107, s32[1024]{0:T(1024)S(1)} %pad_clamp_fusion.1), kind=kCustom, calls=%fused_computation.1 | custom fusion | bytes 4194320 | tf_op jit(solution)/shard_map/jit(_take)/gather | solution.py:154
  188.6 2.9 bitcast_select_fusion
  196.6 4.9 %scatter_fusion = bf16[4096,256]{1,0:T(8,128)(2,1)} fusion(bf16[4096,256]{1,0:T(8,128)(2,1)} %bitcast_select_fusion, s32[256]{0:T(256)} %get-tuple-element.42, bf16[256,256]{1,0:T(8,128)(2,1)S(1)} %copy.41), kind=kCustom, calls=%fused_computation.3 | custom fusion | bytes 394240 | tf_op jit(solution)/shard_map/scatter | solution.py:158
  201.6 6.6 %collective-permute-start.3 = (bf16[4096,256]{1,0:T(8,128)(2,1)}, bf16[4096,256]{1,0:T(8,128)(2,1)S(1)}, u32[]{:S(2)}, u32[]{:S(2)}) collective-permute-start(bf16[4096,256]{1,0:T(8,128)(2,1)} %scatter_fusion), channel_id=1, source_target_pairs={{0,1},{1,2},{2,3},{3,4},{4,5},{5,6},{6,7},{7,8},{8,9},{9,10},{10,1... | collective-permute-start | bytes 6291464 | tf_op jit(solution)/shard_map/ppermute | solution.py:24
  210.6 1.8 fusion.108
  212.4 19.0 %collective-permute-done.3 = bf16[4096,256]{1,0:T(8,128)(2,1)S(1)} collective-permute-done((bf16[4096,256]{1,0:T(8,128)(2,1)}, bf16[4096,256]{1,0:T(8,128)(2,1)S(1)}, u32[]{:S(2)}, u32[]{:S(2)}) %collective-permute-start.3) | collective-permute-done | bytes 2097184 | tf_op jit(solution)/shard_map/ppermute | solution.py:24
  233.2 5.8 %fusion.11 = (f32[256]{0:T(256)S(1)}, f32[256]{0:T(256)S(1)}) fusion(f32[1,256,4096]{1,2,0:T(8,128)S(1)} %get-tuple-element.50, f32[256]{0:T(256)S(1)} %get-tuple-element.49, pred[4096]{0:T(1024)(128)(4,1)S(1)} %get-tuple-element.57, s32[4096]{0:T(1024)S(1)} %get-tuple-element.55, s32[256]{0:T(256)S(1)} %copy-done.10, s32[4096]{0:T(1024)S(1)} %get-tuple-element.20, ...), kind=kLoop, calls=%fused_computation.28 | loop fusion | flops 20971008 | bytes 8468480 | tf_op jit(solution)/shard_map/reduce_sum | solution.py:74
  239.0 3.0 fusion.31
  242.0 5.8 %fusion.25 = bf16[32,32,8,128]{3,2,1,0:T(8,128)(2,1)S(1)} fusion(bf16[128,4096]{1,0:T(8,128)(2,1)S(1)} %copy-done, f32[256,128]{1,0:T(8,128)S(1)} %fusion.31, f32[1,256,4096]{1,2,0:T(8,128)} %copy-done.3, f32[256]{0:T(256)S(1)} %get-tuple-element.51, bf16[4096,256]{1,0:T(8,128)(2,1)} %copy-done.22, f32[256]{0:T(256)S(1)} %get-tuple-element.21, ...), kind=kOutput, calls=%fused_computation.43 | convolution fusion | flops 548536320 | bytes 8561664 | tf_op jit(solution)/shard_map/gch,ghd->cd/dot_general | solution.py:184
  247.8 1.9 copy.53
  249.7 10.2 %all-to-all-start.3 = ((bf16[256,32,128]{2,0,1:T(8,128)(2,1)}), bf16[256,32,128]{2,0,1:T(8,128)(2,1)S(1)}, u32[]{:S(2)}, u32[]{:S(2)}) async-start(bf16[256,32,128]{2,0,1:T(8,128)(2,1)} %bitcast.106), calls=%async_computation.3 | async-start | bytes 4194304 | tf_op jit(solution)/shard_map/all_to_all | solution.py:186
  260.6 58.0 %all-to-all-done.3 = bf16[256,32,128]{2,0,1:T(8,128)(2,1)S(1)} async-done(((bf16[256,32,128]{2,0,1:T(8,128)(2,1)}), bf16[256,32,128]{2,0,1:T(8,128)(2,1)S(1)}, u32[]{:S(2)}, u32[]{:S(2)}) %all-to-all-start.3) | async-done | bytes 2097184 | tf_op jit(solution)/shard_map/all_to_all | solution.py:186
  (95 shorter events, 20.7 us)
Async XLA Ops:
  0.0 242.0 %copy-start = (bf16[128,4096]{1,0:T(8,128)(2,1)S(1)}, bf16[128,4096]{1,0:T(8,128)(2,1)}, u32[]{:S(2)}) copy-start(bf16[128,4096]{1,0:T(8,128)(2,1)} %param.19) | copy-start | bytes 3145732
  0.0 44.1 %copy-start.21 = (s32[32]{0:T(128)S(1)}, s32[32]{0:T(128)}, u32[]{:S(2)}) copy-start(s32[32]{0:T(128)} %constant.256) | copy-start | bytes 388
  0.0 44.1 %copy-start.1 = (bf16[128,8,256]{2,1,0:T(8,128)(2,1)S(1)}, bf16[128,8,256]{2,1,0:T(8,128)(2,1)}, u32[]{:S(2)}) copy-start(bf16[128,8,256]{2,1,0:T(8,128)(2,1)} %param.14) | copy-start | bytes 1572868
  36.6 57.5 %all-to-all-start.1 = ((bf16[256,32,128]{2,0,1:T(8,128)(2,1)}), bf16[256,32,128]{2,0,1:T(8,128)(2,1)}, u32[]{:S(2)}, u32[]{:S(2)}) async-start(bf16[256,32,128]{2,0,1:T(8,128)(2,1)} %broadcast_in_dim.160), calls=%async_computation.1 | async-start | bytes 4194304 | tf_op jit(solution)/shard_map/all_to_all | solution.py:117
  52.1 59.4 %copy-start.24 = (s32[16]{0:T(128)S(1)}, s32[16]{0:T(128)}, u32[]{:S(2)}) copy-start(s32[16]{0:T(128)} %param.24) | copy-start | bytes 196
  52.1 63.2 %copy-start.25 = (s32[64]{0:T(128)S(1)}, s32[64]{0:T(128)}, u32[]{:S(2)}) copy-start(s32[64]{0:T(128)} %param.20) | copy-start | bytes 772
  52.1 63.3 %copy-start.20 = (s32[64]{0:T(128)S(1)}, s32[64]{0:T(128)}, u32[]{:S(2)}) copy-start(s32[64]{0:T(128)} %param.21) | copy-start | bytes 772
  52.1 65.3 %copy-start.19 = (s32[64]{0:T(128)S(1)}, s32[64]{0:T(128)}, u32[]{:S(2)}) copy-start(s32[64]{0:T(128)} %param.22) | copy-start | bytes 772
  52.1 65.7 %copy-start.11 = (bf16[4096]{0:T(1024)(128)(2,1)S(1)}, bf16[4096]{0:T(1024)(128)(2,1)}, u32[]{:S(2)}) copy-start(bf16[4096]{0:T(1024)(128)(2,1)} %param.16) | copy-start | bytes 24580
  52.1 65.7 %copy-start.16 = (pred[4096]{0:T(1024)(128)(4,1)S(1)}, pred[4096]{0:T(1024)(128)(4,1)}, u32[]{:S(2)}) copy-start(pred[4096]{0:T(1024)(128)(4,1)} %constant.260) | copy-start | bytes 12292
  52.1 65.7 %copy-start.17 = (pred[4096]{0:T(1024)(128)(4,1)S(1)}, pred[4096]{0:T(1024)(128)(4,1)}, u32[]{:S(2)}) copy-start(pred[4096]{0:T(1024)(128)(4,1)} %constant.259) | copy-start | bytes 12292
  52.1 65.7 %copy-start.18 = (pred[4096]{0:T(1024)(128)(4,1)S(1)}, pred[4096]{0:T(1024)(128)(4,1)}, u32[]{:S(2)}) copy-start(pred[4096]{0:T(1024)(128)(4,1)} %constant.258) | copy-start | bytes 12292
  94.1 70.3 %all-to-all-start = ((bf16[128,32,256]{2,0,1:T(8,128)(2,1)}), bf16[128,32,256]{2,0,1:T(8,128)(2,1)}, u32[]{:S(2)}, u32[]{:S(2)}) async-start(bf16[128,32,256]{2,0,1:T(8,128)(2,1)} %copy.34), calls=%async_computation | async-start | bytes 4194304 | tf_op jit(solution)/shard_map/all_to_all | solution.py:140
  115.5 55.7 %copy-start.12 = (f32[64]{0:T(128)}, f32[64]{0:T(128)S(1)}, u32[]{:S(2)}) copy-start(f32[64]{0:T(128)S(1)} %negate_power_fusion) | copy-start | bytes 772
  124.9 1.0 copy-start.4
  125.7 44.0 %copy-start.14 = (f32[256]{0:T(256)}, f32[256]{0:T(256)S(1)}, u32[]{:S(2)}) copy-start(f32[256]{0:T(256)S(1)} %add_rsqrt_fusion) | copy-start | bytes 3076
  126.3 65.2 %collective-permute-start.2 = (f32[256,64]{0,1:T(8,128)S(1)}, f32[256,64]{0,1:T(8,128)S(1)}, u32[]{:S(2)}, u32[]{:S(2)}) collective-permute-start(f32[256,64]{0,1:T(8,128)S(1)} %convolution_multiply_fusion.3), channel_id=1, source_target_pairs={{0,48},{16,0},{32,16},{48,32},{64,112},{80,64},{96,80},{112,96},{1... | collective-permute-start | bytes 196616 | tf_op jit(solution)/shard_map/ppermute | solution.py:33
  131.5 60.0 %collective-permute-start.1 = (f32[256,64]{0,1:T(8,128)S(1)}, f32[256,64]{0,1:T(8,128)S(1)}, u32[]{:S(2)}, u32[]{:S(2)}) collective-permute-start(f32[256,64]{0,1:T(8,128)S(1)} %convolution_multiply_fusion.3), channel_id=1, source_target_pairs={{0,32},{16,48},{32,0},{48,16},{64,96},{80,112},{96,64},{112,80},{1... | collective-permute-start | bytes 196616 | tf_op jit(solution)/shard_map/ppermute | solution.py:33
  135.5 56.0 %collective-permute-start = (f32[256,64]{0,1:T(8,128)S(1)}, f32[256,64]{0,1:T(8,128)S(1)}, u32[]{:S(2)}, u32[]{:S(2)}) collective-permute-start(f32[256,64]{0,1:T(8,128)S(1)} %convolution_multiply_fusion.3), channel_id=1, source_target_pairs={{0,16},{16,32},{32,48},{48,0},{64,80},{80,96},{96,112},{112,64},{1... | collective-permute-start | bytes 196616 | tf_op jit(solution)/shard_map/ppermute | solution.py:33
  191.5 0.6 copy-start.5
  191.5 0.6 copy-start.6
  191.6 0.6 copy-start.7
  194.5 15.2 %copy-start.15 = (f32[256]{0:T(256)S(1)}, f32[256]{0:T(256)}, u32[]{:S(2)}) copy-start(f32[256]{0:T(256)} %copy-done.14) | copy-start | bytes 3076
  201.6 8.1 %copy-start.23 = (bf16[4096,128]{1,0:T(8,128)(2,1)S(1)}, bf16[4096,128]{1,0:T(8,128)(2,1)}, u32[]{:S(2)}) copy-start(bf16[4096,128]{1,0:T(8,128)(2,1)} %param.17) | copy-start | bytes 3145732
  201.6 8.7 %copy-start.8 = (f32[256]{0:T(256)S(1)}, f32[256]{0:T(256)}, u32[]{:S(2)}) copy-start(f32[256]{0:T(256)} %convert_element_type.68) | copy-start | bytes 3076
  201.6 8.7 %copy-start.13 = (f32[64]{0:T(128)S(1)}, f32[64]{0:T(128)}, u32[]{:S(2)}) copy-start(f32[64]{0:T(128)} %copy-done.12) | copy-start | bytes 772
  201.6 9.0 %copy-start.2 = (bf16[4096,256]{1,0:T(8,128)(2,1)S(1)}, bf16[4096,256]{1,0:T(8,128)(2,1)}, u32[]{:S(2)}) copy-start(bf16[4096,256]{1,0:T(8,128)(2,1)} %scatter_fusion) | copy-start | bytes 6291460
  201.6 9.0 %copy-start.10 = (s32[256]{0:T(256)S(1)}, s32[256]{0:T(256)}, u32[]{:S(2)}) copy-start(s32[256]{0:T(256)} %copy-done.9) | copy-start | bytes 3076
  201.6 29.8 %collective-permute-start.3 = (bf16[4096,256]{1,0:T(8,128)(2,1)}, bf16[4096,256]{1,0:T(8,128)(2,1)S(1)}, u32[]{:S(2)}, u32[]{:S(2)}) collective-permute-start(bf16[4096,256]{1,0:T(8,128)(2,1)} %scatter_fusion), channel_id=1, source_target_pairs={{0,1},{1,2},{2,3},{3,4},{4,5},{5,6},{6,7},{7,8},{8,9},{9,10},{10,1... | collective-permute-start | bytes 6291464 | tf_op jit(solution)/shard_map/ppermute | solution.py:24
  231.4 1.8 copy-start.22
  233.2 5.8 %copy-start.3 = (f32[1,256,4096]{1,2,0:T(8,128)}, f32[1,256,4096]{1,2,0:T(8,128)S(1)}, u32[]{:S(2)}) copy-start(f32[1,256,4096]{1,2,0:T(8,128)S(1)} %get-tuple-element.52) | copy-start | bytes 12582916
  249.7 68.9 %all-to-all-start.3 = ((bf16[256,32,128]{2,0,1:T(8,128)(2,1)}), bf16[256,32,128]{2,0,1:T(8,128)(2,1)S(1)}, u32[]{:S(2)}, u32[]{:S(2)}) async-start(bf16[256,32,128]{2,0,1:T(8,128)(2,1)} %bitcast.106), calls=%async_computation.3 | async-start | bytes 4194304 | tf_op jit(solution)/shard_map/all_to_all | solution.py:186
  (1 other events, 0.6 us)

commit v2 on v0

--- a/solution.py
+++ b/solution.py
@@ -72,6 +72,35 @@
     totals = first[1] * scale_one + second[1] * scale_two
     summed = first[2] * scale_one[..., None] + second[2] * scale_two[..., None]
     return summed / totals[..., None]
+
+
+def group_gather(piece, axis, size):
+    devices = lax.axis_size(axis)
+    place = lax.axis_index(axis) % size
+    pieces = [piece]
+    for step in range(1, size):
+        pairs = [(i, i - i % size + (i % size + step) % size) for i in range(devices)]
+        pieces.append(lax.ppermute(piece, axis, pairs))
+    stacked = jnp.stack(pieces)
+    order = (place - jnp.arange(size, dtype=jnp.int32)) % size
+    return jnp.take(stacked, order, axis=0)
+
+
+def group_exchange(parts, axis, size):
+    devices = lax.axis_size(axis)
+    place = lax.axis_index(axis) % size
+    mine = [lax.dynamic_index_in_dim(parts, place, 0, keepdims=False)]
+    for step in range(1, size):
+        pairs = [(i, i - i % size + (i % size + step) % size) for i in range(devices)]
+        outgoing = lax.dynamic_index_in_dim(parts, (place + step) % size, 0, keepdims=False)
+        mine.append(lax.ppermute(outgoing, axis, pairs))
+    return jnp.stack(mine)
+
+
+def joined_slot(span_order, shard, spans_here, block):
+    local_order = lax.dynamic_slice_in_dim(span_order, shard * spans_here, spans_here, 0)
+    local_order = local_order - shard * spans_here
+    return jnp.sum(jnp.where(local_order == block, jnp.arange(spans_here, dtype=jnp.int32), 0))
 
 
 def local(
@@ -95,54 +124,77 @@
     slots = recompute_input.shape[0]
     own_cols = recompute_input.shape[1]
     width = norm_gain.shape[0]
-    local_heads = w_query.shape[1] // HEAD_DIM
     spans_here = shard_len // SPAN
-    own_group = blk_index * local_heads // (QH // KVH)
-    targets = np.arange(blk_count) * local_heads // (QH // KVH)
-    wide = lax.all_gather(recompute_input, "blk", axis=1, tiled=True).astype(jnp.float32)
+    group_size = QH // KVH
+    chunks_per_span = SPAN // block_rows
+    pair_cols = w_keyval.shape[1] // blk_count
+    member = blk_index % group_size
+    group = blk_index // group_size
+
+    x_part = jnp.broadcast_to(
+        recompute_input.reshape(1, slots * own_cols), (blk_count, slots * own_cols)
+    )
+    w_part = (
+        w_keyval.reshape(own_cols, blk_count, pair_cols)
+        .transpose(1, 0, 2)
+        .reshape(blk_count, own_cols * pair_cols)
+    )
+    arrived = lax.all_to_all(
+        jnp.concatenate([x_part, w_part], axis=1), "blk", 0, 0, tiled=True
+    )
+    wide = (
+        arrived[:, : slots * own_cols]
+        .reshape(blk_count, slots, own_cols)
+        .transpose(1, 0, 2)
+        .reshape(slots, width)
+        .astype(jnp.float32)
+    )
+    kv_cols = arrived[:, slots * own_cols :].reshape(width, pair_cols)
+
+    pieces = []
+    for step in range(chunks_per_span):
+        chosen = (blk_index % chunks_per_span + step) % KVH
+        pairs = [
+            (k, ((k % chunks_per_span + step) % KVH) * group_size + k // chunks_per_span)
+            for k in range(blk_count)
+        ]
+        outgoing = lax.dynamic_index_in_dim(cache_entries, chosen, 1, keepdims=False)
+        pieces.append(lax.ppermute(outgoing, "blk", pairs))
+    stacked = jnp.stack(pieces)
+    order = (group - jnp.arange(chunks_per_span, dtype=jnp.int32)) % KVH
+    stored = jnp.take(stacked, order, axis=0).reshape(SPAN, 2 * HEAD_DIM)
+
     gains = norm_gain.astype(jnp.float32)
     scaled = (wide * gains[None, :]).astype(jnp.bfloat16)
-    query_acc = jnp.dot(scaled, w_query, preferred_element_type=jnp.float32)
     square_acc = jnp.sum(wide * wide, axis=1)
-    own_gain = lax.dynamic_slice_in_dim(norm_gain, blk_index * own_cols, own_cols, 0).astype(
-        jnp.float32
-    )
-    own_scaled = (recompute_input.astype(jnp.float32) * own_gain[None, :]).astype(jnp.bfloat16)
-    pair_term = jnp.dot(own_scaled, w_keyval, preferred_element_type=jnp.float32)
-    pair_sum = lax.psum(pair_term.astype(jnp.bfloat16), "blk").astype(jnp.float32)
     inv_rms = lax.rsqrt(square_acc / width + NORM_EPS)
-    pair_heads = (pair_sum * inv_rms[:, None]).reshape(slots, KVH, 2 * HEAD_DIM)
-    own_pair = lax.dynamic_index_in_dim(pair_heads, own_group, 1, keepdims=False)
+    query_acc = jnp.dot(scaled, w_query, preferred_element_type=jnp.float32) * inv_rms[:, None]
+    pair_piece = jnp.dot(scaled, kv_cols, preferred_element_type=jnp.float32) * inv_rms[:, None]
+    shared = group_gather(jnp.concatenate([query_acc, pair_piece], axis=1), "blk", group_size)
+    group_pair = shared[:, :, HEAD_DIM:].transpose(1, 0, 2).reshape(slots, group_size * pair_cols)
+
     own_pos = lax.dynamic_slice_in_dim(recompute_pos, kv_index * slots, slots, 0)
     own_count = lax.dynamic_index_in_dim(recompute_count, kv_index, 0, keepdims=False)
     live = jnp.arange(slots, dtype=jnp.int32) < own_count
     query_pos = kv_index * shard_len + own_pos
-    fresh_keys = rotate_half(own_pair[:, :HEAD_DIM], query_pos).astype(jnp.bfloat16)
-    fresh_values = own_pair[:, HEAD_DIM:].astype(jnp.bfloat16)
-    queries = rotate_half(
-        (query_acc * inv_rms[:, None]).reshape(slots, local_heads, HEAD_DIM), query_pos
-    ).astype(jnp.bfloat16)
-    arrived = lax.all_to_all(
-        jnp.take(cache_entries, targets, axis=1), "blk", split_axis=1, concat_axis=0, tiled=True
-    )
-    stored = arrived.reshape(shard_len, 2 * HEAD_DIM)
-    offsets_here = lax.dynamic_slice_in_dim(rotate_offsets, kv_index * spans_here, spans_here, 0)
-    row_shifts = jnp.repeat(offsets_here, SPAN, total_repeat_length=shard_len)
+    fresh_keys = rotate_half(group_pair[:, :HEAD_DIM], query_pos).astype(jnp.bfloat16)
+    fresh_values = group_pair[:, HEAD_DIM:].astype(jnp.bfloat16)
+    queries = rotate_half(shared[:, :, :HEAD_DIM].transpose(1, 0, 2), query_pos).astype(
+        jnp.bfloat16
+    )
+
+    offset = lax.dynamic_index_in_dim(
+        rotate_offsets, kv_index * spans_here + member, 0, keepdims=False
+    )
+    row_shifts = jnp.full((SPAN,), offset, dtype=jnp.int32)
     turned_rows = rotate_half(stored[:, :HEAD_DIM].astype(jnp.float32), row_shifts).astype(
         jnp.bfloat16
     )
     stored = jnp.concatenate([turned_rows, stored[:, HEAD_DIM:]], axis=-1)
-    local_order = (
-        lax.dynamic_slice_in_dim(span_order, kv_index * spans_here, spans_here, 0)
-        - kv_index * spans_here
-    )
-    ordered = jnp.take(stored.reshape(spans_here, SPAN, 2 * HEAD_DIM), local_order, axis=0).reshape(
-        shard_len, 2 * HEAD_DIM
-    )
-    place = jnp.where(live, own_pos, shard_len)
-    merged = ordered.at[place].set(jnp.concatenate([fresh_keys, fresh_values], axis=1), mode="drop")
-    key_pos = kv_index * shard_len + jnp.arange(shard_len, dtype=jnp.int32)
-    key_tenant = tenant_lookup(key_pos, tenant_of_span)
+    own_slot = joined_slot(span_order, kv_index, spans_here, member)
+    place = jnp.where(live & (own_pos // SPAN == own_slot), own_pos % SPAN, SPAN)
+    merged = stored.at[place].set(jnp.concatenate([fresh_keys, fresh_values], axis=1), mode="drop")
+    key_pos = kv_index * shard_len + own_slot * SPAN + jnp.arange(SPAN, dtype=jnp.int32)
     query_tenant = tenant_lookup(query_pos, tenant_of_span)
     own_part = attend_part(
         queries,
@@ -151,10 +203,13 @@
         merged[:, :HEAD_DIM],
         merged[:, HEAD_DIM:],
         key_pos,
-        key_tenant,
+        tenant_lookup(key_pos, tenant_of_span),
     )
     prior = shifted(merged, "kv", 1)
-    prior_pos = key_pos - shard_len
+    prior_slot = joined_slot(span_order, jnp.maximum(kv_index - 1, 0), spans_here, member)
+    prior_pos = (
+        (kv_index - 1) * shard_len + prior_slot * SPAN + jnp.arange(SPAN, dtype=jnp.int32)
+    )
     prior_part = attend_part(
         queries,
         query_pos,
@@ -164,12 +219,23 @@
         prior_pos,
         tenant_lookup(prior_pos, tenant_of_span),
     )
-    heads_out = combine_parts(own_part, prior_part).astype(jnp.bfloat16)
-    out_rows = w_out.reshape(local_heads, HEAD_DIM, width)
-    term = jnp.einsum("gch,ghd->cd", heads_out, out_rows, preferred_element_type=jnp.float32)
-    summed_out = lax.psum_scatter(
-        term.astype(jnp.bfloat16), "blk", scatter_dimension=1, tiled=True
-    ).astype(jnp.float32)
+    top = jnp.maximum(own_part[0], prior_part[0])
+    scale_own = jnp.exp(own_part[0] - top)
+    scale_prior = jnp.exp(prior_part[0] - top)
+    totals = own_part[1] * scale_own + prior_part[1] * scale_prior
+    summed = own_part[2] * scale_own[..., None] + prior_part[2] * scale_prior[..., None]
+    packed = jnp.concatenate([summed, top[..., None], totals[..., None]], axis=-1)
+    gathered = group_exchange(packed, "blk", group_size)
+    part_max = gathered[:, :, HEAD_DIM]
+    best = jnp.max(part_max, axis=0)
+    weight = jnp.exp(part_max - best[None])
+    total = jnp.sum(gathered[:, :, HEAD_DIM + 1] * weight, axis=0)
+    heads_sum = jnp.sum(gathered[:, :, :HEAD_DIM] * weight[..., None], axis=0)
+    heads_out = (heads_sum / total[:, None]).astype(jnp.bfloat16)
+    term = jnp.dot(heads_out, w_out, preferred_element_type=jnp.float32)
+    term_blocks = term.astype(jnp.bfloat16).reshape(slots, blk_count, own_cols)
+    arrived_terms = lax.all_to_all(term_blocks, "blk", 1, 1, tiled=True)
+    summed_out = jnp.sum(arrived_terms.astype(jnp.float32), axis=1)
     return jnp.where(live[:, None], summed_out, 0.0).astype(jnp.bfloat16)
 
 

time: 772 us -> 304 us (0.39)
  the two profiles are of different devices: /device:TPU:6 before, /device:TPU:124 now
where the time goes in v2:
time: 304 us; the launch traced here: 302 us
  waiting for transfers between devices  121 us (40%)
  starting transfers between devices  99 us (33%)
  local copies, waits for them, and re-layouts  48.1 us (16%)
  other arithmetic  25.7 us (8%)
  matrix products  5.73 us (2%)
  between operations  3.1 us (1%)
    all_to_all x1, waiting for transfers between devices, local(): arrived_terms = lax.all_to_all(term_blocks, 'blk', 1, 1, tiled=True)  55.9 us
    ppermute x8, starting transfers between devices, local(): pieces.append(lax.ppermute(outgoing, 'blk', pairs))  47.4 us
    ppermute x8, waiting for transfers between devices, local(): pieces.append(lax.ppermute(outgoing, 'blk', pairs))  40.2 us
    unnamed x48, local copies, waits for them, and re-layouts  27.7 us
    all_to_all x1, starting transfers between devices, local(): lax.all_to_all(jnp.concatenate([x_part, w_part], axis=1), 'blk', 0, 0, ti...  14.9 us
    ppermute x3, starting transfers between devices, group_exchange(): mine.append(lax.ppermute(outgoing, axis, pairs))  13.1 us
    ppermute x3, starting transfers between devices, group_gather(): pieces.append(lax.ppermute(piece, axis, pairs))  13 us
    ppermute x3, waiting for transfers between devices, group_gather(): pieces.append(lax.ppermute(piece, axis, pairs))  9.36 us
  transfers between devices with their start and end apart: 17, of which 8 were waited for; matrix products, arithmetic and copies ran while one was open for 4% of the time, Pallas kernels for 0%

profile of v2, /device:TPU:124, one launch (start us, length us, event | category | flops | bytes accessed | tf_op | source)
XLA Modules:
  0.0 302.2 jit_solution(12790897917955028590)
XLA Ops:
  5.0 5.1 %reduce.3 = bf16[32,40960]{1,0:T(8,128)(2,1)} reduce(bf16[32,1,40960]{2,0,1:T(8,128)(2,1)} %maximum_bitcast_fusion, bf16[]{:T(256)} %broadcast.577), dimensions={1}, to_apply=%copy.192.reduce_sub_computation | reduce | bytes 5242882 | tf_op jit(solution)/shard_map/all_to_all | solution.py:142
  10.1 5.0 %reshape.505 = bf16[32,2,20480]{2,1,0:T(2,128)(2,1)} reshape(bf16[32,40960]{1,0:T(8,128)(2,1)} %reduce.3) | data formatting | bytes 5242880
  15.1 14.9 %all-to-all-start = ((bf16[32,2,20480]{2,1,0:T(2,128)(2,1)}), bf16[32,2,20480]{2,1,0:T(2,128)(2,1)}, u32[]{:S(2)}, u32[]{:S(2)}) async-start(bf16[32,2,20480]{2,1,0:T(2,128)(2,1)} %reshape.505), calls=%async_computation | async-start | bytes 5242880 | tf_op jit(solution)/shard_map/all_to_all | solution.py:142
  31.3 8.1 %collective-permute-start = (bf16[128,256]{1,0:T(8,128)(2,1)S(1)}, bf16[128,256]{1,0:T(8,128)(2,1)S(1)}, u32[]{:S(2)}, u32[]{:S(2)}) collective-permute-start(bf16[128,256]{1,0:T(8,128)(2,1)S(1)} %bitcast.184), channel_id=1, source_target_pairs={{0,0},{16,64},{32,128},{48,192},{64,256},{80,320},{96,384},{112,44... | collective-permute-start | bytes 196616 | tf_op jit(solution)/shard_map/ppermute | solution.py:162
  39.4 3.4 %collective-permute-start.1 = (bf16[128,256]{1,0:T(8,128)(2,1)S(1)}, bf16[128,256]{1,0:T(8,128)(2,1)S(1)}, u32[]{:S(2)}, u32[]{:S(2)}) collective-permute-start(bf16[128,256]{1,0:T(8,128)(2,1)S(1)} %bitcast.183), channel_id=1, source_target_pairs={{0,64},{16,128},{32,192},{48,256},{64,320},{80,384},{96,448},{112,... | collective-permute-start | bytes 196616 | tf_op jit(solution)/shard_map/ppermute | solution.py:162
  42.9 3.3 %collective-permute-start.2 = (bf16[128,256]{1,0:T(8,128)(2,1)S(1)}, bf16[128,256]{1,0:T(8,128)(2,1)S(1)}, u32[]{:S(2)}, u32[]{:S(2)}) collective-permute-start(bf16[128,256]{1,0:T(8,128)(2,1)S(1)} %bitcast.182), channel_id=1, source_target_pairs={{0,128},{16,192},{32,256},{48,320},{64,384},{80,448},{96,0},{112,6... | collective-permute-start | bytes 196616 | tf_op jit(solution)/shard_map/ppermute | solution.py:162
  48.2 14.2 %collective-permute-start.4 = (bf16[128,256]{1,0:T(8,128)(2,1)S(1)}, bf16[128,256]{1,0:T(8,128)(2,1)S(1)}, u32[]{:S(2)}, u32[]{:S(2)}) collective-permute-start(bf16[128,256]{1,0:T(8,128)(2,1)S(1)} %bitcast.180), channel_id=1, source_target_pairs={{0,256},{16,320},{32,384},{48,448},{64,0},{80,64},{96,128},{112,19... | collective-permute-start | bytes 196616 | tf_op jit(solution)/shard_map/ppermute | solution.py:162
  69.2 2.3 fusion.26
  71.4 35.0 %collective-permute-done = bf16[128,256]{1,0:T(8,128)(2,1)S(1)} collective-permute-done((bf16[128,256]{1,0:T(8,128)(2,1)S(1)}, bf16[128,256]{1,0:T(8,128)(2,1)S(1)}, u32[]{:S(2)}, u32[]{:S(2)}) %collective-permute-start) | collective-permute-done | bytes 65568 | tf_op jit(solution)/shard_map/ppermute | solution.py:162
  106.5 12.0 %collective-permute-start.5 = (bf16[128,256]{1,0:T(8,128)(2,1)S(1)}, bf16[128,256]{1,0:T(8,128)(2,1)S(1)}, u32[]{:S(2)}, u32[]{:S(2)}) collective-permute-start(bf16[128,256]{1,0:T(8,128)(2,1)S(1)} %bitcast.187), channel_id=1, source_target_pairs={{0,320},{16,384},{32,448},{48,0},{64,64},{80,128},{96,192},{112,25... | collective-permute-start | bytes 196616 | tf_op jit(solution)/shard_map/ppermute | solution.py:162
  118.5 2.3 collective-permute-start.6
  123.1 4.6 %collective-permute-done.6 = bf16[128,256]{1,0:T(8,128)(2,1)S(1)} collective-permute-done((bf16[128,256]{1,0:T(8,128)(2,1)S(1)}, bf16[128,256]{1,0:T(8,128)(2,1)S(1)}, u32[]{:S(2)}, u32[]{:S(2)}) %collective-permute-start.6) | collective-permute-done | bytes 65568 | tf_op jit(solution)/shard_map/ppermute | solution.py:162
  129.9 10.9 %reshape.506 = bf16[32,1,40960]{2,1,0:T(2,128)(2,1)} reshape(bf16[32,2,20480]{2,1,0:T(2,128)(2,1)} %all-to-all-done) | data formatting | bytes 5242880
  140.8 5.4 %copy.244 = bf16[32,1,40960]{2,0,1:T(8,128)(2,1)S(1)} copy(bf16[32,1,40960]{2,1,0:T(2,128)(2,1)} %reshape.506) | data formatting | bytes 5242880
  146.2 2.2 convert_bitcast_fusion
  148.5 2.2 reshape.469
  150.6 2.9 copy.226
  155.5 2.2 multiply_reduce_fusion
  157.7 3.3 %copy.194 = bf16[256,32,128]{0,2,1:T(8,128)(2,1)S(1)} copy(bf16[256,32,128]{2,0,1:T(8,128)(2,1)} %get-tuple-element.14) | data formatting | bytes 4194304 | tf_op jit(solution)/shard_map/convert_element_type | solution.py:168
  161.0 5.6 %copy.193 = f32[256,32,128]{0,2,1:T(8,128)} copy(f32[256,32,128]{2,0,1:T(8,128)} %bitcast.163) | data formatting | bytes 8388608 | tf_op jit(solution)/shard_map/convert_element_type | solution.py:150
  166.6 2.7 fusion
  170.5 5.0 %collective-permute-start.9 = (f32[256,192]{0,1:T(8,128)S(1)}, f32[256,192]{0,1:T(8,128)S(1)}, u32[]{:S(2)}, u32[]{:S(2)}) collective-permute-start(f32[256,192]{0,1:T(8,128)S(1)} %get-tuple-element.37), channel_id=1, source_target_pairs={{0,32},{16,48},{32,0},{48,16},{64,96},{80,112},{96,64},{112,80},{1... | collective-permute-start | bytes 589832 | tf_op jit(solution)/shard_map/ppermute | solution.py:83
  177.5 6.0 %collective-permute-start.10 = (f32[256,192]{0,1:T(8,128)S(1)}, f32[256,192]{0,1:T(8,128)S(1)}, u32[]{:S(2)}, u32[]{:S(2)}) collective-permute-start(f32[256,192]{0,1:T(8,128)S(1)} %get-tuple-element.37), channel_id=1, source_target_pairs={{0,48},{16,0},{32,16},{48,32},{64,112},{80,64},{96,80},{112,96},{1... | collective-permute-start | bytes 589832 | tf_op jit(solution)/shard_map/ppermute | solution.py:83
  184.0 9.4 %collective-permute-done.8 = f32[256,192]{0,1:T(8,128)S(1)} collective-permute-done((f32[256,192]{0,1:T(8,128)S(1)}, f32[256,192]{0,1:T(8,128)S(1)}, u32[]{:S(2)}, u32[]{:S(2)}) %collective-permute-start.8) | collective-permute-done | bytes 196640 | tf_op jit(solution)/shard_map/ppermute | solution.py:83
  196.5 2.1 collective-permute-start.11
  200.6 6.4 %collective-permute-done.11 = bf16[1024,256]{1,0:T(8,128)(2,1)S(1)} collective-permute-done((bf16[1024,256]{1,0:T(8,128)(2,1)S(1)}, bf16[1024,256]{1,0:T(8,128)(2,1)S(1)}, u32[]{:S(2)}, u32[]{:S(2)}) %collective-permute-start.11) | collective-permute-done | bytes 524320 | tf_op jit(solution)/shard_map/ppermute | solution.py:24
  211.3 3.7 %collective-permute-start.14 = (f32[256,130]{0,1:T(8,128)S(1)}, f32[256,130]{0,1:T(8,128)S(1)}, u32[]{:S(2)}, u32[]{:S(2)}) collective-permute-start(f32[256,130]{0,1:T(8,128)S(1)} %get-tuple-element.19), channel_id=1, source_target_pairs={{0,48},{16,0},{32,16},{48,32},{64,112},{80,64},{96,80},{112,96},{1... | collective-permute-start | bytes 399368 | tf_op jit(solution)/shard_map/ppermute | solution.py:96
  215.0 5.0 %collective-permute-start.13 = (f32[256,130]{0,1:T(8,128)S(1)}, f32[256,130]{0,1:T(8,128)S(1)}, u32[]{:S(2)}, u32[]{:S(2)}) collective-permute-start(f32[256,130]{0,1:T(8,128)S(1)} %get-tuple-element.20), channel_id=1, source_target_pairs={{0,32},{16,48},{32,0},{48,16},{64,96},{80,112},{96,64},{112,80},{1... | collective-permute-start | bytes 399368 | tf_op jit(solution)/shard_map/ppermute | solution.py:96
  220.1 4.4 %collective-permute-start.12 = (f32[256,130]{0,1:T(8,128)S(1)}, f32[256,130]{0,1:T(8,128)S(1)}, u32[]{:S(2)}, u32[]{:S(2)}) collective-permute-start(f32[256,130]{0,1:T(8,128)S(1)} %get-tuple-element.21), channel_id=1, source_target_pairs={{0,16},{16,32},{32,48},{48,0},{64,80},{80,96},{96,112},{112,64},{1... | collective-permute-start | bytes 399368 | tf_op jit(solution)/shard_map/ppermute | solution.py:96
  226.3 6.8 %collective-permute-done.12 = f32[256,130]{0,1:T(8,128)S(1)} collective-permute-done((f32[256,130]{0,1:T(8,128)S(1)}, f32[256,130]{0,1:T(8,128)S(1)}, u32[]{:S(2)}, u32[]{:S(2)}) %collective-permute-start.12) | collective-permute-done | bytes 133152 | tf_op jit(solution)/shard_map/ppermute | solution.py:96
  236.0 8.6 %all-to-all-start.1 = ((bf16[256,32,128]{2,0,1:T(8,128)(2,1)}), bf16[256,32,128]{2,0,1:T(8,128)(2,1)S(1)}, u32[]{:S(2)}, u32[]{:S(2)}) async-start(bf16[256,32,128]{2,0,1:T(8,128)(2,1)} %bitcast.167), calls=%async_computation.1 | async-start | bytes 4194304 | tf_op jit(solution)/shard_map/all_to_all | solution.py:237
  245.3 55.9 %all-to-all-done.1 = bf16[256,32,128]{2,0,1:T(8,128)(2,1)S(1)} async-done(((bf16[256,32,128]{2,0,1:T(8,128)(2,1)}), bf16[256,32,128]{2,0,1:T(8,128)(2,1)S(1)}, u32[]{:S(2)}, u32[]{:S(2)}) %all-to-all-start.1) | async-done | bytes 2097184 | tf_op jit(solution)/shard_map/all_to_all | solution.py:237
  (127 shorter events, 38.1 us)
Async XLA Ops:
  0.0 233.3 %copy-start = (bf16[128,4096]{1,0:T(8,128)(2,1)S(1)}, bf16[128,4096]{1,0:T(8,128)(2,1)}, u32[]{:S(2)}) copy-start(bf16[128,4096]{1,0:T(8,128)(2,1)} %param.16) | copy-start | bytes 3145732
  0.0 2.7 copy-start.7
  10.1 20.0 %copy-start.4 = (bf16[128,8,256]{2,1,0:T(8,128)(2,1)S(1)}, bf16[128,8,256]{2,1,0:T(8,128)(2,1)}, u32[]{:S(2)}) copy-start(bf16[128,8,256]{2,1,0:T(8,128)(2,1)} %param.11) | copy-start | bytes 1572868
  15.1 47.3 %copy-start.10 = (s32[64]{0:T(128)S(1)}, s32[64]{0:T(128)}, u32[]{:S(2)}) copy-start(s32[64]{0:T(128)} %param.18) | copy-start | bytes 772
  15.1 49.4 %copy-start.12 = (s32[64]{0:T(128)S(1)}, s32[64]{0:T(128)}, u32[]{:S(2)}) copy-start(s32[64]{0:T(128)} %param.17) | copy-start | bytes 772
  15.1 50.7 %copy-start.13 = (s32[16]{0:T(128)S(1)}, s32[16]{0:T(128)}, u32[]{:S(2)}) copy-start(s32[16]{0:T(128)} %param.21) | copy-start | bytes 196
  15.1 53.7 %copy-start.9 = (s32[64]{0:T(128)S(1)}, s32[64]{0:T(128)}, u32[]{:S(2)}) copy-start(s32[64]{0:T(128)} %param.19) | copy-start | bytes 772
  15.1 54.0 %copy-start.8 = (bf16[4096]{0:T(1024)(128)(2,1)S(1)}, bf16[4096]{0:T(1024)(128)(2,1)}, u32[]{:S(2)}) copy-start(bf16[4096]{0:T(1024)(128)(2,1)} %param.13) | copy-start | bytes 24580
  15.1 114.8 %all-to-all-start = ((bf16[32,2,20480]{2,1,0:T(2,128)(2,1)}), bf16[32,2,20480]{2,1,0:T(2,128)(2,1)}, u32[]{:S(2)}, u32[]{:S(2)}) async-start(bf16[32,2,20480]{2,1,0:T(2,128)(2,1)} %reshape.505), calls=%async_computation | async-start | bytes 5242880 | tf_op jit(solution)/shard_map/all_to_all | solution.py:142
  31.3 75.2 %collective-permute-start = (bf16[128,256]{1,0:T(8,128)(2,1)S(1)}, bf16[128,256]{1,0:T(8,128)(2,1)S(1)}, u32[]{:S(2)}, u32[]{:S(2)}) collective-permute-start(bf16[128,256]{1,0:T(8,128)(2,1)S(1)} %bitcast.184), channel_id=1, source_target_pairs={{0,0},{16,64},{32,128},{48,192},{64,256},{80,320},{96,384},{112,44... | collective-permute-start | bytes 196616 | tf_op jit(solution)/shard_map/ppermute | solution.py:162
  39.4 79.1 %collective-permute-start.1 = (bf16[128,256]{1,0:T(8,128)(2,1)S(1)}, bf16[128,256]{1,0:T(8,128)(2,1)S(1)}, u32[]{:S(2)}, u32[]{:S(2)}) collective-permute-start(bf16[128,256]{1,0:T(8,128)(2,1)S(1)} %bitcast.183), channel_id=1, source_target_pairs={{0,64},{16,128},{32,192},{48,256},{64,320},{80,384},{96,448},{112,... | collective-permute-start | bytes 196616 | tf_op jit(solution)/shard_map/ppermute | solution.py:162
  42.9 78.0 %collective-permute-start.2 = (bf16[128,256]{1,0:T(8,128)(2,1)S(1)}, bf16[128,256]{1,0:T(8,128)(2,1)S(1)}, u32[]{:S(2)}, u32[]{:S(2)}) collective-permute-start(bf16[128,256]{1,0:T(8,128)(2,1)S(1)} %bitcast.182), channel_id=1, source_target_pairs={{0,128},{16,192},{32,256},{48,320},{64,384},{80,448},{96,0},{112,6... | collective-permute-start | bytes 196616 | tf_op jit(solution)/shard_map/ppermute | solution.py:162
  46.2 76.8 %collective-permute-start.3 = (bf16[128,256]{1,0:T(8,128)(2,1)S(1)}, bf16[128,256]{1,0:T(8,128)(2,1)S(1)}, u32[]{:S(2)}, u32[]{:S(2)}) collective-permute-start(bf16[128,256]{1,0:T(8,128)(2,1)S(1)} %bitcast.181), channel_id=1, source_target_pairs={{0,192},{16,256},{32,320},{48,384},{64,448},{80,0},{96,64},{112,12... | collective-permute-start | bytes 196616 | tf_op jit(solution)/shard_map/ppermute | solution.py:162
  48.2 74.8 %collective-permute-start.4 = (bf16[128,256]{1,0:T(8,128)(2,1)S(1)}, bf16[128,256]{1,0:T(8,128)(2,1)S(1)}, u32[]{:S(2)}, u32[]{:S(2)}) collective-permute-start(bf16[128,256]{1,0:T(8,128)(2,1)S(1)} %bitcast.180), channel_id=1, source_target_pairs={{0,256},{16,320},{32,384},{48,448},{64,0},{80,64},{96,128},{112,19... | collective-permute-start | bytes 196616 | tf_op jit(solution)/shard_map/ppermute | solution.py:162
  106.5 16.6 %collective-permute-start.5 = (bf16[128,256]{1,0:T(8,128)(2,1)S(1)}, bf16[128,256]{1,0:T(8,128)(2,1)S(1)}, u32[]{:S(2)}, u32[]{:S(2)}) collective-permute-start(bf16[128,256]{1,0:T(8,128)(2,1)S(1)} %bitcast.187), channel_id=1, source_target_pairs={{0,320},{16,384},{32,448},{48,0},{64,64},{80,128},{96,192},{112,25... | collective-permute-start | bytes 196616 | tf_op jit(solution)/shard_map/ppermute | solution.py:162
  118.5 9.2 %collective-permute-start.6 = (bf16[128,256]{1,0:T(8,128)(2,1)S(1)}, bf16[128,256]{1,0:T(8,128)(2,1)S(1)}, u32[]{:S(2)}, u32[]{:S(2)}) collective-permute-start(bf16[128,256]{1,0:T(8,128)(2,1)S(1)} %bitcast.186), channel_id=1, source_target_pairs={{0,384},{16,448},{32,0},{48,64},{64,128},{80,192},{96,256},{112,32... | collective-permute-start | bytes 196616 | tf_op jit(solution)/shard_map/ppermute | solution.py:162
  120.9 7.4 %collective-permute-start.7 = (bf16[128,256]{1,0:T(8,128)(2,1)S(1)}, bf16[128,256]{1,0:T(8,128)(2,1)S(1)}, u32[]{:S(2)}, u32[]{:S(2)}) collective-permute-start(bf16[128,256]{1,0:T(8,128)(2,1)S(1)} %bitcast.185), channel_id=1, source_target_pairs={{0,448},{16,0},{32,64},{48,128},{64,192},{80,256},{96,320},{112,38... | collective-permute-start | bytes 196616 | tf_op jit(solution)/shard_map/ppermute | solution.py:162
  153.6 1.9 copy-start.1
  166.6 2.8 copy-start.3
  166.6 3.3 %copy-start.11 = (bf16[4096,128]{1,0:T(8,128)(2,1)S(1)}, bf16[4096,128]{1,0:T(8,128)(2,1)}, u32[]{:S(2)}) copy-start(bf16[4096,128]{1,0:T(8,128)(2,1)} %param.14) | copy-start | bytes 3145732
  169.3 14.2 %copy-start.2 = (f32[1024,128]{1,0:T(8,128)S(1)}, f32[1024,128]{1,0:T(8,128)}, u32[]{:S(2)}) copy-start(f32[1024,128]{1,0:T(8,128)} %get-tuple-element.24) | copy-start | bytes 1572868
  170.5 13.5 %collective-permute-start.9 = (f32[256,192]{0,1:T(8,128)S(1)}, f32[256,192]{0,1:T(8,128)S(1)}, u32[]{:S(2)}, u32[]{:S(2)}) collective-permute-start(f32[256,192]{0,1:T(8,128)S(1)} %get-tuple-element.37), channel_id=1, source_target_pairs={{0,32},{16,48},{32,0},{48,16},{64,96},{80,112},{96,64},{112,80},{1... | collective-permute-start | bytes 589832 | tf_op jit(solution)/shard_map/ppermute | solution.py:83
  175.5 17.8 %collective-permute-start.8 = (f32[256,192]{0,1:T(8,128)S(1)}, f32[256,192]{0,1:T(8,128)S(1)}, u32[]{:S(2)}, u32[]{:S(2)}) collective-permute-start(f32[256,192]{0,1:T(8,128)S(1)} %get-tuple-element.37), channel_id=1, source_target_pairs={{0,16},{16,32},{32,48},{48,0},{64,80},{80,96},{96,112},{112,64},{1... | collective-permute-start | bytes 589832 | tf_op jit(solution)/shard_map/ppermute | solution.py:83
  177.5 15.9 %collective-permute-start.10 = (f32[256,192]{0,1:T(8,128)S(1)}, f32[256,192]{0,1:T(8,128)S(1)}, u32[]{:S(2)}, u32[]{:S(2)}) collective-permute-start(f32[256,192]{0,1:T(8,128)S(1)} %get-tuple-element.37), channel_id=1, source_target_pairs={{0,48},{16,0},{32,16},{48,32},{64,112},{80,64},{96,80},{112,96},{1... | collective-permute-start | bytes 589832 | tf_op jit(solution)/shard_map/ppermute | solution.py:83
  193.4 5.3 %copy-start.6 = (pred[256,1024]{0,1:T(8,128)(4,1)S(1)}, pred[256,1024]{0,1:T(8,128)(4,1)}, u32[]{:S(2)}) copy-start(pred[256,1024]{0,1:T(8,128)(4,1)} %get-tuple-element.45) | copy-start | bytes 786436
  196.5 10.5 %collective-permute-start.11 = (bf16[1024,256]{1,0:T(8,128)(2,1)S(1)}, bf16[1024,256]{1,0:T(8,128)(2,1)S(1)}, u32[]{:S(2)}, u32[]{:S(2)}) collective-permute-start(bf16[1024,256]{1,0:T(8,128)(2,1)S(1)} %scatter_fusion), channel_id=1, source_target_pairs={{0,1},{1,2},{2,3},{3,4},{4,5},{5,6},{6,7},{7,8},{8,9},{9,10},{10,1... | collective-permute-start | bytes 1572872 | tf_op jit(solution)/shard_map/ppermute | solution.py:24
  198.7 8.3 %copy-start.5 = (pred[256,1024]{0,1:T(8,128)(4,1)S(1)}, pred[256,1024]{0,1:T(8,128)(4,1)}, u32[]{:S(2)}) copy-start(pred[256,1024]{0,1:T(8,128)(4,1)} %get-tuple-element.46) | copy-start | bytes 786436
  211.3 13.1 %collective-permute-start.14 = (f32[256,130]{0,1:T(8,128)S(1)}, f32[256,130]{0,1:T(8,128)S(1)}, u32[]{:S(2)}, u32[]{:S(2)}) collective-permute-start(f32[256,130]{0,1:T(8,128)S(1)} %get-tuple-element.19), channel_id=1, source_target_pairs={{0,48},{16,0},{32,16},{48,32},{64,112},{80,64},{96,80},{112,96},{1... | collective-permute-start | bytes 399368 | tf_op jit(solution)/shard_map/ppermute | solution.py:96
  215.0 11.3 %collective-permute-start.13 = (f32[256,130]{0,1:T(8,128)S(1)}, f32[256,130]{0,1:T(8,128)S(1)}, u32[]{:S(2)}, u32[]{:S(2)}) collective-permute-start(f32[256,130]{0,1:T(8,128)S(1)} %get-tuple-element.20), channel_id=1, source_target_pairs={{0,32},{16,48},{32,0},{48,16},{64,96},{80,112},{96,64},{112,80},{1... | collective-permute-start | bytes 399368 | tf_op jit(solution)/shard_map/ppermute | solution.py:96
  220.1 13.1 %collective-permute-start.12 = (f32[256,130]{0,1:T(8,128)S(1)}, f32[256,130]{0,1:T(8,128)S(1)}, u32[]{:S(2)}, u32[]{:S(2)}) collective-permute-start(f32[256,130]{0,1:T(8,128)S(1)} %get-tuple-element.21), channel_id=1, source_target_pairs={{0,16},{16,32},{32,48},{48,0},{64,80},{80,96},{96,112},{112,64},{1... | collective-permute-start | bytes 399368 | tf_op jit(solution)/shard_map/ppermute | solution.py:96
  236.0 65.2 %all-to-all-start.1 = ((bf16[256,32,128]{2,0,1:T(8,128)(2,1)}), bf16[256,32,128]{2,0,1:T(8,128)(2,1)S(1)}, u32[]{:S(2)}, u32[]{:S(2)}) async-start(bf16[256,32,128]{2,0,1:T(8,128)(2,1)} %bitcast.167), calls=%async_computation.1 | async-start | bytes 4194304 | tf_op jit(solution)/shard_map/all_to_all | solution.py:237

commit v3 on v2

--- a/solution.py
+++ b/solution.py
@@ -97,10 +97,15 @@
     return jnp.stack(mine)
 
 
-def joined_slot(span_order, shard, spans_here, block):
+def joined_rows(span_order, shard, spans_here, stored_rows):
     local_order = lax.dynamic_slice_in_dim(span_order, shard * spans_here, spans_here, 0)
     local_order = local_order - shard * spans_here
-    return jnp.sum(jnp.where(local_order == block, jnp.arange(spans_here, dtype=jnp.int32), 0))
+    blocks = jnp.arange(spans_here, dtype=jnp.int32)
+    inverse = jnp.sum(
+        jnp.where(local_order[None, :] == blocks[:, None], blocks[None, :], 0), axis=1
+    )
+    slot = jnp.take(inverse, stored_rows // SPAN)
+    return shard * spans_here * SPAN + slot * SPAN + stored_rows % SPAN
 
 
 def local(
@@ -126,50 +131,43 @@
     width = norm_gain.shape[0]
     spans_here = shard_len // SPAN
     group_size = QH // KVH
-    chunks_per_span = SPAN // block_rows
     pair_cols = w_keyval.shape[1] // blk_count
     member = blk_index % group_size
     group = blk_index // group_size
 
-    x_part = jnp.broadcast_to(
-        recompute_input.reshape(1, slots * own_cols), (blk_count, slots * own_cols)
-    )
+    rows_each = block_rows // group_size
+    x_part = jnp.broadcast_to(recompute_input[None], (blk_count, slots, own_cols))
     w_part = (
         w_keyval.reshape(own_cols, blk_count, pair_cols)
         .transpose(1, 0, 2)
-        .reshape(blk_count, own_cols * pair_cols)
+        .reshape(blk_count, own_cols * pair_cols // HEAD_DIM, HEAD_DIM)
+    )
+    c_part = (
+        cache_entries.reshape(group_size, rows_each, KVH, 2 * HEAD_DIM)
+        .transpose(2, 0, 1, 3)
+        .reshape(blk_count, rows_each * 2, HEAD_DIM)
     )
     arrived = lax.all_to_all(
-        jnp.concatenate([x_part, w_part], axis=1), "blk", 0, 0, tiled=True
-    )
-    wide = (
-        arrived[:, : slots * own_cols]
-        .reshape(blk_count, slots, own_cols)
-        .transpose(1, 0, 2)
-        .reshape(slots, width)
-        .astype(jnp.float32)
-    )
-    kv_cols = arrived[:, slots * own_cols :].reshape(width, pair_cols)
-
-    pieces = []
-    for step in range(chunks_per_span):
-        chosen = (blk_index % chunks_per_span + step) % KVH
-        pairs = [
-            (k, ((k % chunks_per_span + step) % KVH) * group_size + k // chunks_per_span)
-            for k in range(blk_count)
-        ]
-        outgoing = lax.dynamic_index_in_dim(cache_entries, chosen, 1, keepdims=False)
-        pieces.append(lax.ppermute(outgoing, "blk", pairs))
-    stacked = jnp.stack(pieces)
-    order = (group - jnp.arange(chunks_per_span, dtype=jnp.int32)) % KVH
-    stored = jnp.take(stacked, order, axis=0).reshape(SPAN, 2 * HEAD_DIM)
-
-    gains = norm_gain.astype(jnp.float32)
-    scaled = (wide * gains[None, :]).astype(jnp.bfloat16)
-    square_acc = jnp.sum(wide * wide, axis=1)
+        jnp.concatenate([x_part, w_part, c_part], axis=1), "blk", 0, 0, tiled=True
+    )
+    w_rows = own_cols * pair_cols // HEAD_DIM
+    wide = arrived[:, :slots].astype(jnp.float32)
+    kv_cols = arrived[:, slots : slots + w_rows].reshape(blk_count, own_cols, pair_cols)
+    stored = arrived[:, slots + w_rows :].reshape(blk_count * rows_each, 2 * HEAD_DIM)
+
+    gains = norm_gain.astype(jnp.float32).reshape(blk_count, 1, own_cols)
+    scaled = (wide * gains).astype(jnp.bfloat16)
+    square_acc = jnp.sum(wide * wide, axis=(0, 2))
     inv_rms = lax.rsqrt(square_acc / width + NORM_EPS)
-    query_acc = jnp.dot(scaled, w_query, preferred_element_type=jnp.float32) * inv_rms[:, None]
-    pair_piece = jnp.dot(scaled, kv_cols, preferred_element_type=jnp.float32) * inv_rms[:, None]
+    query_acc = jnp.einsum(
+        "ksc,kcd->sd",
+        scaled,
+        w_query.reshape(blk_count, own_cols, HEAD_DIM),
+        preferred_element_type=jnp.float32,
+    ) * inv_rms[:, None]
+    pair_piece = jnp.einsum(
+        "ksc,kcd->sd", scaled, kv_cols, preferred_element_type=jnp.float32
+    ) * inv_rms[:, None]
     shared = group_gather(jnp.concatenate([query_acc, pair_piece], axis=1), "blk", group_size)
     group_pair = shared[:, :, HEAD_DIM:].transpose(1, 0, 2).reshape(slots, group_size * pair_cols)
 
@@ -183,18 +181,22 @@
         jnp.bfloat16
     )
 
-    offset = lax.dynamic_index_in_dim(
-        rotate_offsets, kv_index * spans_here + member, 0, keepdims=False
-    )
-    row_shifts = jnp.full((SPAN,), offset, dtype=jnp.int32)
+    local_rows = jnp.arange(blk_count * rows_each, dtype=jnp.int32)
+    stored_rows = (local_rows // rows_each) * block_rows + member * rows_each + local_rows % rows_each
+    key_pos = joined_rows(span_order, kv_index, spans_here, stored_rows)
+    offsets = lax.dynamic_slice_in_dim(rotate_offsets, kv_index * spans_here, spans_here, 0)
+    row_shifts = jnp.take(offsets, stored_rows // SPAN)
     turned_rows = rotate_half(stored[:, :HEAD_DIM].astype(jnp.float32), row_shifts).astype(
         jnp.bfloat16
     )
     stored = jnp.concatenate([turned_rows, stored[:, HEAD_DIM:]], axis=-1)
-    own_slot = joined_slot(span_order, kv_index, spans_here, member)
-    place = jnp.where(live & (own_pos // SPAN == own_slot), own_pos % SPAN, SPAN)
+    local_order = lax.dynamic_slice_in_dim(span_order, kv_index * spans_here, spans_here, 0)
+    slot_rows = (jnp.take(local_order, own_pos // SPAN) - kv_index * spans_here) * SPAN + own_pos % SPAN
+    mine = live & ((slot_rows % block_rows) // rows_each == member)
+    place = jnp.where(
+        mine, (slot_rows // block_rows) * rows_each + slot_rows % rows_each, blk_count * rows_each
+    )
     merged = stored.at[place].set(jnp.concatenate([fresh_keys, fresh_values], axis=1), mode="drop")
-    key_pos = kv_index * shard_len + own_slot * SPAN + jnp.arange(SPAN, dtype=jnp.int32)
     query_tenant = tenant_lookup(query_pos, tenant_of_span)
     own_part = attend_part(
         queries,
@@ -206,10 +208,8 @@
         tenant_lookup(key_pos, tenant_of_span),
     )
     prior = shifted(merged, "kv", 1)
-    prior_slot = joined_slot(span_order, jnp.maximum(kv_index - 1, 0), spans_here, member)
-    prior_pos = (
-        (kv_index - 1) * shard_len + prior_slot * SPAN + jnp.arange(SPAN, dtype=jnp.int32)
-    )
+    prior_pos = joined_rows(span_order, jnp.maximum(kv_index - 1, 0), spans_here, stored_rows)
+    prior_pos = jnp.where(kv_index > 0, prior_pos, -1)
     prior_part = attend_part(
         queries,
         query_pos,

time: 304 us -> 258 us (0.85)
  the two profiles are of different devices: /device:TPU:124 before, /device:TPU:46 now
where the time goes in v3:
time: 258 us; the launch traced here: 257 us
  waiting for transfers between devices  142 us (55%)
  starting transfers between devices  56.4 us (22%)
  other arithmetic  35 us (14%)
  local copies, waits for them, and re-layouts  13.3 us (5%)
  matrix products  9.35 us (4%)
    all_to_all x1, waiting for transfers between devices, local(): arrived_terms = lax.all_to_all(term_blocks, 'blk', 1, 1, tiled=True)  63 us
    all_to_all x1, waiting for transfers between devices, local(): lax.all_to_all(jnp.concatenate([x_part, w_part, c_part], axis=1), 'blk',...  59.4 us
    ppermute x3, starting transfers between devices, group_exchange(): mine.append(lax.ppermute(outgoing, axis, pairs))  17.9 us
    all_to_all x1, starting transfers between devices, local(): lax.all_to_all(jnp.concatenate([x_part, w_part, c_part], axis=1), 'blk',...  15.9 us
    all_to_all x1, starting transfers between devices, local(): arrived_terms = lax.all_to_all(term_blocks, 'blk', 1, 1, tiled=True)  10.6 us
    ppermute x3, starting transfers between devices, group_gather(): pieces.append(lax.ppermute(piece, axis, pairs))  9.86 us
    select_n x3, other arithmetic, tenant_lookup(): span_ids = positions // SPAN  8.96 us
    ppermute x3, waiting for transfers between devices, group_gather(): pieces.append(lax.ppermute(piece, axis, pairs))  7.01 us
  transfers between devices with their start and end apart: 9, of which 7 were waited for; matrix products, arithmetic and copies ran while one was open for 13% of the time, Pallas kernels for 0%

profile of v3, /device:TPU:46, one launch (start us, length us, event | category | flops | bytes accessed | tf_op | source)
XLA Modules:
  0.0 257.1 jit_solution(1650359797014070111)
XLA Ops:
  0.0 1.4 copy.103
  3.2 1.8 pad_maximum_fusion
  5.1 15.9 %all-to-all-start = ((bf16[32,384,128]{2,1,0:T(8,128)(2,1)}), bf16[32,384,128]{2,1,0:T(8,128)(2,1)}, u32[]{:S(2)}, u32[]{:S(2)}) async-start(bf16[32,384,128]{2,1,0:T(8,128)(2,1)} %pad_maximum_fusion), calls=%async_computation | async-start | bytes 6291456 | tf_op jit(solution)/shard_map/all_to_all | solution.py:150
  22.5 3.9 %and_select_fusion.10 = (s32[256]{0:T(256)S(1)}, s32[256]{0:T(256)S(1)}, s32[256]{0:T(256)S(1)}) fusion(s32[4096]{0:T(1024)} %param.22, s32[]{:T(128)S(6)} %select_n.209, s32[]{:T(128)S(6)} %mul.234, s32[]{:T(128)S(6)} %select_n.215, s32[]{:T(128)S(6)} %mul.236, s32[]{:T(128)} %bitcast.16, s32[]{:T(128)} %bitcast.15, s32[]{:T(128)} %bitcast.14, ...), kind=kLoop, calls=%fused_computation.182 | loop fusion | flops 26112 | bytes 4132 | tf_op jit(solution)/shard_map/jit(floor_divide)/jit(_where)/select_n | solution.py:42
  27.3 2.5 broadcast_compare_fusion.2
  30.5 2.5 broadcast_compare_fusion.3
  33.0 2.5 fusion.76
  35.5 2.5 add_select_fusion
  38.1 2.5 add_select_fusion.1
  40.6 2.5 fusion.78
  43.7 2.5 select_convert_fusion.1
  46.5 2.2 fusion.42
  48.7 59.4 %all-to-all-done = bf16[32,384,128]{2,1,0:T(8,128)(2,1)} async-done(((bf16[32,384,128]{2,1,0:T(8,128)(2,1)}), bf16[32,384,128]{2,1,0:T(8,128)(2,1)}, u32[]{:S(2)}, u32[]{:S(2)}) %all-to-all-start) | async-done | bytes 3145760 | tf_op jit(solution)/shard_map/all_to_all | solution.py:150
  108.1 1.3 fusion.100
  109.8 2.2 fusion.1
  112.0 2.3 fusion.37
  114.3 2.4 fusion.31
  117.4 1.9 collective-permute-start
  119.4 1.9 collective-permute-start.1
  121.3 6.0 %collective-permute-start.2 = (f32[256,192]{0,1:T(8,128)}, f32[256,192]{0,1:T(8,128)S(1)}, u32[]{:S(2)}, u32[]{:S(2)}) collective-permute-start(f32[256,192]{0,1:T(8,128)} %get-tuple-element.30), channel_id=1, source_target_pairs={{0,48},{16,0},{32,16},{48,32},{64,112},{80,64},{96,80},{112,96},{1... | collective-permute-start | bytes 589832 | tf_op jit(solution)/shard_map/ppermute | solution.py:83
  129.5 4.7 %collective-permute-done = f32[256,192]{0,1:T(8,128)S(1)} collective-permute-done((f32[256,192]{0,1:T(8,128)}, f32[256,192]{0,1:T(8,128)S(1)}, u32[]{:S(2)}, u32[]{:S(2)}) %collective-permute-start) | collective-permute-done | bytes 196640 | tf_op jit(solution)/shard_map/ppermute | solution.py:83
  134.2 2.3 collective-permute-done.2
  137.9 1.8 scatter_fusion
  139.7 2.1 collective-permute-start.3
  143.7 6.4 %collective-permute-done.3 = bf16[1024,256]{1,0:T(8,128)(2,1)S(1)} collective-permute-done((bf16[1024,256]{1,0:T(8,128)(2,1)S(1)}, bf16[1024,256]{1,0:T(8,128)(2,1)S(1)}, u32[]{:S(2)}, u32[]{:S(2)}) %collective-permute-start.3) | collective-permute-done | bytes 524320 | tf_op jit(solution)/shard_map/ppermute | solution.py:24
  154.5 10.5 %collective-permute-start.4 = (f32[256,130]{0,1:T(8,128)S(1)}, f32[256,130]{0,1:T(8,128)S(1)}, u32[]{:S(2)}, u32[]{:S(2)}) collective-permute-start(f32[256,130]{0,1:T(8,128)S(1)} %get-tuple-element.22), channel_id=1, source_target_pairs={{0,16},{16,32},{32,48},{48,0},{64,80},{80,96},{96,112},{112,64},{1... | collective-permute-start | bytes 399368 | tf_op jit(solution)/shard_map/ppermute | solution.py:96
  165.0 1.9 collective-permute-start.5
  167.0 5.5 %collective-permute-start.6 = (f32[256,130]{0,1:T(8,128)S(1)}, f32[256,130]{0,1:T(8,128)S(1)}, u32[]{:S(2)}, u32[]{:S(2)}) collective-permute-start(f32[256,130]{0,1:T(8,128)S(1)} %get-tuple-element.20), channel_id=1, source_target_pairs={{0,48},{16,0},{32,16},{48,32},{64,112},{80,64},{96,80},{112,96},{1... | collective-permute-start | bytes 399368 | tf_op jit(solution)/shard_map/ppermute | solution.py:96
  172.5 5.4 %collective-permute-done.5 = f32[256,130]{0,1:T(8,128)S(1)} collective-permute-done((f32[256,130]{0,1:T(8,128)S(1)}, f32[256,130]{0,1:T(8,128)S(1)}, u32[]{:S(2)}, u32[]{:S(2)}) %collective-permute-start.5) | collective-permute-done | bytes 133152 | tf_op jit(solution)/shard_map/ppermute | solution.py:96
  180.0 1.9 copy.144
  181.9 10.6 %all-to-all-start.1 = ((bf16[256,32,128]{2,0,1:T(8,128)(2,1)}), bf16[256,32,128]{2,0,1:T(8,128)(2,1)S(1)}, u32[]{:S(2)}, u32[]{:S(2)}) async-start(bf16[256,32,128]{2,0,1:T(8,128)(2,1)} %bitcast.124), calls=%async_computation.1 | async-start | bytes 4194304 | tf_op jit(solution)/shard_map/all_to_all | solution.py:237
  193.1 63.0 %all-to-all-done.1 = bf16[256,32,128]{2,0,1:T(8,128)(2,1)S(1)} async-done(((bf16[256,32,128]{2,0,1:T(8,128)(2,1)}), bf16[256,32,128]{2,0,1:T(8,128)(2,1)S(1)}, u32[]{:S(2)}, u32[]{:S(2)}) %all-to-all-start.1) | async-done | bytes 2097184 | tf_op jit(solution)/shard_map/all_to_all | solution.py:237
  (84 shorter events, 20.0 us)
Async XLA Ops:
  0.0 179.2 %copy-start = (bf16[128,4096]{1,0:T(8,128)(2,1)S(1)}, bf16[128,4096]{1,0:T(8,128)(2,1)}, u32[]{:S(2)}) copy-start(bf16[128,4096]{1,0:T(8,128)(2,1)} %param.18) | copy-start | bytes 3145732
  0.0 2.4 copy-start.2
  0.0 2.7 %copy-start.3 = (bf16[256,128]{1,0:T(8,128)(2,1)S(1)}, bf16[256,128]{1,0:T(8,128)(2,1)}, u32[]{:S(2)}) copy-start(bf16[256,128]{1,0:T(8,128)(2,1)} %param.14) | copy-start | bytes 196612
  5.1 16.0 %copy-start.8 = (s32[16]{0:T(128)S(1)}, s32[16]{0:T(128)}, u32[]{:S(2)}) copy-start(s32[16]{0:T(128)} %param.23) | copy-start | bytes 196
  5.1 16.7 %copy-start.6 = (s32[64]{0:T(128)S(1)}, s32[64]{0:T(128)}, u32[]{:S(2)}) copy-start(s32[64]{0:T(128)} %param.20) | copy-start | bytes 772
  5.1 21.3 %copy-start.9 = (s32[64]{0:T(128)S(1)}, s32[64]{0:T(128)}, u32[]{:S(2)}) copy-start(s32[64]{0:T(128)} %param.19) | copy-start | bytes 772
  5.1 41.1 %copy-start.5 = (s32[64]{0:T(128)S(1)}, s32[64]{0:T(128)}, u32[]{:S(2)}) copy-start(s32[64]{0:T(128)} %param.21) | copy-start | bytes 772
  5.1 41.4 %copy-start.4 = (bf16[4096]{0:T(1024)(128)(2,1)S(1)}, bf16[4096]{0:T(1024)(128)(2,1)}, u32[]{:S(2)}) copy-start(bf16[4096]{0:T(1024)(128)(2,1)} %param.15) | copy-start | bytes 24580
  5.1 103.0 %all-to-all-start = ((bf16[32,384,128]{2,1,0:T(8,128)(2,1)}), bf16[32,384,128]{2,1,0:T(8,128)(2,1)}, u32[]{:S(2)}, u32[]{:S(2)}) async-start(bf16[32,384,128]{2,1,0:T(8,128)(2,1)} %pad_maximum_fusion), calls=%async_computation | async-start | bytes 6291456 | tf_op jit(solution)/shard_map/all_to_all | solution.py:150
  109.8 4.5 %copy-start.7 = (bf16[4096,128]{1,0:T(8,128)(2,1)S(1)}, bf16[4096,128]{1,0:T(8,128)(2,1)}, u32[]{:S(2)}) copy-start(bf16[4096,128]{1,0:T(8,128)(2,1)} %param.16) | copy-start | bytes 3145732
  117.4 16.8 %collective-permute-start = (f32[256,192]{0,1:T(8,128)}, f32[256,192]{0,1:T(8,128)S(1)}, u32[]{:S(2)}, u32[]{:S(2)}) collective-permute-start(f32[256,192]{0,1:T(8,128)} %get-tuple-element.30), channel_id=1, source_target_pairs={{0,16},{16,32},{32,48},{48,0},{64,80},{80,96},{96,112},{112,64},{1... | collective-permute-start | bytes 589832 | tf_op jit(solution)/shard_map/ppermute | solution.py:83
  119.4 14.9 %collective-permute-start.1 = (f32[256,192]{0,1:T(8,128)}, f32[256,192]{0,1:T(8,128)S(1)}, u32[]{:S(2)}, u32[]{:S(2)}) collective-permute-start(f32[256,192]{0,1:T(8,128)} %get-tuple-element.30), channel_id=1, source_target_pairs={{0,32},{16,48},{32,0},{48,16},{64,96},{80,112},{96,64},{112,80},{1... | collective-permute-start | bytes 589832 | tf_op jit(solution)/shard_map/ppermute | solution.py:83
  121.3 15.2 %collective-permute-start.2 = (f32[256,192]{0,1:T(8,128)}, f32[256,192]{0,1:T(8,128)S(1)}, u32[]{:S(2)}, u32[]{:S(2)}) collective-permute-start(f32[256,192]{0,1:T(8,128)} %get-tuple-element.30), channel_id=1, source_target_pairs={{0,48},{16,0},{32,16},{48,32},{64,112},{80,64},{96,80},{112,96},{1... | collective-permute-start | bytes 589832 | tf_op jit(solution)/shard_map/ppermute | solution.py:83
  137.3 4.5 %copy-start.1 = (pred[256,1024]{0,1:T(8,128)(4,1)S(1)}, pred[256,1024]{0,1:T(8,128)(4,1)}, u32[]{:S(2)}) copy-start(pred[256,1024]{0,1:T(8,128)(4,1)} %get-tuple-element.36) | copy-start | bytes 786436
  139.7 10.5 %collective-permute-start.3 = (bf16[1024,256]{1,0:T(8,128)(2,1)S(1)}, bf16[1024,256]{1,0:T(8,128)(2,1)S(1)}, u32[]{:S(2)}, u32[]{:S(2)}) collective-permute-start(bf16[1024,256]{1,0:T(8,128)(2,1)S(1)} %scatter_fusion), channel_id=1, source_target_pairs={{0,1},{1,2},{2,3},{3,4},{4,5},{5,6},{6,7},{7,8},{8,9},{9,10},{10,1... | collective-permute-start | bytes 1572872 | tf_op jit(solution)/shard_map/ppermute | solution.py:24
  154.5 18.0 %collective-permute-start.4 = (f32[256,130]{0,1:T(8,128)S(1)}, f32[256,130]{0,1:T(8,128)S(1)}, u32[]{:S(2)}, u32[]{:S(2)}) collective-permute-start(f32[256,130]{0,1:T(8,128)S(1)} %get-tuple-element.22), channel_id=1, source_target_pairs={{0,16},{16,32},{32,48},{48,0},{64,80},{80,96},{96,112},{112,64},{1... | collective-permute-start | bytes 399368 | tf_op jit(solution)/shard_map/ppermute | solution.py:96
  165.0 12.9 %collective-permute-start.5 = (f32[256,130]{0,1:T(8,128)S(1)}, f32[256,130]{0,1:T(8,128)S(1)}, u32[]{:S(2)}, u32[]{:S(2)}) collective-permute-start(f32[256,130]{0,1:T(8,128)S(1)} %get-tuple-element.21), channel_id=1, source_target_pairs={{0,32},{16,48},{32,0},{48,16},{64,96},{80,112},{96,64},{112,80},{1... | collective-permute-start | bytes 399368 | tf_op jit(solution)/shard_map/ppermute | solution.py:96
  167.0 12.1 %collective-permute-start.6 = (f32[256,130]{0,1:T(8,128)S(1)}, f32[256,130]{0,1:T(8,128)S(1)}, u32[]{:S(2)}, u32[]{:S(2)}) collective-permute-start(f32[256,130]{0,1:T(8,128)S(1)} %get-tuple-element.20), channel_id=1, source_target_pairs={{0,48},{16,0},{32,16},{48,32},{64,112},{80,64},{96,80},{112,96},{1... | collective-permute-start | bytes 399368 | tf_op jit(solution)/shard_map/ppermute | solution.py:96
  181.9 74.2 %all-to-all-start.1 = ((bf16[256,32,128]{2,0,1:T(8,128)(2,1)}), bf16[256,32,128]{2,0,1:T(8,128)(2,1)S(1)}, u32[]{:S(2)}, u32[]{:S(2)}) async-start(bf16[256,32,128]{2,0,1:T(8,128)(2,1)} %bitcast.124), calls=%async_computation.1 | async-start | bytes 4194304 | tf_op jit(solution)/shard_map/all_to_all | solution.py:237

commit v4 on v3

--- a/solution.py
+++ b/solution.py
@@ -147,13 +147,13 @@
         .transpose(2, 0, 1, 3)
         .reshape(blk_count, rows_each * 2, HEAD_DIM)
     )
-    arrived = lax.all_to_all(
-        jnp.concatenate([x_part, w_part, c_part], axis=1), "blk", 0, 0, tiled=True
-    )
-    w_rows = own_cols * pair_cols // HEAD_DIM
+    arrived = lax.all_to_all(jnp.concatenate([x_part, w_part], axis=1), "blk", 0, 0, tiled=True)
     wide = arrived[:, :slots].astype(jnp.float32)
-    kv_cols = arrived[:, slots : slots + w_rows].reshape(blk_count, own_cols, pair_cols)
-    stored = arrived[:, slots + w_rows :].reshape(blk_count * rows_each, 2 * HEAD_DIM)
+    kv_cols = arrived[:, slots:].reshape(blk_count, own_cols, pair_cols)
+    arrived, c_part = lax.optimization_barrier((arrived, c_part))
+    stored = lax.all_to_all(c_part, "blk", 0, 0, tiled=True).reshape(
+        blk_count * rows_each, 2 * HEAD_DIM
+    )
 
     gains = norm_gain.astype(jnp.float32).reshape(blk_count, 1, own_cols)
     scaled = (wide * gains).astype(jnp.bfloat16)

time: 258 us -> 253 us (0.981)
  the two profiles are of different devices: /device:TPU:46 before, /device:TPU:14 now
where the time goes in v4:
time: 253 us; the launch traced here: 252 us
  starting transfers between devices  97.9 us (39%)
  waiting for transfers between devices  95 us (38%)
  other arithmetic  34.9 us (14%)
  local copies, waits for them, and re-layouts  14 us (6%)
  matrix products  9.58 us (4%)
    all_to_all x1, waiting for transfers between devices, local(): lax.all_to_all(jnp.concatenate([x_part, w_part], axis=1), 'blk', 0, 0, ti...  37.5 us
    all_to_all x1, starting transfers between devices, local(): arrived_terms = lax.all_to_all(term_blocks, 'blk', 1, 1, tiled=True)  31.8 us
    all_to_all x1, waiting for transfers between devices, local(): arrived_terms = lax.all_to_all(term_blocks, 'blk', 1, 1, tiled=True)  28.8 us
    all_to_all x1, starting transfers between devices, local(): lax.all_to_all(c_part, 'blk', 0, 0, tiled=True)  21.2 us
    all_to_all x1, starting transfers between devices, local(): lax.all_to_all(jnp.concatenate([x_part, w_part], axis=1), 'blk', 0, 0, ti...  16.4 us
    ppermute x3, starting transfers between devices, group_gather(): pieces.append(lax.ppermute(piece, axis, pairs))  15.2 us
    all_to_all x1, waiting for transfers between devices, local(): lax.all_to_all(c_part, 'blk', 0, 0, tiled=True)  13.8 us
    ppermute x3, starting transfers between devices, group_exchange(): mine.append(lax.ppermute(outgoing, axis, pairs))  11.3 us
  transfers between devices with their start and end apart: 10, of which 6 were waited for; matrix products, arithmetic and copies ran while one was open for 13% of the time, Pallas kernels for 0%

profile of v4, /device:TPU:14, one launch (start us, length us, event | category | flops | bytes accessed | tf_op | source)
XLA Modules:
  0.0 252.1 jit_solution(14477901162369765428)
XLA Ops:
  0.0 1.4 copy.102
  2.9 1.7 pad_maximum_fusion
  4.7 16.4 %all-to-all-start = ((bf16[32,320,128]{2,1,0:T(8,128)(2,1)}), bf16[32,320,128]{2,1,0:T(8,128)(2,1)}, u32[]{:S(2)}, u32[]{:S(2)}) async-start(bf16[32,320,128]{2,1,0:T(8,128)(2,1)} %pad_maximum_fusion), calls=%async_computation | async-start | bytes 5242880 | tf_op jit(solution)/shard_map/all_to_all | solution.py:150
  22.5 3.9 %and_select_fusion.10 = (s32[256]{0:T(256)S(1)}, s32[256]{0:T(256)S(1)}, s32[256]{0:T(256)S(1)}) fusion(s32[4096]{0:T(1024)} %param.22, s32[]{:T(128)S(6)} %select_n.209, s32[]{:T(128)S(6)} %mul.234, s32[]{:T(128)S(6)} %select_n.215, s32[]{:T(128)S(6)} %mul.236, s32[]{:T(128)} %bitcast.16, s32[]{:T(128)} %bitcast.15, s32[]{:T(128)} %bitcast.14, ...), kind=kLoop, calls=%fused_computation.183 | loop fusion | flops 26112 | bytes 4132 | tf_op jit(solution)/shard_map/jit(floor_divide)/jit(_where)/select_n | solution.py:42
  28.4 2.5 broadcast_compare_fusion.2
  31.6 2.6 %broadcast_compare_fusion.3 = pred[1024]{0:T(1024)(128)(4,1)S(1)} fusion(s32[]{:T(128)} %bitcast.36, s32[]{:T(128)} %bitcast.35, s32[]{:T(128)} %bitcast.34, s32[]{:T(128)} %bitcast.33, s32[]{:T(128)S(6)} %mul.239, s32[]{:T(128)S(6)} %mul.274, pred[]{:T(512)S(6)} %gt.3), kind=kLoop, calls=%fused_computation.165 | loop fusion | flops 53248 | bytes 1049 | tf_op jit(solution)/shard_map/ge | solution.py:56
  34.2 2.6 %fusion.76 = s32[1024]{0:T(1024)S(1)} fusion(s32[]{:T(128)} %bitcast.36, s32[]{:T(128)} %bitcast.35, s32[]{:T(128)} %bitcast.34, s32[]{:T(128)} %bitcast.33, s32[]{:T(128)S(6)} %mul.274, s32[]{:T(128)S(6)} %mul.239, pred[]{:T(512)S(6)} %gt.3), kind=kLoop, calls=%fused_computation.136 | loop fusion | flops 52224 | bytes 4121 | tf_op jit(solution)/shard_map/jit(_where)/select_n | solution.py:212
  36.8 2.6 %add_select_fusion = s32[1024]{0:T(1024)S(1)} fusion(s32[]{:T(128)} %bitcast.36, s32[]{:T(128)} %bitcast.35, s32[]{:T(128)} %bitcast.34, s32[]{:T(128)} %bitcast.33, s32[]{:T(128)S(6)} %mul.239, s32[]{:T(128)S(6)} %mul.274, pred[]{:T(512)S(6)} %gt.3), kind=kLoop, calls=%fused_computation.100 | loop fusion | flops 67584 | bytes 4121 | tf_op jit(solution)/shard_map/jit(floor_divide)/jit(_where)/select_n | solution.py:42
  39.4 2.5 add_select_fusion.1
  41.9 2.5 fusion.78
  45.0 2.5 select_convert_fusion.1
  47.8 37.5 %all-to-all-done = bf16[32,320,128]{2,1,0:T(8,128)(2,1)} async-done(((bf16[32,320,128]{2,1,0:T(8,128)(2,1)}), bf16[32,320,128]{2,1,0:T(8,128)(2,1)}, u32[]{:S(2)}, u32[]{:S(2)}) %all-to-all-start) | async-done | bytes 2621472 | tf_op jit(solution)/shard_map/all_to_all | solution.py:150
  85.3 2.1 fusion.1
  88.9 2.3 fusion.37
  91.2 2.6 %fusion.31 = f32[256,128]{0,1:T(8,128)S(1)} fusion(bf16[32,128,128]{2,1,0:T(8,128)(2,1)} %bitcast.141, f32[32,128]{1,0:T(8,128)S(1)} %bitcast_convert_fusion, bf16[32,320,128]{2,1,0:T(8,128)(2,1)} %all-to-all-done, f32[256]{0:T(256)S(1)} %add_rsqrt_fusion), kind=kOutput, calls=%fused_computation.35 | convolution fusion | flops 271613952 | bytes 3294208 | tf_op jit(solution)/shard_map/ksc,kcd->sd/dot_general | solution.py:162
  93.9 3.2 %collective-permute-start = (f32[256,192]{0,1:T(8,128)S(1)}, f32[256,192]{0,1:T(8,128)S(1)}, u32[]{:S(2)}, u32[]{:S(2)}) collective-permute-start(f32[256,192]{0,1:T(8,128)S(1)} %get-tuple-element.30), channel_id=1, source_target_pairs={{0,16},{16,32},{32,48},{48,0},{64,80},{80,96},{96,112},{112,64},{1... | collective-permute-start | bytes 589832 | tf_op jit(solution)/shard_map/ppermute | solution.py:83
  97.1 10.0 %collective-permute-start.1 = (f32[256,192]{0,1:T(8,128)S(1)}, f32[256,192]{0,1:T(8,128)S(1)}, u32[]{:S(2)}, u32[]{:S(2)}) collective-permute-start(f32[256,192]{0,1:T(8,128)S(1)} %get-tuple-element.30), channel_id=1, source_target_pairs={{0,32},{16,48},{32,0},{48,16},{64,96},{80,112},{96,64},{112,80},{1... | collective-permute-start | bytes 589832 | tf_op jit(solution)/shard_map/ppermute | solution.py:83
  107.1 1.9 collective-permute-start.2
  109.1 2.2 fusion.42
  111.3 21.2 %all-to-all-start.1 = ((bf16[32,64,128]{2,1,0:T(8,128)(2,1)}), bf16[32,64,128]{2,1,0:T(8,128)(2,1)S(1)}, u32[]{:S(2)}, u32[]{:S(2)}) async-start(bf16[32,64,128]{2,1,0:T(8,128)(2,1)} %reshape.376), calls=%async_computation.1 | async-start | bytes 1048576 | tf_op jit(solution)/shard_map/all_to_all | solution.py:154
  134.7 13.8 %all-to-all-done.1 = bf16[32,64,128]{2,1,0:T(8,128)(2,1)S(1)} async-done(((bf16[32,64,128]{2,1,0:T(8,128)(2,1)}), bf16[32,64,128]{2,1,0:T(8,128)(2,1)S(1)}, u32[]{:S(2)}, u32[]{:S(2)}) %all-to-all-start.1) | async-done | bytes 524320 | tf_op jit(solution)/shard_map/all_to_all | solution.py:154
  150.7 1.8 scatter_fusion
  152.5 2.1 collective-permute-start.3
  156.5 6.5 %collective-permute-done.3 = bf16[1024,256]{1,0:T(8,128)(2,1)S(1)} collective-permute-done((bf16[1024,256]{1,0:T(8,128)(2,1)S(1)}, bf16[1024,256]{1,0:T(8,128)(2,1)S(1)}, u32[]{:S(2)}, u32[]{:S(2)}) %collective-permute-start.3) | collective-permute-done | bytes 524320 | tf_op jit(solution)/shard_map/ppermute | solution.py:24
  167.3 2.1 collective-permute-start.4
  169.4 5.1 %collective-permute-start.5 = (f32[256,130]{0,1:T(8,128)S(1)}, f32[256,130]{0,1:T(8,128)S(1)}, u32[]{:S(2)}, u32[]{:S(2)}) collective-permute-start(f32[256,130]{0,1:T(8,128)S(1)} %get-tuple-element.21), channel_id=1, source_target_pairs={{0,32},{16,48},{32,0},{48,16},{64,96},{80,112},{96,64},{112,80},{1... | collective-permute-start | bytes 399368 | tf_op jit(solution)/shard_map/ppermute | solution.py:96
  174.5 4.1 %collective-permute-start.6 = (f32[256,130]{0,1:T(8,128)S(1)}, f32[256,130]{0,1:T(8,128)S(1)}, u32[]{:S(2)}, u32[]{:S(2)}) collective-permute-start(f32[256,130]{0,1:T(8,128)S(1)} %get-tuple-element.20), channel_id=1, source_target_pairs={{0,48},{16,0},{32,16},{48,32},{64,112},{80,64},{96,80},{112,96},{1... | collective-permute-start | bytes 399368 | tf_op jit(solution)/shard_map/ppermute | solution.py:96
  178.6 1.7 collective-permute-done.5
  180.3 6.7 %collective-permute-done.6 = f32[256,130]{0,1:T(8,128)S(1)} collective-permute-done((f32[256,130]{0,1:T(8,128)S(1)}, f32[256,130]{0,1:T(8,128)S(1)}, u32[]{:S(2)}, u32[]{:S(2)}) %collective-permute-start.6) | collective-permute-done | bytes 133152 | tf_op jit(solution)/shard_map/ppermute | solution.py:96
  187.9 1.9 copy.144
  189.9 31.8 %all-to-all-start.2 = ((bf16[256,32,128]{2,0,1:T(8,128)(2,1)}), bf16[256,32,128]{2,0,1:T(8,128)(2,1)S(1)}, u32[]{:S(2)}, u32[]{:S(2)}) async-start(bf16[256,32,128]{2,0,1:T(8,128)(2,1)} %bitcast.125), calls=%async_computation.2 | async-start | bytes 4194304 | tf_op jit(solution)/shard_map/all_to_all | solution.py:237
  222.2 28.8 %all-to-all-done.2 = bf16[256,32,128]{2,0,1:T(8,128)(2,1)S(1)} async-done(((bf16[256,32,128]{2,0,1:T(8,128)(2,1)}), bf16[256,32,128]{2,0,1:T(8,128)(2,1)S(1)}, u32[]{:S(2)}, u32[]{:S(2)}) %all-to-all-start.2) | async-done | bytes 2097184 | tf_op jit(solution)/shard_map/all_to_all | solution.py:237
  (88 shorter events, 20.7 us)
Async XLA Ops:
  0.0 187.2 %copy-start = (bf16[128,4096]{1,0:T(8,128)(2,1)S(1)}, bf16[128,4096]{1,0:T(8,128)(2,1)}, u32[]{:S(2)}) copy-start(bf16[128,4096]{1,0:T(8,128)(2,1)} %param.18) | copy-start | bytes 3145732
  0.0 2.4 copy-start.5
  2.9 18.2 %copy-start.9 = (s32[16]{0:T(128)S(1)}, s32[16]{0:T(128)}, u32[]{:S(2)}) copy-start(s32[16]{0:T(128)} %param.23) | copy-start | bytes 196
  2.9 18.8 %copy-start.8 = (s32[64]{0:T(128)S(1)}, s32[64]{0:T(128)}, u32[]{:S(2)}) copy-start(s32[64]{0:T(128)} %param.20) | copy-start | bytes 772
  2.9 23.5 %copy-start.10 = (s32[64]{0:T(128)S(1)}, s32[64]{0:T(128)}, u32[]{:S(2)}) copy-start(s32[64]{0:T(128)} %param.19) | copy-start | bytes 772
  2.9 23.5 %copy-start.2 = (bf16[128,8,256]{2,1,0:T(8,128)(2,1)S(1)}, bf16[128,8,256]{2,1,0:T(8,128)(2,1)}, u32[]{:S(2)}) copy-start(bf16[128,8,256]{2,1,0:T(8,128)(2,1)} %param.13) | copy-start | bytes 1572868
  4.7 42.8 %copy-start.7 = (s32[64]{0:T(128)S(1)}, s32[64]{0:T(128)}, u32[]{:S(2)}) copy-start(s32[64]{0:T(128)} %param.21) | copy-start | bytes 772
  4.7 43.1 %copy-start.6 = (bf16[4096]{0:T(1024)(128)(2,1)S(1)}, bf16[4096]{0:T(1024)(128)(2,1)}, u32[]{:S(2)}) copy-start(bf16[4096]{0:T(1024)(128)(2,1)} %param.15) | copy-start | bytes 24580
  4.7 80.6 %all-to-all-start = ((bf16[32,320,128]{2,1,0:T(8,128)(2,1)}), bf16[32,320,128]{2,1,0:T(8,128)(2,1)}, u32[]{:S(2)}, u32[]{:S(2)}) async-start(bf16[32,320,128]{2,1,0:T(8,128)(2,1)} %pad_maximum_fusion), calls=%async_computation | async-start | bytes 5242880 | tf_op jit(solution)/shard_map/all_to_all | solution.py:150
  93.9 38.7 %collective-permute-start = (f32[256,192]{0,1:T(8,128)S(1)}, f32[256,192]{0,1:T(8,128)S(1)}, u32[]{:S(2)}, u32[]{:S(2)}) collective-permute-start(f32[256,192]{0,1:T(8,128)S(1)} %get-tuple-element.30), channel_id=1, source_target_pairs={{0,16},{16,32},{32,48},{48,0},{64,80},{80,96},{96,112},{112,64},{1... | collective-permute-start | bytes 589832 | tf_op jit(solution)/shard_map/ppermute | solution.py:83
  97.1 35.4 %collective-permute-start.1 = (f32[256,192]{0,1:T(8,128)S(1)}, f32[256,192]{0,1:T(8,128)S(1)}, u32[]{:S(2)}, u32[]{:S(2)}) collective-permute-start(f32[256,192]{0,1:T(8,128)S(1)} %get-tuple-element.30), channel_id=1, source_target_pairs={{0,32},{16,48},{32,0},{48,16},{64,96},{80,112},{96,64},{112,80},{1... | collective-permute-start | bytes 589832 | tf_op jit(solution)/shard_map/ppermute | solution.py:83
  107.1 25.4 %collective-permute-start.2 = (f32[256,192]{0,1:T(8,128)S(1)}, f32[256,192]{0,1:T(8,128)S(1)}, u32[]{:S(2)}, u32[]{:S(2)}) collective-permute-start(f32[256,192]{0,1:T(8,128)S(1)} %get-tuple-element.30), channel_id=1, source_target_pairs={{0,48},{16,0},{32,16},{48,32},{64,112},{80,64},{96,80},{112,96},{1... | collective-permute-start | bytes 589832 | tf_op jit(solution)/shard_map/ppermute | solution.py:83
  111.3 37.2 %all-to-all-start.1 = ((bf16[32,64,128]{2,1,0:T(8,128)(2,1)}), bf16[32,64,128]{2,1,0:T(8,128)(2,1)S(1)}, u32[]{:S(2)}, u32[]{:S(2)}) async-start(bf16[32,64,128]{2,1,0:T(8,128)(2,1)} %reshape.376), calls=%async_computation.1 | async-start | bytes 1048576 | tf_op jit(solution)/shard_map/all_to_all | solution.py:154
  134.7 19.9 %copy-start.1 = (pred[256,1024]{0,1:T(8,128)(4,1)S(1)}, pred[256,1024]{0,1:T(8,128)(4,1)}, u32[]{:S(2)}) copy-start(pred[256,1024]{0,1:T(8,128)(4,1)} %get-tuple-element.36) | copy-start | bytes 786436
  148.7 5.9 %copy-start.3 = (bf16[256,4,64]{0,2,1:T(8,128)(2,1)S(1)}, bf16[256,4,64]{0,2,1:T(8,128)(2,1)}, u32[]{:S(2)}) copy-start(bf16[256,4,64]{0,2,1:T(8,128)(2,1)} %get-tuple-element.16) | copy-start | bytes 393220
  148.7 5.9 %copy-start.4 = (bf16[256,4,64]{0,2,1:T(8,128)(2,1)S(1)}, bf16[256,4,64]{0,2,1:T(8,128)(2,1)}, u32[]{:S(2)}) copy-start(bf16[256,4,64]{0,2,1:T(8,128)(2,1)} %get-tuple-element.17) | copy-start | bytes 393220
  152.5 10.5 %collective-permute-start.3 = (bf16[1024,256]{1,0:T(8,128)(2,1)S(1)}, bf16[1024,256]{1,0:T(8,128)(2,1)S(1)}, u32[]{:S(2)}, u32[]{:S(2)}) collective-permute-start(bf16[1024,256]{1,0:T(8,128)(2,1)S(1)} %scatter_fusion), channel_id=1, source_target_pairs={{0,1},{1,2},{2,3},{3,4},{4,5},{5,6},{6,7},{7,8},{8,9},{9,10},{10,1... | collective-permute-start | bytes 1572872 | tf_op jit(solution)/shard_map/ppermute | solution.py:24
  167.3 11.3 %collective-permute-start.4 = (f32[256,130]{0,1:T(8,128)S(1)}, f32[256,130]{0,1:T(8,128)S(1)}, u32[]{:S(2)}, u32[]{:S(2)}) collective-permute-start(f32[256,130]{0,1:T(8,128)S(1)} %get-tuple-element.22), channel_id=1, source_target_pairs={{0,16},{16,32},{32,48},{48,0},{64,80},{80,96},{96,112},{112,64},{1... | collective-permute-start | bytes 399368 | tf_op jit(solution)/shard_map/ppermute | solution.py:96
  169.4 11.0 %collective-permute-start.5 = (f32[256,130]{0,1:T(8,128)S(1)}, f32[256,130]{0,1:T(8,128)S(1)}, u32[]{:S(2)}, u32[]{:S(2)}) collective-permute-start(f32[256,130]{0,1:T(8,128)S(1)} %get-tuple-element.21), channel_id=1, source_target_pairs={{0,32},{16,48},{32,0},{48,16},{64,96},{80,112},{96,64},{112,80},{1... | collective-permute-start | bytes 399368 | tf_op jit(solution)/shard_map/ppermute | solution.py:96
  174.5 12.5 %collective-permute-start.6 = (f32[256,130]{0,1:T(8,128)S(1)}, f32[256,130]{0,1:T(8,128)S(1)}, u32[]{:S(2)}, u32[]{:S(2)}) collective-permute-start(f32[256,130]{0,1:T(8,128)S(1)} %get-tuple-element.20), channel_id=1, source_target_pairs={{0,48},{16,0},{32,16},{48,32},{64,112},{80,64},{96,80},{112,96},{1... | collective-permute-start | bytes 399368 | tf_op jit(solution)/shard_map/ppermute | solution.py:96
  189.9 61.2 %all-to-all-start.2 = ((bf16[256,32,128]{2,0,1:T(8,128)(2,1)}), bf16[256,32,128]{2,0,1:T(8,128)(2,1)S(1)}, u32[]{:S(2)}, u32[]{:S(2)}) async-start(bf16[256,32,128]{2,0,1:T(8,128)(2,1)} %bitcast.125), calls=%async_computation.2 | async-start | bytes 4194304 | tf_op jit(solution)/shard_map/all_to_all | solution.py:237

commit v5 on v4

--- a/solution.py
+++ b/solution.py
@@ -14,6 +14,7 @@
 
 
 NEG_FILL = -1e30
+RING_FAST = 4
 ROPE_BASE = 10000.0
 NORM_EPS = 1e-05
 
@@ -72,6 +73,30 @@
     totals = first[1] * scale_one + second[1] * scale_two
     summed = first[2] * scale_one[..., None] + second[2] * scale_two[..., None]
     return summed / totals[..., None]
+
+
+def ring_pairs(devices, size, stride, shift):
+    pairs = []
+    for i in range(devices):
+        coord = (i // stride) % size
+        pairs.append((i, i + ((coord + shift) % size - coord) * stride))
+    return pairs
+
+
+def ring_gather(piece, axis, size, stride):
+    devices = lax.axis_size(axis)
+    coord = (lax.axis_index(axis) // stride) % size
+    by_offset = {0: piece}
+    forward = piece
+    backward = piece
+    for step in range(1, size // 2 + 1):
+        forward = lax.ppermute(forward, axis, ring_pairs(devices, size, stride, 1))
+        by_offset[(-step) % size] = forward
+        if step < size - step:
+            backward = lax.ppermute(backward, axis, ring_pairs(devices, size, stride, -1))
+            by_offset[step] = backward
+    stacked = jnp.stack([by_offset[o] for o in range(size)])
+    return jnp.take(stacked, (jnp.arange(size, dtype=jnp.int32) - coord) % size, axis=0)
 
 
 def group_gather(piece, axis, size):
@@ -136,7 +161,6 @@
     group = blk_index // group_size
 
     rows_each = block_rows // group_size
-    x_part = jnp.broadcast_to(recompute_input[None], (blk_count, slots, own_cols))
     w_part = (
         w_keyval.reshape(own_cols, blk_count, pair_cols)
         .transpose(1, 0, 2)
@@ -147,13 +171,13 @@
         .transpose(2, 0, 1, 3)
         .reshape(blk_count, rows_each * 2, HEAD_DIM)
     )
-    arrived = lax.all_to_all(jnp.concatenate([x_part, w_part], axis=1), "blk", 0, 0, tiled=True)
-    wide = arrived[:, :slots].astype(jnp.float32)
-    kv_cols = arrived[:, slots:].reshape(blk_count, own_cols, pair_cols)
-    arrived, c_part = lax.optimization_barrier((arrived, c_part))
-    stored = lax.all_to_all(c_part, "blk", 0, 0, tiled=True).reshape(
-        blk_count * rows_each, 2 * HEAD_DIM
-    )
+    w_rows = w_part.shape[1]
+    near = ring_gather(recompute_input, "blk", RING_FAST, 1)
+    wide = ring_gather(near, "blk", blk_count // RING_FAST, RING_FAST)
+    wide = wide.reshape(blk_count, slots, own_cols).astype(jnp.float32)
+    moved = lax.all_to_all(jnp.concatenate([w_part, c_part], axis=1), "blk", 0, 0, tiled=True)
+    kv_cols = moved[:, :w_rows].reshape(blk_count, own_cols, pair_cols)
+    stored = moved[:, w_rows:].reshape(blk_count * rows_each, 2 * HEAD_DIM)
 
     gains = norm_gain.astype(jnp.float32).reshape(blk_count, 1, own_cols)
     scaled = (wide * gains).astype(jnp.bfloat16)

time: 253 us -> 260 us (1.028)
  the two profiles are of different devices: /device:TPU:14 before, /device:TPU:50 now
where the time goes in v5:
time: 260 us; the launch traced here: 258 us
  starting transfers between devices  95.9 us (37%)
  waiting for transfers between devices  88.2 us (34%)
  other arithmetic  40 us (15%)
  local copies, waits for them, and re-layouts  25.9 us (10%)
  matrix products  7.46 us (3%)
    all_to_all x1, waiting for transfers between devices, local(): arrived_terms = lax.all_to_all(term_blocks, 'blk', 1, 1, tiled=True)  59.5 us
    ppermute x6, starting transfers between devices, ring_gather(): forward = lax.ppermute(forward, axis, ring_pairs(devices, size, stride, 1))  20.4 us
    ppermute x4, starting transfers between devices, ring_gather(): lax.ppermute(backward, axis, ring_pairs(devices, size, stride, -1))  17.5 us
    all_to_all x1, starting transfers between devices, local(): arrived_terms = lax.all_to_all(term_blocks, 'blk', 1, 1, tiled=True)  15.3 us
    ppermute x3, starting transfers between devices, group_exchange(): mine.append(lax.ppermute(outgoing, axis, pairs))  14.9 us
    ppermute x3, starting transfers between devices, group_gather(): pieces.append(lax.ppermute(piece, axis, pairs))  14.9 us
    all_to_all x1, starting transfers between devices, local(): lax.all_to_all(jnp.concatenate([w_part, c_part], axis=1), 'blk', 0, 0, ti...  10.8 us
    ppermute x6, waiting for transfers between devices, ring_gather(): forward = lax.ppermute(forward, axis, ring_pairs(devices, size, stride, 1))  10.2 us
  transfers between devices with their start and end apart: 19, of which 10 were waited for; matrix products, arithmetic and copies ran while one was open for 21% of the time, Pallas kernels for 0%

profile of v5, /device:TPU:50, one launch (start us, length us, event | category | flops | bytes accessed | tf_op | source)
XLA Modules:
  0.0 258.3 jit_solution(18332792956439828145)
XLA Ops:
  0.0 6.2 %collective-permute-start.1 = (bf16[256,128]{1,0:T(8,128)(2,1)}, bf16[256,128]{1,0:T(8,128)(2,1)S(1)}, u32[]{:S(2)}, u32[]{:S(2)}) collective-permute-start(bf16[256,128]{1,0:T(8,128)(2,1)} %param.14), channel_id=1, source_target_pairs={{0,16},{16,32},{32,48},{48,0},{64,80},{80,96},{96,112},{112,64},{1... | collective-permute-start | bytes 196616 | tf_op jit(solution)/shard_map/ppermute | solution.py:93
  6.2 6.8 %collective-permute-start = (bf16[256,128]{1,0:T(8,128)(2,1)}, bf16[256,128]{1,0:T(8,128)(2,1)}, u32[]{:S(2)}, u32[]{:S(2)}) collective-permute-start(bf16[256,128]{1,0:T(8,128)(2,1)} %param.14), channel_id=1, source_target_pairs={{0,48},{16,0},{32,16},{48,32},{64,112},{80,64},{96,80},{112,96},{1... | collective-permute-start | bytes 196616 | tf_op jit(solution)/shard_map/ppermute | solution.py:96
  16.8 10.8 %all-to-all-start = ((bf16[32,128,128]{2,1,0:T(8,128)(2,1)}), bf16[32,128,128]{2,1,0:T(8,128)(2,1)}, u32[]{:S(2)}, u32[]{:S(2)}) async-start(bf16[32,128,128]{2,1,0:T(8,128)(2,1)} %pad_maximum_fusion), calls=%async_computation | async-start | bytes 2097152 | tf_op jit(solution)/shard_map/all_to_all | solution.py:178
  28.5 2.5 fusion.61
  31.0 2.5 broadcast_compare_fusion.3
  33.6 2.5 add_select_fusion
  36.7 2.5 broadcast_compare_fusion.2
  39.2 2.5 add_select_fusion.1
  41.8 2.5 fusion.63
  46.3 4.5 %and_select_fusion.14 = (s32[256]{0:T(256)S(1)}, s32[256]{0:T(256)S(1)}, s32[256]{0:T(256)}) fusion(s32[4096]{0:T(1024)} %param.22, s32[]{:T(128)S(6)} %select_n.304, s32[]{:T(128)S(6)} %mul.235, s32[]{:T(128)S(6)} %select_n.310, s32[]{:T(128)S(6)} %mul.237, s32[]{:T(128)} %bitcast.16, s32[]{:T(128)} %bitcast.15, s32[]{:T(128)} %bitcast.14, s32[]{:T(128)} %bitcast.13, ...), kind=kLoop, calls=%fused_computation.213 | loop fusion | flops 26112 | bytes 4132 | tf_op jit(solution)/shard_map/jit(floor_divide)/jit(_where)/select_n | solution.py:43
  53.3 4.3 %collective-permute-start.2 = (bf16[256,128]{1,0:T(8,128)(2,1)S(1)}, bf16[256,128]{1,0:T(8,128)(2,1)S(1)}, u32[]{:S(2)}, u32[]{:S(2)}) collective-permute-start(bf16[256,128]{1,0:T(8,128)(2,1)S(1)} %collective-permute-done.1), channel_id=1, source_target_pairs={{0,16},{16,32},{32,48},{48,0},{64,80},{80,96},{96,112},{112,64},{1... | collective-permute-start | bytes 196616 | tf_op jit(solution)/shard_map/ppermute | solution.py:93
  57.6 4.6 %collective-permute-done.2 = bf16[256,128]{1,0:T(8,128)(2,1)S(1)} collective-permute-done((bf16[256,128]{1,0:T(8,128)(2,1)S(1)}, bf16[256,128]{1,0:T(8,128)(2,1)S(1)}, u32[]{:S(2)}, u32[]{:S(2)}) %collective-permute-start.2) | collective-permute-done | bytes 65568 | tf_op jit(solution)/shard_map/ppermute | solution.py:93
  63.8 2.5 collective-permute-start.6
  67.1 3.3 %collective-permute-start.3 = (bf16[4,256,128]{2,1,0:T(8,128)(2,1)S(1)}, bf16[4,256,128]{2,1,0:T(8,128)(2,1)S(1)}, u32[]{:S(2)}, u32[]{:S(2)}) collective-permute-start(bf16[4,256,128]{2,1,0:T(8,128)(2,1)S(1)} %broadcast_select_fusion.1), channel_id=1, source_target_pairs={{0,448},{16,464},{32,480},{48,496},{64,0},{80,16},{96,32},{112,48}... | collective-permute-start | bytes 786440 | tf_op jit(solution)/shard_map/ppermute | solution.py:96
  72.1 2.5 collective-permute-start.7
  75.1 2.5 select_convert_fusion.1
  77.6 3.3 %collective-permute-start.4 = (bf16[4,256,128]{2,1,0:T(8,128)(2,1)S(1)}, bf16[4,256,128]{2,1,0:T(8,128)(2,1)S(1)}, u32[]{:S(2)}, u32[]{:S(2)}) collective-permute-start(bf16[4,256,128]{2,1,0:T(8,128)(2,1)S(1)} %collective-permute-done.3), channel_id=1, source_target_pairs={{0,448},{16,464},{32,480},{48,496},{64,0},{80,16},{96,32},{112,48}... | collective-permute-start | bytes 786440 | tf_op jit(solution)/shard_map/ppermute | solution.py:96
  81.6 2.5 collective-permute-start.8
  85.9 4.1 %collective-permute-start.5 = (bf16[4,256,128]{2,1,0:T(8,128)(2,1)S(1)}, bf16[4,256,128]{2,1,0:T(8,128)(2,1)S(1)}, u32[]{:S(2)}, u32[]{:S(2)}) collective-permute-start(bf16[4,256,128]{2,1,0:T(8,128)(2,1)S(1)} %collective-permute-done.4), channel_id=1, source_target_pairs={{0,448},{16,464},{32,480},{48,496},{64,0},{80,16},{96,32},{112,48}... | collective-permute-start | bytes 786440 | tf_op jit(solution)/shard_map/ppermute | solution.py:96
  95.5 3.9 %collective-permute-done.9 = bf16[4,256,128]{2,1,0:T(8,128)(2,1)S(1)} collective-permute-done((bf16[4,256,128]{2,1,0:T(8,128)(2,1)S(1)}, bf16[4,256,128]{2,1,0:T(8,128)(2,1)S(1)}, u32[]{:S(2)}, u32[]{:S(2)}) %collective-permute-start.9) | collective-permute-done | bytes 262176 | tf_op jit(solution)/shard_map/ppermute | solution.py:93
  102.3 2.7 %gather_fusion.1 = bf16[8,4,256,128]{3,2,1,0:T(8,128)(2,1)S(1)} fusion(bf16[8,4,256,128]{3,2,1,0:T(8,128)(2,1)} %bitcast_dynamic-update-slice_fusion, s32[1024]{0:T(1024)} %pad_clamp_fusion.1), kind=kCustom, calls=%fused_computation.1 | custom fusion | bytes 4194336 | tf_op jit(solution)/shard_map/jit(_take)/gather | solution.py:99
  117.0 2.8 %collective-permute-start.10 = (f32[256,192]{0,1:T(8,128)}, f32[256,192]{0,1:T(8,128)S(1)}, u32[]{:S(2)}, u32[]{:S(2)}) collective-permute-start(f32[256,192]{0,1:T(8,128)} %get-tuple-element.30), channel_id=1, source_target_pairs={{0,16},{16,32},{32,48},{48,0},{64,80},{80,96},{96,112},{112,64},{1... | collective-permute-start | bytes 589832 | tf_op jit(solution)/shard_map/ppermute | solution.py:108
  119.9 6.0 %collective-permute-start.11 = (f32[256,192]{0,1:T(8,128)}, f32[256,192]{0,1:T(8,128)S(1)}, u32[]{:S(2)}, u32[]{:S(2)}) collective-permute-start(f32[256,192]{0,1:T(8,128)} %get-tuple-element.30), channel_id=1, source_target_pairs={{0,32},{16,48},{32,0},{48,16},{64,96},{80,112},{96,64},{112,80},{1... | collective-permute-start | bytes 589832 | tf_op jit(solution)/shard_map/ppermute | solution.py:108
  125.9 6.0 %collective-permute-start.12 = (f32[256,192]{0,1:T(8,128)}, f32[256,192]{0,1:T(8,128)S(1)}, u32[]{:S(2)}, u32[]{:S(2)}) collective-permute-start(f32[256,192]{0,1:T(8,128)} %get-tuple-element.30), channel_id=1, source_target_pairs={{0,48},{16,0},{32,16},{48,32},{64,112},{80,64},{96,80},{112,96},{1... | collective-permute-start | bytes 589832 | tf_op jit(solution)/shard_map/ppermute | solution.py:108
  135.8 4.3 %collective-permute-done.12 = f32[256,192]{0,1:T(8,128)S(1)} collective-permute-done((f32[256,192]{0,1:T(8,128)}, f32[256,192]{0,1:T(8,128)S(1)}, u32[]{:S(2)}, u32[]{:S(2)}) %collective-permute-start.12) | collective-permute-done | bytes 196640 | tf_op jit(solution)/shard_map/ppermute | solution.py:108
  147.3 6.4 %collective-permute-done.13 = bf16[1024,256]{1,0:T(8,128)(2,1)S(1)} collective-permute-done((bf16[1024,256]{1,0:T(8,128)(2,1)S(1)}, bf16[1024,256]{1,0:T(8,128)(2,1)S(1)}, u32[]{:S(2)}, u32[]{:S(2)}) %collective-permute-start.13) | collective-permute-done | bytes 524320 | tf_op jit(solution)/shard_map/ppermute | solution.py:25
  158.1 4.3 %collective-permute-start.14 = (f32[256,130]{0,1:T(8,128)S(1)}, f32[256,130]{0,1:T(8,128)S(1)}, u32[]{:S(2)}, u32[]{:S(2)}) collective-permute-start(f32[256,130]{0,1:T(8,128)S(1)} %get-tuple-element.22), channel_id=1, source_target_pairs={{0,16},{16,32},{32,48},{48,0},{64,80},{80,96},{96,112},{112,64},{1... | collective-permute-start | bytes 399368 | tf_op jit(solution)/shard_map/ppermute | solution.py:121
  162.3 5.6 %collective-permute-start.15 = (f32[256,130]{0,1:T(8,128)S(1)}, f32[256,130]{0,1:T(8,128)S(1)}, u32[]{:S(2)}, u32[]{:S(2)}) collective-permute-start(f32[256,130]{0,1:T(8,128)S(1)} %get-tuple-element.21), channel_id=1, source_target_pairs={{0,32},{16,48},{32,0},{48,16},{64,96},{80,112},{96,64},{112,80},{1... | collective-permute-start | bytes 399368 | tf_op jit(solution)/shard_map/ppermute | solution.py:121
  168.0 5.1 %collective-permute-start.16 = (f32[256,130]{0,1:T(8,128)S(1)}, f32[256,130]{0,1:T(8,128)S(1)}, u32[]{:S(2)}, u32[]{:S(2)}) collective-permute-start(f32[256,130]{0,1:T(8,128)S(1)} %get-tuple-element.20), channel_id=1, source_target_pairs={{0,48},{16,0},{32,16},{48,32},{64,112},{80,64},{96,80},{112,96},{1... | collective-permute-start | bytes 399368 | tf_op jit(solution)/shard_map/ppermute | solution.py:121
  173.0 4.2 %collective-permute-done.15 = f32[256,130]{0,1:T(8,128)S(1)} collective-permute-done((f32[256,130]{0,1:T(8,128)S(1)}, f32[256,130]{0,1:T(8,128)S(1)}, u32[]{:S(2)}, u32[]{:S(2)}) %collective-permute-start.15) | collective-permute-done | bytes 133152 | tf_op jit(solution)/shard_map/ppermute | solution.py:121
  181.7 15.3 %all-to-all-start.1 = ((bf16[256,32,128]{2,0,1:T(8,128)(2,1)}), bf16[256,32,128]{2,0,1:T(8,128)(2,1)S(1)}, u32[]{:S(2)}, u32[]{:S(2)}) async-start(bf16[256,32,128]{2,0,1:T(8,128)(2,1)} %bitcast.157), calls=%async_computation.1 | async-start | bytes 4194304 | tf_op jit(solution)/shard_map/all_to_all | solution.py:261
  197.7 59.5 %all-to-all-done.1 = bf16[256,32,128]{2,0,1:T(8,128)(2,1)S(1)} async-done(((bf16[256,32,128]{2,0,1:T(8,128)(2,1)}), bf16[256,32,128]{2,0,1:T(8,128)(2,1)S(1)}, u32[]{:S(2)}, u32[]{:S(2)}) %all-to-all-start.1) | async-done | bytes 2097184 | tf_op jit(solution)/shard_map/all_to_all | solution.py:261
  (132 shorter events, 58.2 us)
Async XLA Ops:
  0.0 179.0 %copy-start = (bf16[128,4096]{1,0:T(8,128)(2,1)S(1)}, bf16[128,4096]{1,0:T(8,128)(2,1)}, u32[]{:S(2)}) copy-start(bf16[128,4096]{1,0:T(8,128)(2,1)} %param.18) | copy-start | bytes 3145732
  0.0 15.4 %copy-start.4 = (bf16[128,8,256]{2,1,0:T(8,128)(2,1)S(1)}, bf16[128,8,256]{2,1,0:T(8,128)(2,1)}, u32[]{:S(2)}) copy-start(bf16[128,8,256]{2,1,0:T(8,128)(2,1)} %param.13) | copy-start | bytes 1572868
  0.0 53.3 %collective-permute-start.1 = (bf16[256,128]{1,0:T(8,128)(2,1)}, bf16[256,128]{1,0:T(8,128)(2,1)S(1)}, u32[]{:S(2)}, u32[]{:S(2)}) collective-permute-start(bf16[256,128]{1,0:T(8,128)(2,1)} %param.14), channel_id=1, source_target_pairs={{0,16},{16,32},{32,48},{48,0},{64,80},{80,96},{96,112},{112,64},{1... | collective-permute-start | bytes 196616 | tf_op jit(solution)/shard_map/ppermute | solution.py:93
  6.2 51.4 %collective-permute-start = (bf16[256,128]{1,0:T(8,128)(2,1)}, bf16[256,128]{1,0:T(8,128)(2,1)}, u32[]{:S(2)}, u32[]{:S(2)}) collective-permute-start(bf16[256,128]{1,0:T(8,128)(2,1)} %param.14), channel_id=1, source_target_pairs={{0,48},{16,0},{32,16},{48,32},{64,112},{80,64},{96,80},{112,96},{1... | collective-permute-start | bytes 196616 | tf_op jit(solution)/shard_map/ppermute | solution.py:96
  14.8 12.8 %copy-start.9 = (s32[64]{0:T(128)S(1)}, s32[64]{0:T(128)}, u32[]{:S(2)}) copy-start(s32[64]{0:T(128)} %param.20) | copy-start | bytes 772
  14.8 30.1 %copy-start.6 = (bf16[4096]{0:T(1024)(128)(2,1)S(1)}, bf16[4096]{0:T(1024)(128)(2,1)}, u32[]{:S(2)}) copy-start(bf16[4096]{0:T(1024)(128)(2,1)} %param.15) | copy-start | bytes 24580
  14.8 30.8 %copy-start.12 = (s32[16]{0:T(128)S(1)}, s32[16]{0:T(128)}, u32[]{:S(2)}) copy-start(s32[16]{0:T(128)} %param.23) | copy-start | bytes 196
  14.9 36.0 %copy-start.8 = (s32[64]{0:T(128)S(1)}, s32[64]{0:T(128)}, u32[]{:S(2)}) copy-start(s32[64]{0:T(128)} %param.21) | copy-start | bytes 772
  14.9 47.4 %copy-start.5 = (bf16[256,128]{1,0:T(8,128)(2,1)S(1)}, bf16[256,128]{1,0:T(8,128)(2,1)}, u32[]{:S(2)}) copy-start(bf16[256,128]{1,0:T(8,128)(2,1)} %param.14) | copy-start | bytes 196612
  15.5 50.9 %copy-start.13 = (s32[64]{0:T(128)S(1)}, s32[64]{0:T(128)}, u32[]{:S(2)}) copy-start(s32[64]{0:T(128)} %param.19) | copy-start | bytes 772
  16.8 92.9 %all-to-all-start = ((bf16[32,128,128]{2,1,0:T(8,128)(2,1)}), bf16[32,128,128]{2,1,0:T(8,128)(2,1)}, u32[]{:S(2)}, u32[]{:S(2)}) async-start(bf16[32,128,128]{2,1,0:T(8,128)(2,1)} %pad_maximum_fusion), calls=%async_computation | async-start | bytes 2097152 | tf_op jit(solution)/shard_map/all_to_all | solution.py:178
  53.3 8.9 %collective-permute-start.2 = (bf16[256,128]{1,0:T(8,128)(2,1)S(1)}, bf16[256,128]{1,0:T(8,128)(2,1)S(1)}, u32[]{:S(2)}, u32[]{:S(2)}) collective-permute-start(bf16[256,128]{1,0:T(8,128)(2,1)S(1)} %collective-permute-done.1), channel_id=1, source_target_pairs={{0,16},{16,32},{32,48},{48,0},{64,80},{80,96},{96,112},{112,64},{1... | collective-permute-start | bytes 196616 | tf_op jit(solution)/shard_map/ppermute | solution.py:93
  63.8 8.3 %collective-permute-start.6 = (bf16[4,256,128]{2,1,0:T(8,128)(2,1)S(1)}, bf16[4,256,128]{2,1,0:T(8,128)(2,1)S(1)}, u32[]{:S(2)}, u32[]{:S(2)}) collective-permute-start(bf16[4,256,128]{2,1,0:T(8,128)(2,1)S(1)} %broadcast_select_fusion.1), channel_id=1, source_target_pairs={{0,64},{16,80},{32,96},{48,112},{64,128},{80,144},{96,160},{112,17... | collective-permute-start | bytes 786440 | tf_op jit(solution)/shard_map/ppermute | solution.py:93
  67.1 10.5 %collective-permute-start.3 = (bf16[4,256,128]{2,1,0:T(8,128)(2,1)S(1)}, bf16[4,256,128]{2,1,0:T(8,128)(2,1)S(1)}, u32[]{:S(2)}, u32[]{:S(2)}) collective-permute-start(bf16[4,256,128]{2,1,0:T(8,128)(2,1)S(1)} %broadcast_select_fusion.1), channel_id=1, source_target_pairs={{0,448},{16,464},{32,480},{48,496},{64,0},{80,16},{96,32},{112,48}... | collective-permute-start | bytes 786440 | tf_op jit(solution)/shard_map/ppermute | solution.py:96
  72.1 9.5 %collective-permute-start.7 = (bf16[4,256,128]{2,1,0:T(8,128)(2,1)S(1)}, bf16[4,256,128]{2,1,0:T(8,128)(2,1)S(1)}, u32[]{:S(2)}, u32[]{:S(2)}) collective-permute-start(bf16[4,256,128]{2,1,0:T(8,128)(2,1)S(1)} %collective-permute-done.6), channel_id=1, source_target_pairs={{0,64},{16,80},{32,96},{48,112},{64,128},{80,144},{96,160},{112,17... | collective-permute-start | bytes 786440 | tf_op jit(solution)/shard_map/ppermute | solution.py:93
  77.6 8.3 %collective-permute-start.4 = (bf16[4,256,128]{2,1,0:T(8,128)(2,1)S(1)}, bf16[4,256,128]{2,1,0:T(8,128)(2,1)S(1)}, u32[]{:S(2)}, u32[]{:S(2)}) collective-permute-start(bf16[4,256,128]{2,1,0:T(8,128)(2,1)S(1)} %collective-permute-done.3), channel_id=1, source_target_pairs={{0,448},{16,464},{32,480},{48,496},{64,0},{80,16},{96,32},{112,48}... | collective-permute-start | bytes 786440 | tf_op jit(solution)/shard_map/ppermute | solution.py:96
  81.6 9.1 %collective-permute-start.8 = (bf16[4,256,128]{2,1,0:T(8,128)(2,1)S(1)}, bf16[4,256,128]{2,1,0:T(8,128)(2,1)S(1)}, u32[]{:S(2)}, u32[]{:S(2)}) collective-permute-start(bf16[4,256,128]{2,1,0:T(8,128)(2,1)S(1)} %collective-permute-done.7), channel_id=1, source_target_pairs={{0,64},{16,80},{32,96},{48,112},{64,128},{80,144},{96,160},{112,17... | collective-permute-start | bytes 786440 | tf_op jit(solution)/shard_map/ppermute | solution.py:93
  85.9 8.9 %collective-permute-start.5 = (bf16[4,256,128]{2,1,0:T(8,128)(2,1)S(1)}, bf16[4,256,128]{2,1,0:T(8,128)(2,1)S(1)}, u32[]{:S(2)}, u32[]{:S(2)}) collective-permute-start(bf16[4,256,128]{2,1,0:T(8,128)(2,1)S(1)} %collective-permute-done.4), channel_id=1, source_target_pairs={{0,448},{16,464},{32,480},{48,496},{64,0},{80,16},{96,32},{112,48}... | collective-permute-start | bytes 786440 | tf_op jit(solution)/shard_map/ppermute | solution.py:96
  90.7 8.7 %collective-permute-start.9 = (bf16[4,256,128]{2,1,0:T(8,128)(2,1)S(1)}, bf16[4,256,128]{2,1,0:T(8,128)(2,1)S(1)}, u32[]{:S(2)}, u32[]{:S(2)}) collective-permute-start(bf16[4,256,128]{2,1,0:T(8,128)(2,1)S(1)} %collective-permute-done.8), channel_id=1, source_target_pairs={{0,64},{16,80},{32,96},{48,112},{64,128},{80,144},{96,160},{112,17... | collective-permute-start | bytes 786440 | tf_op jit(solution)/shard_map/ppermute | solution.py:93
  105.0 3.8 %copy-start.3 = (bf16[4096,128]{1,0:T(8,128)(2,1)S(1)}, bf16[4096,128]{1,0:T(8,128)(2,1)}, u32[]{:S(2)}) copy-start(bf16[4096,128]{1,0:T(8,128)(2,1)} %param.16) | copy-start | bytes 3145732
  117.0 18.7 %collective-permute-start.10 = (f32[256,192]{0,1:T(8,128)}, f32[256,192]{0,1:T(8,128)S(1)}, u32[]{:S(2)}, u32[]{:S(2)}) collective-permute-start(f32[256,192]{0,1:T(8,128)} %get-tuple-element.30), channel_id=1, source_target_pairs={{0,16},{16,32},{32,48},{48,0},{64,80},{80,96},{96,112},{112,64},{1... | collective-permute-start | bytes 589832 | tf_op jit(solution)/shard_map/ppermute | solution.py:108
  119.9 15.9 %collective-permute-start.11 = (f32[256,192]{0,1:T(8,128)}, f32[256,192]{0,1:T(8,128)S(1)}, u32[]{:S(2)}, u32[]{:S(2)}) collective-permute-start(f32[256,192]{0,1:T(8,128)} %get-tuple-element.30), channel_id=1, source_target_pairs={{0,32},{16,48},{32,0},{48,16},{64,96},{80,112},{96,64},{112,80},{1... | collective-permute-start | bytes 589832 | tf_op jit(solution)/shard_map/ppermute | solution.py:108
  125.9 14.2 %collective-permute-start.12 = (f32[256,192]{0,1:T(8,128)}, f32[256,192]{0,1:T(8,128)S(1)}, u32[]{:S(2)}, u32[]{:S(2)}) collective-permute-start(f32[256,192]{0,1:T(8,128)} %get-tuple-element.30), channel_id=1, source_target_pairs={{0,48},{16,0},{32,16},{48,32},{64,112},{80,64},{96,80},{112,96},{1... | collective-permute-start | bytes 589832 | tf_op jit(solution)/shard_map/ppermute | solution.py:108
  133.2 7.6 %copy-start.11 = (pred[4]{0:T(512)(128)(4,1)S(1)}, pred[4]{0:T(512)(128)(4,1)}, u32[]{:S(2)}) copy-start(pred[4]{0:T(512)(128)(4,1)} %compare_and_fusion.3) | copy-start | bytes 16
  135.5 5.5 %copy-start.10 = (f32[64]{0:T(128)S(1)}, f32[64]{0:T(128)}, u32[]{:S(2)}) copy-start(f32[64]{0:T(128)} %negate_power_fusion) | copy-start | bytes 772
  135.7 5.7 %copy-start.7 = (s32[256]{0:T(256)S(1)}, s32[256]{0:T(256)}, u32[]{:S(2)}) copy-start(s32[256]{0:T(256)} %get-tuple-element.31) | copy-start | bytes 3076
  140.8 4.7 %copy-start.2 = (pred[256,1024]{0,1:T(8,128)(4,1)S(1)}, pred[256,1024]{0,1:T(8,128)(4,1)}, u32[]{:S(2)}) copy-start(pred[256,1024]{0,1:T(8,128)(4,1)} %get-tuple-element.36) | copy-start | bytes 786436
  143.3 10.5 %collective-permute-start.13 = (bf16[1024,256]{1,0:T(8,128)(2,1)S(1)}, bf16[1024,256]{1,0:T(8,128)(2,1)S(1)}, u32[]{:S(2)}, u32[]{:S(2)}) collective-permute-start(bf16[1024,256]{1,0:T(8,128)(2,1)S(1)} %scatter_fusion), channel_id=1, source_target_pairs={{0,1},{1,2},{2,3},{3,4},{4,5},{5,6},{6,7},{7,8},{8,9},{9,10},{10,1... | collective-permute-start | bytes 1572872 | tf_op jit(solution)/shard_map/ppermute | solution.py:25
  158.1 15.0 %collective-permute-start.14 = (f32[256,130]{0,1:T(8,128)S(1)}, f32[256,130]{0,1:T(8,128)S(1)}, u32[]{:S(2)}, u32[]{:S(2)}) collective-permute-start(f32[256,130]{0,1:T(8,128)S(1)} %get-tuple-element.22), channel_id=1, source_target_pairs={{0,16},{16,32},{32,48},{48,0},{64,80},{80,96},{96,112},{112,64},{1... | collective-permute-start | bytes 399368 | tf_op jit(solution)/shard_map/ppermute | solution.py:121
  162.3 14.8 %collective-permute-start.15 = (f32[256,130]{0,1:T(8,128)S(1)}, f32[256,130]{0,1:T(8,128)S(1)}, u32[]{:S(2)}, u32[]{:S(2)}) collective-permute-start(f32[256,130]{0,1:T(8,128)S(1)} %get-tuple-element.21), channel_id=1, source_target_pairs={{0,32},{16,48},{32,0},{48,16},{64,96},{80,112},{96,64},{112,80},{1... | collective-permute-start | bytes 399368 | tf_op jit(solution)/shard_map/ppermute | solution.py:121
  168.0 10.9 %collective-permute-start.16 = (f32[256,130]{0,1:T(8,128)S(1)}, f32[256,130]{0,1:T(8,128)S(1)}, u32[]{:S(2)}, u32[]{:S(2)}) collective-permute-start(f32[256,130]{0,1:T(8,128)S(1)} %get-tuple-element.20), channel_id=1, source_target_pairs={{0,48},{16,0},{32,16},{48,32},{64,112},{80,64},{96,80},{112,96},{1... | collective-permute-start | bytes 399368 | tf_op jit(solution)/shard_map/ppermute | solution.py:121
  181.7 75.6 %all-to-all-start.1 = ((bf16[256,32,128]{2,0,1:T(8,128)(2,1)}), bf16[256,32,128]{2,0,1:T(8,128)(2,1)S(1)}, u32[]{:S(2)}, u32[]{:S(2)}) async-start(bf16[256,32,128]{2,0,1:T(8,128)(2,1)} %bitcast.157), calls=%async_computation.1 | async-start | bytes 4194304 | tf_op jit(solution)/shard_map/all_to_all | solution.py:261
  (1 other events, 1.3 us)

commit v6 on v4

--- a/solution.py
+++ b/solution.py
@@ -74,27 +74,19 @@
     return summed / totals[..., None]
 
 
+def member_groups(devices, size):
+    return [list(range(start, start + size)) for start in range(0, devices, size)]
+
+
 def group_gather(piece, axis, size):
-    devices = lax.axis_size(axis)
-    place = lax.axis_index(axis) % size
-    pieces = [piece]
-    for step in range(1, size):
-        pairs = [(i, i - i % size + (i % size + step) % size) for i in range(devices)]
-        pieces.append(lax.ppermute(piece, axis, pairs))
-    stacked = jnp.stack(pieces)
-    order = (place - jnp.arange(size, dtype=jnp.int32)) % size
-    return jnp.take(stacked, order, axis=0)
+    spread = jnp.broadcast_to(piece[None], (size,) + piece.shape)
+    groups = member_groups(lax.axis_size(axis), size)
+    return lax.all_to_all(spread, axis, 0, 0, axis_index_groups=groups, tiled=True)
 
 
 def group_exchange(parts, axis, size):
-    devices = lax.axis_size(axis)
-    place = lax.axis_index(axis) % size
-    mine = [lax.dynamic_index_in_dim(parts, place, 0, keepdims=False)]
-    for step in range(1, size):
-        pairs = [(i, i - i % size + (i % size + step) % size) for i in range(devices)]
-        outgoing = lax.dynamic_index_in_dim(parts, (place + step) % size, 0, keepdims=False)
-        mine.append(lax.ppermute(outgoing, axis, pairs))
-    return jnp.stack(mine)
+    groups = member_groups(lax.axis_size(axis), size)
+    return lax.all_to_all(parts, axis, 0, 0, axis_index_groups=groups, tiled=True)
 
 
 def joined_rows(span_order, shard, spans_here, stored_rows):

time: 253 us -> 257 us (1.016)
  the two profiles are of different devices: /device:TPU:14 before, /device:TPU:49 now
where the time goes in v6:
time: 257 us; the launch traced here: 256 us
  waiting for transfers between devices  129 us (50%)
  starting transfers between devices  45.2 us (18%)
  other arithmetic  34.7 us (14%)
  blocking collectives  18.7 us (7%)
  local copies, waits for them, and re-layouts  16 us (6%)
  matrix products  11.7 us (5%)
    all_to_all x1, waiting for transfers between devices, local(): arrived_terms = lax.all_to_all(term_blocks, 'blk', 1, 1, tiled=True)  62.9 us
    all_to_all x1, waiting for transfers between devices, local(): lax.all_to_all(jnp.concatenate([x_part, w_part], axis=1), 'blk', 0, 0, ti...  48.5 us
    all_to_all x1, blocking collectives, group_exchange(): lax.all_to_all(parts, axis, 0, 0, axis_index_groups=groups, tiled=True)  18.7 us
    all_to_all x1, starting transfers between devices, local(): lax.all_to_all(jnp.concatenate([x_part, w_part], axis=1), 'blk', 0, 0, ti...  15.3 us
    all_to_all x1, starting transfers between devices, local(): lax.all_to_all(c_part, 'blk', 0, 0, tiled=True)  11.2 us
    all_to_all x1, waiting for transfers between devices, group_gather(): lax.all_to_all(spread, axis, 0, 0, axis_index_groups=groups, tiled=True)  10.5 us
    select_n x3, other arithmetic, tenant_lookup(): span_ids = positions // SPAN  8.92 us
    ppermute x1, starting transfers between devices, shifted(): return lax.ppermute(shard, axis, pairs)  7.16 us
  transfers between devices with their start and end apart: 5, of which 5 were waited for; matrix products, arithmetic and copies ran while one was open for 17% of the time, Pallas kernels for 0%

profile of v6, /device:TPU:49, one launch (start us, length us, event | category | flops | bytes accessed | tf_op | source)
XLA Modules:
  0.0 255.8 jit_solution(14610843323203445593)
XLA Ops:
  0.0 1.4 copy.89
  2.9 1.7 pad_maximum_fusion
  4.7 15.3 %all-to-all-start = ((bf16[32,320,128]{2,1,0:T(8,128)(2,1)}), bf16[32,320,128]{2,1,0:T(8,128)(2,1)}, u32[]{:S(2)}, u32[]{:S(2)}) async-start(bf16[32,320,128]{2,1,0:T(8,128)(2,1)} %pad_maximum_fusion), calls=%async_computation | async-start | bytes 5242880 | tf_op jit(solution)/shard_map/all_to_all | solution.py:142
  22.7 2.4 broadcast_compare_fusion.2
  25.8 2.5 broadcast_compare_fusion.3
  28.9 3.9 %and_select_fusion.8 = (s32[256]{0:T(256)S(1)}, s32[256]{0:T(256)S(1)}, s32[256]{0:T(256)S(1)}) fusion(s32[4096]{0:T(1024)} %param.22, s32[]{:T(128)S(6)} %select_n.143, s32[]{:T(128)S(6)} %mul.234, s32[]{:T(128)S(6)} %select_n.149, s32[]{:T(128)S(6)} %mul.236, s32[]{:T(128)} %bitcast.16, s32[]{:T(128)} %bitcast.15, s32[]{:T(128)} %bitcast.14, s32[]{:T(128)} %bitcast.13, ...), kind=kLoop, calls=%fused_computation.163 | loop fusion | flops 26112 | bytes 4132 | tf_op jit(solution)/shard_map/jit(floor_divide)/jit(_where)/select_n | solution.py:42
  32.9 2.5 fusion.76
  35.4 2.5 add_select_fusion
  38.0 2.4 add_select_fusion.1
  40.4 2.4 fusion.78
  43.5 2.4 select_convert_fusion.1
  45.9 48.5 %all-to-all-done = bf16[32,320,128]{2,1,0:T(8,128)(2,1)} async-done(((bf16[32,320,128]{2,1,0:T(8,128)(2,1)}), bf16[32,320,128]{2,1,0:T(8,128)(2,1)}, u32[]{:S(2)}, u32[]{:S(2)}) %all-to-all-start) | async-done | bytes 2621472 | tf_op jit(solution)/shard_map/all_to_all | solution.py:142
  94.4 11.2 %all-to-all-start.1 = ((bf16[32,64,128]{2,1,0:T(8,128)(2,1)}), bf16[32,64,128]{2,1,0:T(8,128)(2,1)S(1)}, u32[]{:S(2)}, u32[]{:S(2)}) async-start(bf16[32,64,128]{2,1,0:T(8,128)(2,1)} %reshape.323), calls=%async_computation.1 | async-start | bytes 1048576 | tf_op jit(solution)/shard_map/all_to_all | solution.py:146
  105.7 2.1 fusion.1
  109.3 2.3 fusion.37
  111.6 2.7 %fusion.31 = f32[256,128]{0,1:T(8,128)S(1)} fusion(bf16[32,128,128]{2,1,0:T(8,128)(2,1)} %bitcast.116, f32[32,128]{1,0:T(8,128)S(1)} %bitcast_convert_fusion, bf16[32,320,128]{2,1,0:T(8,128)(2,1)} %all-to-all-done, f32[256]{0:T(256)S(1)} %add_rsqrt_fusion), kind=kOutput, calls=%fused_computation.34 | convolution fusion | flops 271613952 | bytes 3294208 | tf_op jit(solution)/shard_map/ksc,kcd->sd/dot_general | solution.py:154
  114.3 5.4 %all-to-all-done.1 = bf16[32,64,128]{2,1,0:T(8,128)(2,1)S(1)} async-done(((bf16[32,64,128]{2,1,0:T(8,128)(2,1)}), bf16[32,64,128]{2,1,0:T(8,128)(2,1)S(1)}, u32[]{:S(2)}, u32[]{:S(2)}) %all-to-all-start.1) | async-done | bytes 524320 | tf_op jit(solution)/shard_map/all_to_all | solution.py:146
  120.6 5.7 %all-to-all-start.2 = ((f32[4,256,192]{1,2,0:T(8,128)}), f32[4,256,192]{1,2,0:T(8,128)S(1)}, u32[]{:S(2)}, u32[]{:S(2)}) async-start(f32[4,256,192]{1,2,0:T(8,128)} %broadcast_in_dim.178), calls=%async_computation.2 | async-start | bytes 1572864 | tf_op jit(solution)/shard_map/all_to_all | solution.py:84
  126.6 1.3 fusion.42
  129.0 1.2 fusion.52
  130.5 1.2 pad_maximum_fusion.2
  131.7 10.5 %all-to-all-done.2 = f32[4,256,192]{1,2,0:T(8,128)S(1)} async-done(((f32[4,256,192]{1,2,0:T(8,128)}), f32[4,256,192]{1,2,0:T(8,128)S(1)}, u32[]{:S(2)}, u32[]{:S(2)}) %all-to-all-start.2) | async-done | bytes 786464 | tf_op jit(solution)/shard_map/all_to_all | solution.py:84
  142.7 1.8 scatter_fusion
  144.4 7.2 %collective-permute-start = (bf16[1024,256]{1,0:T(8,128)(2,1)S(1)}, bf16[1024,256]{1,0:T(8,128)(2,1)}, u32[]{:S(2)}, u32[]{:S(2)}) collective-permute-start(bf16[1024,256]{1,0:T(8,128)(2,1)S(1)} %scatter_fusion), channel_id=1, source_target_pairs={{0,1},{1,2},{2,3},{3,4},{4,5},{5,6},{6,7},{7,8},{8,9},{9,10},{10,1... | collective-permute-start | bytes 1572872 | tf_op jit(solution)/shard_map/ppermute | solution.py:24
  155.8 1.7 collective-permute-done
  157.5 1.8 fusion.3
  159.4 1.2 fusion.19
  161.7 2.0 fusion.25
  163.8 18.7 %all_to_all.25 = f32[4,256,130]{1,2,0:T(8,128)S(1)} all-to-all(f32[4,256,130]{1,2,0:T(8,128)S(1)} %pad_maximum_fusion.1), channel_id=1, replica_groups={{0,16,32,48},{64,80,96,112},{128,144,160,176},{192,208,224,240},{256,27..., dimensions={0} | all-to-all | bytes 1064960 | tf_op jit(solution)/shard_map/all_to_all | solution.py:89
  183.3 1.9 copy.131
  185.3 5.9 %all-to-all-start.4 = ((bf16[256,32,128]{2,0,1:T(8,128)(2,1)}), bf16[256,32,128]{2,0,1:T(8,128)(2,1)S(1)}, u32[]{:S(2)}, u32[]{:S(2)}) async-start(bf16[256,32,128]{2,0,1:T(8,128)(2,1)} %bitcast.108), calls=%async_computation.4 | async-start | bytes 4194304 | tf_op jit(solution)/shard_map/all_to_all | solution.py:229
  191.9 62.9 %all-to-all-done.4 = bf16[256,32,128]{2,0,1:T(8,128)(2,1)S(1)} async-done(((bf16[256,32,128]{2,0,1:T(8,128)(2,1)}), bf16[256,32,128]{2,0,1:T(8,128)(2,1)S(1)}, u32[]{:S(2)}, u32[]{:S(2)}) %all-to-all-start.4) | async-done | bytes 2097184 | tf_op jit(solution)/shard_map/all_to_all | solution.py:229
  (69 shorter events, 18.5 us)
Async XLA Ops:
  0.0 182.6 %copy-start = (bf16[128,4096]{1,0:T(8,128)(2,1)S(1)}, bf16[128,4096]{1,0:T(8,128)(2,1)}, u32[]{:S(2)}) copy-start(bf16[128,4096]{1,0:T(8,128)(2,1)} %param.18) | copy-start | bytes 3145732
  0.0 2.4 copy-start.2
  2.9 17.1 %copy-start.1 = (bf16[128,8,256]{2,1,0:T(8,128)(2,1)S(1)}, bf16[128,8,256]{2,1,0:T(8,128)(2,1)}, u32[]{:S(2)}) copy-start(bf16[128,8,256]{2,1,0:T(8,128)(2,1)} %param.13) | copy-start | bytes 1572868
  4.6 16.4 %copy-start.6 = (s32[16]{0:T(128)S(1)}, s32[16]{0:T(128)}, u32[]{:S(2)}) copy-start(s32[16]{0:T(128)} %param.23) | copy-start | bytes 196
  4.6 17.1 %copy-start.7 = (s32[64]{0:T(128)S(1)}, s32[64]{0:T(128)}, u32[]{:S(2)}) copy-start(s32[64]{0:T(128)} %param.19) | copy-start | bytes 772
  4.6 17.2 %copy-start.5 = (s32[64]{0:T(128)S(1)}, s32[64]{0:T(128)}, u32[]{:S(2)}) copy-start(s32[64]{0:T(128)} %param.20) | copy-start | bytes 772
  4.6 41.2 %copy-start.3 = (bf16[4096]{0:T(1024)(128)(2,1)S(1)}, bf16[4096]{0:T(1024)(128)(2,1)}, u32[]{:S(2)}) copy-start(bf16[4096]{0:T(1024)(128)(2,1)} %param.15) | copy-start | bytes 24580
  4.7 89.8 %all-to-all-start = ((bf16[32,320,128]{2,1,0:T(8,128)(2,1)}), bf16[32,320,128]{2,1,0:T(8,128)(2,1)}, u32[]{:S(2)}, u32[]{:S(2)}) async-start(bf16[32,320,128]{2,1,0:T(8,128)(2,1)} %pad_maximum_fusion), calls=%async_computation | async-start | bytes 5242880 | tf_op jit(solution)/shard_map/all_to_all | solution.py:142
  94.4 25.3 %all-to-all-start.1 = ((bf16[32,64,128]{2,1,0:T(8,128)(2,1)}), bf16[32,64,128]{2,1,0:T(8,128)(2,1)S(1)}, u32[]{:S(2)}, u32[]{:S(2)}) async-start(bf16[32,64,128]{2,1,0:T(8,128)(2,1)} %reshape.323), calls=%async_computation.1 | async-start | bytes 1048576 | tf_op jit(solution)/shard_map/all_to_all | solution.py:146
  111.6 14.7 %copy-start.4 = (s32[64]{0:T(128)S(1)}, s32[64]{0:T(128)}, u32[]{:S(2)}) copy-start(s32[64]{0:T(128)} %param.21) | copy-start | bytes 772
  120.6 21.5 %all-to-all-start.2 = ((f32[4,256,192]{1,2,0:T(8,128)}), f32[4,256,192]{1,2,0:T(8,128)S(1)}, u32[]{:S(2)}, u32[]{:S(2)}) async-start(f32[4,256,192]{1,2,0:T(8,128)} %broadcast_in_dim.178), calls=%async_computation.2 | async-start | bytes 1572864 | tf_op jit(solution)/shard_map/all_to_all | solution.py:84
  144.4 13.1 %collective-permute-start = (bf16[1024,256]{1,0:T(8,128)(2,1)S(1)}, bf16[1024,256]{1,0:T(8,128)(2,1)}, u32[]{:S(2)}, u32[]{:S(2)}) collective-permute-start(bf16[1024,256]{1,0:T(8,128)(2,1)S(1)} %scatter_fusion), channel_id=1, source_target_pairs={{0,1},{1,2},{2,3},{3,4},{4,5},{5,6},{6,7},{7,8},{8,9},{9,10},{10,1... | collective-permute-start | bytes 1572872 | tf_op jit(solution)/shard_map/ppermute | solution.py:24
  185.3 69.5 %all-to-all-start.4 = ((bf16[256,32,128]{2,0,1:T(8,128)(2,1)}), bf16[256,32,128]{2,0,1:T(8,128)(2,1)S(1)}, u32[]{:S(2)}, u32[]{:S(2)}) async-start(bf16[256,32,128]{2,0,1:T(8,128)(2,1)} %bitcast.108), calls=%async_computation.4 | async-start | bytes 4194304 | tf_op jit(solution)/shard_map/all_to_all | solution.py:229

commit v7 on v6

--- a/solution.py
+++ b/solution.py
@@ -139,13 +139,13 @@
         .transpose(2, 0, 1, 3)
         .reshape(blk_count, rows_each * 2, HEAD_DIM)
     )
-    arrived = lax.all_to_all(jnp.concatenate([x_part, w_part], axis=1), "blk", 0, 0, tiled=True)
-    wide = arrived[:, :slots].astype(jnp.float32)
-    kv_cols = arrived[:, slots:].reshape(blk_count, own_cols, pair_cols)
-    arrived, c_part = lax.optimization_barrier((arrived, c_part))
-    stored = lax.all_to_all(c_part, "blk", 0, 0, tiled=True).reshape(
-        blk_count * rows_each, 2 * HEAD_DIM
-    )
+    arrived = lax.all_to_all(x_part, "blk", 0, 0, tiled=True)
+    wide = arrived.astype(jnp.float32)
+    arrived, w_part, c_part = lax.optimization_barrier((arrived, w_part, c_part))
+    w_rows = w_part.shape[1]
+    moved = lax.all_to_all(jnp.concatenate([w_part, c_part], axis=1), "blk", 0, 0, tiled=True)
+    kv_cols = moved[:, :w_rows].reshape(blk_count, own_cols, pair_cols)
+    stored = moved[:, w_rows:].reshape(blk_count * rows_each, 2 * HEAD_DIM)
 
     gains = norm_gain.astype(jnp.float32).reshape(blk_count, 1, own_cols)
     scaled = (wide * gains).astype(jnp.bfloat16)
@@ -224,10 +224,14 @@
     total = jnp.sum(gathered[:, :, HEAD_DIM + 1] * weight, axis=0)
     heads_sum = jnp.sum(gathered[:, :, :HEAD_DIM] * weight[..., None], axis=0)
     heads_out = (heads_sum / total[:, None]).astype(jnp.bfloat16)
-    term = jnp.dot(heads_out, w_out, preferred_element_type=jnp.float32)
-    term_blocks = term.astype(jnp.bfloat16).reshape(slots, blk_count, own_cols)
-    arrived_terms = lax.all_to_all(term_blocks, "blk", 1, 1, tiled=True)
-    summed_out = jnp.sum(arrived_terms.astype(jnp.float32), axis=1)
+    term = jnp.einsum(
+        "ch,hkd->kcd",
+        heads_out,
+        w_out.reshape(HEAD_DIM, blk_count, own_cols),
+        preferred_element_type=jnp.float32,
+    )
+    arrived_terms = lax.all_to_all(term.astype(jnp.bfloat16), "blk", 0, 0, tiled=True)
+    summed_out = jnp.sum(arrived_terms.astype(jnp.float32), axis=0)
     return jnp.where(live[:, None], summed_out, 0.0).astype(jnp.bfloat16)
 
 

time: 257 us -> 255 us (level)
  the two profiles are of different devices: /device:TPU:49 before, /device:TPU:48 now
where the time goes in v7:
time: 255 us; the launch traced here: 254 us
  waiting for transfers between devices  116 us (45%)
  starting transfers between devices  46.1 us (18%)
  other arithmetic  34.2 us (13%)
  local copies, waits for them, and re-layouts  27.9 us (11%)
  blocking collectives  17.9 us (7%)
  matrix products  12 us (5%)
    all_to_all x1, waiting for transfers between devices, local(): lax.all_to_all(term.astype(jnp.bfloat16), 'blk', 0, 0, tiled=True)  56.1 us
    all_to_all x1, waiting for transfers between devices, local(): arrived = lax.all_to_all(x_part, 'blk', 0, 0, tiled=True)  45.3 us
    all_to_all x1, blocking collectives, group_exchange(): lax.all_to_all(parts, axis, 0, 0, axis_index_groups=groups, tiled=True)  17.9 us
    all_to_all x1, starting transfers between devices, local(): arrived = lax.all_to_all(x_part, 'blk', 0, 0, tiled=True)  15.6 us
    all_to_all x1, waiting for transfers between devices, group_gather(): lax.all_to_all(spread, axis, 0, 0, axis_index_groups=groups, tiled=True)  13.4 us
    all_to_all x1, starting transfers between devices, local(): lax.all_to_all(term.astype(jnp.bfloat16), 'blk', 0, 0, tiled=True)  12.1 us
    all_to_all x1, starting transfers between devices, local(): lax.all_to_all(jnp.concatenate([w_part, c_part], axis=1), 'blk', 0, 0, ti...  10.5 us
    select_n x3, other arithmetic, tenant_lookup(): span_ids = positions // SPAN  8.98 us
  transfers between devices with their start and end apart: 5, of which 4 were waited for; matrix products, arithmetic and copies ran while one was open for 20% of the time, Pallas kernels for 0%

profile of v7, /device:TPU:48, one launch (start us, length us, event | category | flops | bytes accessed | tf_op | source)
XLA Modules:
  0.0 254.2 jit_solution(7728951289185108965)
XLA Ops:
  0.0 2.8 %broadcast_in_dim.174 = bf16[32,256,128]{2,1,0:T(8,128)(2,1)} broadcast(bf16[256,128]{1,0:T(8,128)(2,1)} %param.14), dimensions={1,2} | broadcast | bytes 2162688 | tf_op jit(solution)/shard_map/broadcast_in_dim | solution.py:131
  2.8 15.6 %all-to-all-start = ((bf16[32,256,128]{2,1,0:T(8,128)(2,1)}), bf16[32,256,128]{2,1,0:T(8,128)(2,1)S(1)}, u32[]{:S(2)}, u32[]{:S(2)}) async-start(bf16[32,256,128]{2,1,0:T(8,128)(2,1)} %broadcast_in_dim.174), calls=%async_computation | async-start | bytes 4194304 | tf_op jit(solution)/shard_map/all_to_all | solution.py:142
  18.4 2.0 copy.95
  20.5 2.4 copy.96
  22.9 2.5 reshape.321
  25.3 2.0 copy.143
  27.3 2.0 reshape.323
  30.9 45.3 %all-to-all-done = bf16[32,256,128]{2,1,0:T(8,128)(2,1)S(1)} async-done(((bf16[32,256,128]{2,1,0:T(8,128)(2,1)}), bf16[32,256,128]{2,1,0:T(8,128)(2,1)S(1)}, u32[]{:S(2)}, u32[]{:S(2)}) %all-to-all-start) | async-done | bytes 2097184 | tf_op jit(solution)/shard_map/all_to_all | solution.py:142
  76.1 2.3 pad_maximum_fusion
  78.5 10.5 %all-to-all-start.1 = ((bf16[32,128,128]{2,1,0:T(8,128)(2,1)}), bf16[32,128,128]{2,1,0:T(8,128)(2,1)}, u32[]{:S(2)}, u32[]{:S(2)}) async-start(bf16[32,128,128]{2,1,0:T(8,128)(2,1)} %pad_maximum_fusion), calls=%async_computation.1 | async-start | bytes 2097152 | tf_op jit(solution)/shard_map/all_to_all | solution.py:146
  89.0 2.5 broadcast_compare_fusion.2
  92.2 2.7 %broadcast_compare_fusion.3 = pred[1024]{0:T(1024)(128)(4,1)S(1)} fusion(s32[]{:T(128)} %bitcast.31, s32[]{:T(128)} %bitcast.30, s32[]{:T(128)} %bitcast.29, s32[]{:T(128)} %bitcast.28, s32[]{:T(128)S(6)} %mul.239, s32[]{:T(128)S(6)} %mul.274, pred[]{:T(512)S(6)} %gt.3), kind=kLoop, calls=%fused_computation.148 | loop fusion | flops 53248 | bytes 1049 | tf_op jit(solution)/shard_map/ge | solution.py:56
  95.5 3.8 %and_select_fusion.8 = (s32[256]{0:T(256)S(1)}, s32[256]{0:T(256)S(1)}, s32[256]{0:T(256)S(1)}) fusion(s32[4096]{0:T(1024)} %param.22, s32[]{:T(128)S(6)} %select_n.143, s32[]{:T(128)S(6)} %mul.234, s32[]{:T(128)S(6)} %select_n.149, s32[]{:T(128)S(6)} %mul.236, s32[]{:T(128)} %bitcast.16, s32[]{:T(128)} %bitcast.15, s32[]{:T(128)} %bitcast.14, s32[]{:T(128)} %bitcast.13, ...), kind=kLoop, calls=%fused_computation.163 | loop fusion | flops 26112 | bytes 4132 | tf_op jit(solution)/shard_map/jit(floor_divide)/jit(_where)/select_n | solution.py:42
  99.3 2.7 %fusion.77 = s32[1024]{0:T(1024)S(1)} fusion(s32[]{:T(128)} %bitcast.31, s32[]{:T(128)} %bitcast.30, s32[]{:T(128)} %bitcast.29, s32[]{:T(128)} %bitcast.28, s32[]{:T(128)S(6)} %mul.274, s32[]{:T(128)S(6)} %mul.239, pred[]{:T(512)S(6)} %gt.3), kind=kLoop, calls=%fused_computation.125 | loop fusion | flops 52224 | bytes 4121 | tf_op jit(solution)/shard_map/jit(_where)/select_n | solution.py:204
  102.0 2.7 %add_select_fusion = s32[1024]{0:T(1024)S(1)} fusion(s32[]{:T(128)} %bitcast.31, s32[]{:T(128)} %bitcast.30, s32[]{:T(128)} %bitcast.29, s32[]{:T(128)} %bitcast.28, s32[]{:T(128)S(6)} %mul.239, s32[]{:T(128)S(6)} %mul.274, pred[]{:T(512)S(6)} %gt.3), kind=kLoop, calls=%fused_computation.92 | loop fusion | flops 67584 | bytes 4121 | tf_op jit(solution)/shard_map/jit(floor_divide)/jit(_where)/select_n | solution.py:42
  104.7 2.5 add_select_fusion.1
  107.2 2.5 fusion.79
  110.3 2.4 select_convert_fusion.1
  113.2 2.0 fusion.30
  116.2 2.3 fusion.96
  118.5 2.4 reshape.326
  120.9 1.9 fusion.36
  123.8 5.7 %all-to-all-start.2 = ((f32[4,256,192]{1,2,0:T(8,128)}), f32[4,256,192]{1,2,0:T(8,128)S(1)}, u32[]{:S(2)}, u32[]{:S(2)}) async-start(f32[4,256,192]{1,2,0:T(8,128)} %broadcast_in_dim.178), calls=%async_computation.2 | async-start | bytes 1572864 | tf_op jit(solution)/shard_map/all_to_all | solution.py:84
  136.0 13.4 %all-to-all-done.2 = f32[4,256,192]{1,2,0:T(8,128)S(1)} async-done(((f32[4,256,192]{1,2,0:T(8,128)}), f32[4,256,192]{1,2,0:T(8,128)S(1)}, u32[]{:S(2)}, u32[]{:S(2)}) %all-to-all-start.2) | async-done | bytes 786464 | tf_op jit(solution)/shard_map/all_to_all | solution.py:84
  149.9 1.8 scatter_fusion
  151.7 2.1 collective-permute-start
  158.0 1.8 fusion.3
  162.1 2.0 fusion.24
  164.2 17.9 %all_to_all.25 = f32[4,256,130]{1,2,0:T(8,128)S(1)} all-to-all(f32[4,256,130]{1,2,0:T(8,128)S(1)} %pad_maximum_fusion.1), channel_id=1, replica_groups={{0,16,32,48},{64,80,96,112},{128,144,160,176},{192,208,224,240},{256,27..., dimensions={0} | all-to-all | bytes 1064960 | tf_op jit(solution)/shard_map/all_to_all | solution.py:89
  182.2 2.1 convert_bitcast_fusion
  184.3 12.1 %all-to-all-start.4 = ((bf16[32,256,128]{2,1,0:T(8,128)(2,1)}), bf16[32,256,128]{2,1,0:T(8,128)(2,1)S(1)}, u32[]{:S(2)}, u32[]{:S(2)}) async-start(bf16[32,256,128]{2,1,0:T(8,128)(2,1)} %convert_bitcast_fusion), calls=%async_computation.4 | async-start | bytes 4194304 | tf_op jit(solution)/shard_map/all_to_all | solution.py:233
  197.0 56.1 %all-to-all-done.4 = bf16[32,256,128]{2,1,0:T(8,128)(2,1)S(1)} async-done(((bf16[32,256,128]{2,1,0:T(8,128)(2,1)}), bf16[32,256,128]{2,1,0:T(8,128)(2,1)S(1)}, u32[]{:S(2)}, u32[]{:S(2)}) %all-to-all-start.4) | async-done | bytes 2097184 | tf_op jit(solution)/shard_map/all_to_all | solution.py:233
  (64 shorter events, 21.0 us)
Async XLA Ops:
  0.0 182.2 %copy-start = (bf16[128,4096]{1,0:T(8,128)(2,1)S(1)}, bf16[128,4096]{1,0:T(8,128)(2,1)}, u32[]{:S(2)}) copy-start(bf16[128,4096]{1,0:T(8,128)(2,1)} %param.18) | copy-start | bytes 3145732
  2.8 73.4 %all-to-all-start = ((bf16[32,256,128]{2,1,0:T(8,128)(2,1)}), bf16[32,256,128]{2,1,0:T(8,128)(2,1)S(1)}, u32[]{:S(2)}, u32[]{:S(2)}) async-start(bf16[32,256,128]{2,1,0:T(8,128)(2,1)} %broadcast_in_dim.174), calls=%async_computation | async-start | bytes 4194304 | tf_op jit(solution)/shard_map/all_to_all | solution.py:142
  18.4 10.9 %copy-start.3 = (s32[64]{0:T(128)S(1)}, s32[64]{0:T(128)}, u32[]{:S(2)}) copy-start(s32[64]{0:T(128)} %param.20) | copy-start | bytes 772
  22.8 68.6 %copy-start.4 = (s32[64]{0:T(128)S(1)}, s32[64]{0:T(128)}, u32[]{:S(2)}) copy-start(s32[64]{0:T(128)} %param.19) | copy-start | bytes 772
  22.8 68.7 %copy-start.5 = (s32[16]{0:T(128)S(1)}, s32[16]{0:T(128)}, u32[]{:S(2)}) copy-start(s32[16]{0:T(128)} %param.23) | copy-start | bytes 196
  22.9 89.9 %copy-start.1 = (bf16[4096]{0:T(1024)(128)(2,1)S(1)}, bf16[4096]{0:T(1024)(128)(2,1)}, u32[]{:S(2)}) copy-start(bf16[4096]{0:T(1024)(128)(2,1)} %param.15) | copy-start | bytes 24580
  78.5 37.8 %all-to-all-start.1 = ((bf16[32,128,128]{2,1,0:T(8,128)(2,1)}), bf16[32,128,128]{2,1,0:T(8,128)(2,1)}, u32[]{:S(2)}, u32[]{:S(2)}) async-start(bf16[32,128,128]{2,1,0:T(8,128)(2,1)} %pad_maximum_fusion), calls=%async_computation.1 | async-start | bytes 2097152 | tf_op jit(solution)/shard_map/all_to_all | solution.py:146
  118.5 11.0 %copy-start.2 = (s32[64]{0:T(128)S(1)}, s32[64]{0:T(128)}, u32[]{:S(2)}) copy-start(s32[64]{0:T(128)} %param.21) | copy-start | bytes 772
  123.8 25.6 %all-to-all-start.2 = ((f32[4,256,192]{1,2,0:T(8,128)}), f32[4,256,192]{1,2,0:T(8,128)S(1)}, u32[]{:S(2)}, u32[]{:S(2)}) async-start(f32[4,256,192]{1,2,0:T(8,128)} %broadcast_in_dim.178), calls=%async_computation.2 | async-start | bytes 1572864 | tf_op jit(solution)/shard_map/all_to_all | solution.py:84
  151.7 6.3 %collective-permute-start = (bf16[1024,256]{1,0:T(8,128)(2,1)S(1)}, bf16[1024,256]{1,0:T(8,128)(2,1)}, u32[]{:S(2)}, u32[]{:S(2)}) collective-permute-start(bf16[1024,256]{1,0:T(8,128)(2,1)S(1)} %scatter_fusion), channel_id=1, source_target_pairs={{0,1},{1,2},{2,3},{3,4},{4,5},{5,6},{6,7},{7,8},{8,9},{9,10},{10,1... | collective-permute-start | bytes 1572872 | tf_op jit(solution)/shard_map/ppermute | solution.py:24
  184.3 68.9 %all-to-all-start.4 = ((bf16[32,256,128]{2,1,0:T(8,128)(2,1)}), bf16[32,256,128]{2,1,0:T(8,128)(2,1)S(1)}, u32[]{:S(2)}, u32[]{:S(2)}) async-start(bf16[32,256,128]{2,1,0:T(8,128)(2,1)} %convert_bitcast_fusion), calls=%async_computation.4 | async-start | bytes 4194304 | tf_op jit(solution)/shard_map/all_to_all | solution.py:233

commit v8 on v7

--- a/solution.py
+++ b/solution.py
@@ -72,6 +72,12 @@
     totals = first[1] * scale_one + second[1] * scale_two
     summed = first[2] * scale_one[..., None] + second[2] * scale_two[..., None]
     return summed / totals[..., None]
+
+
+def split_wide(values):
+    high = values.astype(jnp.bfloat16)
+    low = (values - high.astype(jnp.float32)).astype(jnp.bfloat16)
+    return high, low
 
 
 def member_groups(devices, size):
@@ -129,8 +135,18 @@
 
     rows_each = block_rows // group_size
     x_part = jnp.broadcast_to(recompute_input[None], (blk_count, slots, own_cols))
+    quarter = pair_cols // 2
+    key_members = HEAD_DIM // pair_cols
+    groups_w = w_keyval.reshape(own_cols, KVH, 2 * HEAD_DIM)
+    sorted_w = []
+    for m in range(key_members):
+        sorted_w.append(groups_w[:, :, m * quarter : (m + 1) * quarter])
+        second = HEAD_DIM // 2 + m * quarter
+        sorted_w.append(groups_w[:, :, second : second + quarter])
+    sorted_w.append(groups_w[:, :, HEAD_DIM:])
     w_part = (
-        w_keyval.reshape(own_cols, blk_count, pair_cols)
+        jnp.concatenate(sorted_w, axis=2)
+        .reshape(own_cols, blk_count, pair_cols)
         .transpose(1, 0, 2)
         .reshape(blk_count, own_cols * pair_cols // HEAD_DIM, HEAD_DIM)
     )
@@ -160,18 +176,32 @@
     pair_piece = jnp.einsum(
         "ksc,kcd->sd", scaled, kv_cols, preferred_element_type=jnp.float32
     ) * inv_rms[:, None]
-    shared = group_gather(jnp.concatenate([query_acc, pair_piece], axis=1), "blk", group_size)
-    group_pair = shared[:, :, HEAD_DIM:].transpose(1, 0, 2).reshape(slots, group_size * pair_cols)
-
     own_pos = lax.dynamic_slice_in_dim(recompute_pos, kv_index * slots, slots, 0)
     own_count = lax.dynamic_index_in_dim(recompute_count, kv_index, 0, keepdims=False)
     live = jnp.arange(slots, dtype=jnp.int32) < own_count
     query_pos = kv_index * shard_len + own_pos
-    fresh_keys = rotate_half(group_pair[:, :HEAD_DIM], query_pos).astype(jnp.bfloat16)
-    fresh_values = group_pair[:, HEAD_DIM:].astype(jnp.bfloat16)
-    queries = rotate_half(shared[:, :, :HEAD_DIM].transpose(1, 0, 2), query_pos).astype(
-        jnp.bfloat16
-    )
+    own_query = rotate_half(query_acc.reshape(slots, 1, HEAD_DIM), query_pos)
+    own_query = own_query.astype(jnp.bfloat16).reshape(slots, HEAD_DIM)
+    inverse = ROPE_BASE ** (
+        -(jnp.arange(HEAD_DIM // 2, dtype=jnp.float32) * 2.0 / HEAD_DIM)
+    )
+    freq = lax.dynamic_slice_in_dim(inverse, (member % key_members) * quarter, quarter, 0)
+    angles = query_pos.astype(jnp.float32)[:, None] * freq[None, :]
+    cosine = jnp.cos(angles)
+    sine = jnp.sin(angles)
+    first = pair_piece[:, :quarter]
+    second = pair_piece[:, quarter:]
+    turned = jnp.concatenate([first * cosine - second * sine, second * cosine + first * sine], axis=1)
+    own_piece = jnp.where(member < key_members, turned, pair_piece).astype(jnp.bfloat16)
+    shared = group_gather(jnp.concatenate([own_query, own_piece], axis=1), "blk", group_size)
+    queries = shared[:, :, :HEAD_DIM].transpose(1, 0, 2)
+    pieces = shared[:, :, HEAD_DIM:]
+    fresh_keys = jnp.concatenate(
+        [pieces[m, :, :quarter] for m in range(key_members)]
+        + [pieces[m, :, quarter:] for m in range(key_members)],
+        axis=1,
+    )
+    fresh_values = jnp.concatenate([pieces[m] for m in range(key_members, group_size)], axis=1)
 
     local_rows = jnp.arange(blk_count * rows_each, dtype=jnp.int32)
     stored_rows = (local_rows // rows_each) * block_rows + member * rows_each + local_rows % rows_each
@@ -216,12 +246,18 @@
     scale_prior = jnp.exp(prior_part[0] - top)
     totals = own_part[1] * scale_own + prior_part[1] * scale_prior
     summed = own_part[2] * scale_own[..., None] + prior_part[2] * scale_prior[..., None]
-    packed = jnp.concatenate([summed, top[..., None], totals[..., None]], axis=-1)
-    gathered = group_exchange(packed, "blk", group_size)
-    part_max = gathered[:, :, HEAD_DIM]
+    top_hi, top_lo = split_wide(top)
+    total_hi, total_lo = split_wide(totals)
+    packed = jnp.concatenate(
+        [summed.astype(jnp.bfloat16)] + [v[..., None] for v in (top_hi, top_lo, total_hi, total_lo)],
+        axis=-1,
+    )
+    gathered = group_exchange(packed, "blk", group_size).astype(jnp.float32)
+    part_max = gathered[:, :, HEAD_DIM] + gathered[:, :, HEAD_DIM + 1]
+    part_total = gathered[:, :, HEAD_DIM + 2] + gathered[:, :, HEAD_DIM + 3]
     best = jnp.max(part_max, axis=0)
     weight = jnp.exp(part_max - best[None])
-    total = jnp.sum(gathered[:, :, HEAD_DIM + 1] * weight, axis=0)
+    total = jnp.sum(part_total * weight, axis=0)
     heads_sum = jnp.sum(gathered[:, :, :HEAD_DIM] * weight[..., None], axis=0)
     heads_out = (heads_sum / total[:, None]).astype(jnp.bfloat16)
     term = jnp.einsum(

time: 255 us -> 236 us (0.925)
  the two profiles are of different devices: /device:TPU:48 before, /device:TPU:34 now
where the time goes in v8:
time: 236 us; the launch traced here: 235 us
  waiting for transfers between devices  111 us (47%)
  starting transfers between devices  37.6 us (16%)
  other arithmetic  33.9 us (14%)
  local copies, waits for them, and re-layouts  28.3 us (12%)
  blocking collectives  13.3 us (6%)
  matrix products  9.96 us (4%)
    all_to_all x1, waiting for transfers between devices, local(): lax.all_to_all(term.astype(jnp.bfloat16), 'blk', 0, 0, tiled=True)  53.9 us
    all_to_all x1, waiting for transfers between devices, local(): arrived = lax.all_to_all(x_part, 'blk', 0, 0, tiled=True)  27.5 us
    all_to_all x1, waiting for transfers between devices, local(): lax.all_to_all(jnp.concatenate([w_part, c_part], axis=1), 'blk', 0, 0, ti...  16 us
    all_to_all x1, starting transfers between devices, local(): arrived = lax.all_to_all(x_part, 'blk', 0, 0, tiled=True)  15.8 us
    all_to_all x1, blocking collectives, group_exchange(): lax.all_to_all(parts, axis, 0, 0, axis_index_groups=groups, tiled=True)  13.3 us
    select_n x3, other arithmetic, tenant_lookup(): span_ids = positions // SPAN  8.99 us
    all_to_all x1, starting transfers between devices, local(): lax.all_to_all(term.astype(jnp.bfloat16), 'blk', 0, 0, tiled=True)  8.73 us
    all_to_all x1, waiting for transfers between devices, group_gather(): lax.all_to_all(spread, axis, 0, 0, axis_index_groups=groups, tiled=True)  7.45 us
  transfers between devices with their start and end apart: 5, of which 5 were waited for; matrix products, arithmetic and copies ran while one was open for 21% of the time, Pallas kernels for 0%

profile of v8, /device:TPU:34, one launch (start us, length us, event | category | flops | bytes accessed | tf_op | source)
XLA Modules:
  0.0 234.9 jit_solution(11662716821610864224)
XLA Ops:
  0.0 2.8 %broadcast_in_dim.176 = bf16[32,256,128]{2,1,0:T(8,128)(2,1)} broadcast(bf16[256,128]{1,0:T(8,128)(2,1)} %param.14), dimensions={1,2} | broadcast | bytes 2162688 | tf_op jit(solution)/shard_map/broadcast_in_dim | solution.py:137
  2.8 15.8 %all-to-all-start = ((bf16[32,256,128]{2,1,0:T(8,128)(2,1)}), bf16[32,256,128]{2,1,0:T(8,128)(2,1)S(1)}, u32[]{:S(2)}, u32[]{:S(2)}) async-start(bf16[32,256,128]{2,1,0:T(8,128)(2,1)} %broadcast_in_dim.176), calls=%async_computation | async-start | bytes 4194304 | tf_op jit(solution)/shard_map/all_to_all | solution.py:158
  18.7 2.1 copy.102
  23.5 2.4 %copy.103 = bf16[32,128,64]{2,1,0:T(8,128)(2,1)} copy(bf16[32,128,64]{1,2,0:T(8,128)(2,1)} %bitcast.191) | data formatting | bytes 1048576 | tf_op jit(solution)/shard_map/transpose | solution.py:150
  25.9 2.4 %reshape.425 = bf16[32,64,128]{2,1,0:T(8,128)(2,1)} reshape(bf16[32,128,64]{2,1,0:T(8,128)(2,1)} %copy.103) | data formatting | bytes 1048576 | tf_op jit(solution)/shard_map/reshape | solution.py:151
  28.3 2.0 copy.159
  30.3 2.0 reshape.427
  33.6 3.9 %and_select_fusion.8 = (s32[256]{0:T(256)S(1)}, s32[256]{0:T(256)S(1)}, s32[256]{0:T(256)S(1)}) fusion(s32[4096]{0:T(1024)} %param.22, s32[]{:T(128)S(6)} %select_n.158, s32[]{:T(128)S(6)} %mul.239, s32[]{:T(128)S(6)} %select_n.164, s32[]{:T(128)S(6)} %mul.241, s32[]{:T(128)} %bitcast.17, s32[]{:T(128)} %bitcast.16, s32[]{:T(128)} %bitcast.15, s32[]{:T(128)} %bitcast.14, ...), kind=kLoop, calls=%fused_computation.202 | loop fusion | flops 26112 | bytes 4132 | tf_op jit(solution)/shard_map/jit(floor_divide)/jit(_where)/select_n | solution.py:42
  38.5 2.5 %broadcast_compare_fusion.3 = pred[1024]{0:T(1024)(128)(4,1)S(1)} fusion(s32[]{:T(128)} %bitcast.38, s32[]{:T(128)} %bitcast.37, s32[]{:T(128)} %bitcast.36, s32[]{:T(128)} %bitcast.35, s32[]{:T(128)S(6)} %mul.244, s32[]{:T(128)S(6)} %mul.281, pred[]{:T(512)S(6)} %gt.3), kind=kLoop, calls=%fused_computation.187 | loop fusion | flops 53248 | bytes 1049 | tf_op jit(solution)/shard_map/ge | solution.py:56
  41.1 2.5 %fusion.111 = s32[1024]{0:T(1024)S(1)} fusion(s32[]{:T(128)} %bitcast.38, s32[]{:T(128)} %bitcast.37, s32[]{:T(128)} %bitcast.36, s32[]{:T(128)} %bitcast.35, s32[]{:T(128)S(6)} %mul.281, s32[]{:T(128)S(6)} %mul.244, pred[]{:T(512)S(6)} %gt.3), kind=kLoop, calls=%fused_computation.164 | loop fusion | flops 52224 | bytes 4121 | tf_op jit(solution)/shard_map/jit(_where)/select_n | solution.py:234
  43.6 2.5 %add_select_fusion = s32[1024]{0:T(1024)S(1)} fusion(s32[]{:T(128)} %bitcast.38, s32[]{:T(128)} %bitcast.37, s32[]{:T(128)} %bitcast.36, s32[]{:T(128)} %bitcast.35, s32[]{:T(128)S(6)} %mul.244, s32[]{:T(128)S(6)} %mul.281, pred[]{:T(512)S(6)} %gt.3), kind=kLoop, calls=%fused_computation.121 | loop fusion | flops 67584 | bytes 4121 | tf_op jit(solution)/shard_map/jit(floor_divide)/jit(_where)/select_n | solution.py:42
  46.8 2.5 %add_select_fusion.1 = s32[1024]{0:T(1024)S(1)} fusion(s32[]{:T(128)} %bitcast.4, s32[]{:T(128)} %bitcast.3, s32[]{:T(128)} %bitcast.2, s32[]{:T(128)} %bitcast.1, s32[]{:T(128)S(6)} %mul.244, s32[]{:T(128)S(6)} %mul.239), kind=kLoop, calls=%fused_computation.125 | loop fusion | flops 66560 | bytes 4120 | tf_op jit(solution)/shard_map/jit(floor_divide)/jit(_where)/select_n | solution.py:42
  49.3 2.5 %fusion.113 = s32[1024]{0:T(1024)S(1)} fusion(s32[]{:T(128)} %bitcast.4, s32[]{:T(128)} %bitcast.3, s32[]{:T(128)} %bitcast.2, s32[]{:T(128)} %bitcast.1, s32[]{:T(128)S(6)} %mul.244, s32[]{:T(128)S(6)} %mul.239), kind=kLoop, calls=%fused_computation.168 | loop fusion | flops 51200 | bytes 4120 | tf_op jit(solution)/shard_map/add | solution.py:106
  51.9 27.5 %all-to-all-done = bf16[32,256,128]{2,1,0:T(8,128)(2,1)S(1)} async-done(((bf16[32,256,128]{2,1,0:T(8,128)(2,1)}), bf16[32,256,128]{2,1,0:T(8,128)(2,1)S(1)}, u32[]{:S(2)}, u32[]{:S(2)}) %all-to-all-start) | async-done | bytes 2097184 | tf_op jit(solution)/shard_map/all_to_all | solution.py:158
  79.4 2.3 pad_maximum_fusion
  81.7 7.4 %all-to-all-start.1 = ((bf16[32,128,128]{2,1,0:T(8,128)(2,1)}), bf16[32,128,128]{2,1,0:T(8,128)(2,1)}, u32[]{:S(2)}, u32[]{:S(2)}) async-start(bf16[32,128,128]{2,1,0:T(8,128)(2,1)} %pad_maximum_fusion), calls=%async_computation.1 | async-start | bytes 2097152 | tf_op jit(solution)/shard_map/all_to_all | solution.py:162
  89.2 2.5 %broadcast_compare_fusion.2 = pred[1024]{0:T(1024)(128)(4,1)S(1)} fusion(s32[]{:T(128)} %bitcast.4, s32[]{:T(128)} %bitcast.3, s32[]{:T(128)} %bitcast.2, s32[]{:T(128)} %bitcast.1, s32[]{:T(128)S(6)} %mul.244, s32[]{:T(128)S(6)} %mul.239), kind=kLoop, calls=%fused_computation.186 | loop fusion | flops 52224 | bytes 1048 | tf_op jit(solution)/shard_map/ge | solution.py:56
  92.3 2.5 %select_convert_fusion.1 = f32[1024]{0:T(1024)S(1)} fusion(s32[]{:T(128)} %bitcast.13, s32[]{:T(128)} %bitcast.12, s32[]{:T(128)} %bitcast.11, s32[]{:T(128)} %bitcast.10, s32[]{:T(128)S(6)} %mul.244), kind=kLoop, calls=%fused_computation.165 | loop fusion | flops 45056 | bytes 4116 | tf_op jit(solution)/shard_map/convert_element_type | solution.py:30
  95.1 2.2 fusion.52
  97.8 2.0 fusion.36
  100.2 16.0 %all-to-all-done.1 = bf16[32,128,128]{2,1,0:T(8,128)(2,1)} async-done(((bf16[32,128,128]{2,1,0:T(8,128)(2,1)}), bf16[32,128,128]{2,1,0:T(8,128)(2,1)}, u32[]{:S(2)}, u32[]{:S(2)}) %all-to-all-start.1) | async-done | bytes 1048608 | tf_op jit(solution)/shard_map/all_to_all | solution.py:162
  116.1 2.3 fusion.130
  118.4 2.4 %reshape.431 = bf16[32,128,64]{2,1,0:T(8,128)(2,1)} reshape(bf16[32,64,128]{2,1,0:T(8,128)(2,1)} %get-tuple-element.18) | data formatting | bytes 1048576 | tf_op jit(solution)/shard_map/reshape | solution.py:163
  120.8 1.9 fusion.42
  123.7 3.5 %all-to-all-start.2 = ((bf16[4,256,192]{1,2,0:T(8,128)(2,1)}), bf16[4,256,192]{1,2,0:T(8,128)(2,1)S(1)}, u32[]{:S(2)}, u32[]{:S(2)}) async-start(bf16[4,256,192]{1,2,0:T(8,128)(2,1)} %broadcast_in_dim.180), calls=%async_computation.2 | async-start | bytes 786432 | tf_op jit(solution)/shard_map/all_to_all | solution.py:90
  130.5 7.5 %all-to-all-done.2 = bf16[4,256,192]{1,2,0:T(8,128)(2,1)S(1)} async-done(((bf16[4,256,192]{1,2,0:T(8,128)(2,1)}), bf16[4,256,192]{1,2,0:T(8,128)(2,1)S(1)}, u32[]{:S(2)}, u32[]{:S(2)}) %all-to-all-start.2) | async-done | bytes 393248 | tf_op jit(solution)/shard_map/all_to_all | solution.py:90
  140.1 2.1 collective-permute-start
  144.1 6.5 %collective-permute-done = bf16[1024,256]{1,0:T(8,128)(2,1)S(1)} collective-permute-done((bf16[1024,256]{1,0:T(8,128)(2,1)S(1)}, bf16[1024,256]{1,0:T(8,128)(2,1)S(1)}, u32[]{:S(2)}, u32[]{:S(2)}) %collective-permute-start) | collective-permute-done | bytes 524320 | tf_op jit(solution)/shard_map/ppermute | solution.py:24
  155.0 13.3 %all_to_all.25 = bf16[4,256,132]{1,2,0:T(8,128)(2,1)S(1)} all-to-all(bf16[4,256,132]{1,2,0:T(8,128)(2,1)S(1)} %concatenate.43), channel_id=1, replica_groups={{0,16,32,48},{64,80,96,112},{128,144,160,176},{192,208,224,240},{256,27..., dimensions={0} | all-to-all | bytes 540672 | tf_op jit(solution)/shard_map/all_to_all | solution.py:95
  168.5 2.1 convert_bitcast_fusion
  170.6 8.7 %all-to-all-start.4 = ((bf16[32,256,128]{2,1,0:T(8,128)(2,1)}), bf16[32,256,128]{2,1,0:T(8,128)(2,1)S(1)}, u32[]{:S(2)}, u32[]{:S(2)}) async-start(bf16[32,256,128]{2,1,0:T(8,128)(2,1)} %convert_bitcast_fusion), calls=%async_computation.4 | async-start | bytes 4194304 | tf_op jit(solution)/shard_map/all_to_all | solution.py:269
  179.9 53.9 %all-to-all-done.4 = bf16[32,256,128]{2,1,0:T(8,128)(2,1)S(1)} async-done(((bf16[32,256,128]{2,1,0:T(8,128)(2,1)}), bf16[32,256,128]{2,1,0:T(8,128)(2,1)S(1)}, u32[]{:S(2)}, u32[]{:S(2)}) %all-to-all-start.4) | async-done | bytes 2097184 | tf_op jit(solution)/shard_map/all_to_all | solution.py:269
  (81 shorter events, 21.7 us)
Async XLA Ops:
  0.0 168.5 %copy-start = (bf16[128,4096]{1,0:T(8,128)(2,1)S(1)}, bf16[128,4096]{1,0:T(8,128)(2,1)}, u32[]{:S(2)}) copy-start(bf16[128,4096]{1,0:T(8,128)(2,1)} %param.18) | copy-start | bytes 3145732
  2.8 76.6 %all-to-all-start = ((bf16[32,256,128]{2,1,0:T(8,128)(2,1)}), bf16[32,256,128]{2,1,0:T(8,128)(2,1)S(1)}, u32[]{:S(2)}, u32[]{:S(2)}) async-start(bf16[32,256,128]{2,1,0:T(8,128)(2,1)} %broadcast_in_dim.176), calls=%async_computation | async-start | bytes 4194304 | tf_op jit(solution)/shard_map/all_to_all | solution.py:158
  18.6 13.7 %copy-start.5 = (s32[16]{0:T(128)S(1)}, s32[16]{0:T(128)}, u32[]{:S(2)}) copy-start(s32[16]{0:T(128)} %param.23) | copy-start | bytes 196
  18.7 14.2 %copy-start.4 = (s32[64]{0:T(128)S(1)}, s32[64]{0:T(128)}, u32[]{:S(2)}) copy-start(s32[64]{0:T(128)} %param.20) | copy-start | bytes 772
  18.7 18.9 %copy-start.6 = (s32[64]{0:T(128)S(1)}, s32[64]{0:T(128)}, u32[]{:S(2)}) copy-start(s32[64]{0:T(128)} %param.19) | copy-start | bytes 772
  25.9 69.0 %copy-start.3 = (s32[64]{0:T(128)S(1)}, s32[64]{0:T(128)}, u32[]{:S(2)}) copy-start(s32[64]{0:T(128)} %param.21) | copy-start | bytes 772
  25.9 69.2 %copy-start.2 = (bf16[4096]{0:T(1024)(128)(2,1)S(1)}, bf16[4096]{0:T(1024)(128)(2,1)}, u32[]{:S(2)}) copy-start(bf16[4096]{0:T(1024)(128)(2,1)} %param.15) | copy-start | bytes 24580
  81.7 34.4 %all-to-all-start.1 = ((bf16[32,128,128]{2,1,0:T(8,128)(2,1)}), bf16[32,128,128]{2,1,0:T(8,128)(2,1)}, u32[]{:S(2)}, u32[]{:S(2)}) async-start(bf16[32,128,128]{2,1,0:T(8,128)(2,1)} %pad_maximum_fusion), calls=%async_computation.1 | async-start | bytes 2097152 | tf_op jit(solution)/shard_map/all_to_all | solution.py:162
  123.7 14.2 %all-to-all-start.2 = ((bf16[4,256,192]{1,2,0:T(8,128)(2,1)}), bf16[4,256,192]{1,2,0:T(8,128)(2,1)S(1)}, u32[]{:S(2)}, u32[]{:S(2)}) async-start(bf16[4,256,192]{1,2,0:T(8,128)(2,1)} %broadcast_in_dim.180), calls=%async_computation.2 | async-start | bytes 786432 | tf_op jit(solution)/shard_map/all_to_all | solution.py:90
  128.5 13.7 %copy-start.1 = (pred[256,1024]{0,1:T(8,128)(4,1)S(1)}, pred[256,1024]{0,1:T(8,128)(4,1)}, u32[]{:S(2)}) copy-start(pred[256,1024]{0,1:T(8,128)(4,1)} %get-tuple-element.39) | copy-start | bytes 786436
  140.1 10.5 %collective-permute-start = (bf16[1024,256]{1,0:T(8,128)(2,1)S(1)}, bf16[1024,256]{1,0:T(8,128)(2,1)S(1)}, u32[]{:S(2)}, u32[]{:S(2)}) collective-permute-start(bf16[1024,256]{1,0:T(8,128)(2,1)S(1)} %scatter_fusion), channel_id=1, source_target_pairs={{0,1},{1,2},{2,3},{3,4},{4,5},{5,6},{6,7},{7,8},{8,9},{9,10},{10,1... | collective-permute-start | bytes 1572872 | tf_op jit(solution)/shard_map/ppermute | solution.py:24
  170.6 63.3 %all-to-all-start.4 = ((bf16[32,256,128]{2,1,0:T(8,128)(2,1)}), bf16[32,256,128]{2,1,0:T(8,128)(2,1)S(1)}, u32[]{:S(2)}, u32[]{:S(2)}) async-start(bf16[32,256,128]{2,1,0:T(8,128)(2,1)} %convert_bitcast_fusion), calls=%async_computation.4 | async-start | bytes 4194304 | tf_op jit(solution)/shard_map/all_to_all | solution.py:269

commit v9 on v8

--- a/solution.py
+++ b/solution.py
@@ -72,12 +72,6 @@
     totals = first[1] * scale_one + second[1] * scale_two
     summed = first[2] * scale_one[..., None] + second[2] * scale_two[..., None]
     return summed / totals[..., None]
-
-
-def split_wide(values):
-    high = values.astype(jnp.bfloat16)
-    low = (values - high.astype(jnp.float32)).astype(jnp.bfloat16)
-    return high, low
 
 
 def member_groups(devices, size):
@@ -246,15 +240,10 @@
     scale_prior = jnp.exp(prior_part[0] - top)
     totals = own_part[1] * scale_own + prior_part[1] * scale_prior
     summed = own_part[2] * scale_own[..., None] + prior_part[2] * scale_prior[..., None]
-    top_hi, top_lo = split_wide(top)
-    total_hi, total_lo = split_wide(totals)
-    packed = jnp.concatenate(
-        [summed.astype(jnp.bfloat16)] + [v[..., None] for v in (top_hi, top_lo, total_hi, total_lo)],
-        axis=-1,
-    )
-    gathered = group_exchange(packed, "blk", group_size).astype(jnp.float32)
-    part_max = gathered[:, :, HEAD_DIM] + gathered[:, :, HEAD_DIM + 1]
-    part_total = gathered[:, :, HEAD_DIM + 2] + gathered[:, :, HEAD_DIM + 3]
+    packed = jnp.concatenate([summed, top[..., None], totals[..., None]], axis=-1)
+    gathered = group_exchange(packed, "blk", group_size)
+    part_max = gathered[:, :, HEAD_DIM]
+    part_total = gathered[:, :, HEAD_DIM + 1]
     best = jnp.max(part_max, axis=0)
     weight = jnp.exp(part_max - best[None])
     total = jnp.sum(part_total * weight, axis=0)

time: 236 us -> 246 us (1.042)
  the two profiles are of different devices: /device:TPU:34 before, /device:TPU:26 now
where the time goes in v9:
time: 246 us; the launch traced here: 245 us
  waiting for transfers between devices  111 us (45%)
  starting transfers between devices  38.6 us (16%)
  other arithmetic  34.4 us (14%)
  local copies, waits for them, and re-layouts  28.8 us (12%)
  blocking collectives  19.7 us (8%)
  matrix products  11.8 us (5%)
    all_to_all x1, waiting for transfers between devices, local(): lax.all_to_all(term.astype(jnp.bfloat16), 'blk', 0, 0, tiled=True)  56.7 us
    all_to_all x1, waiting for transfers between devices, local(): arrived = lax.all_to_all(x_part, 'blk', 0, 0, tiled=True)  23.9 us
    all_to_all x1, blocking collectives, group_exchange(): lax.all_to_all(parts, axis, 0, 0, axis_index_groups=groups, tiled=True)  19.7 us
    all_to_all x1, waiting for transfers between devices, local(): lax.all_to_all(jnp.concatenate([w_part, c_part], axis=1), 'blk', 0, 0, ti...  17.6 us
    all_to_all x1, starting transfers between devices, local(): arrived = lax.all_to_all(x_part, 'blk', 0, 0, tiled=True)  15.9 us
    all_to_all x1, starting transfers between devices, local(): lax.all_to_all(jnp.concatenate([w_part, c_part], axis=1), 'blk', 0, 0, ti...  11.5 us
    select_n x3, other arithmetic, tenant_lookup(): span_ids = positions // SPAN  8.8 us
    all_to_all x1, waiting for transfers between devices, group_gather(): lax.all_to_all(spread, axis, 0, 0, axis_index_groups=groups, tiled=True)  6.56 us
  transfers between devices with their start and end apart: 5, of which 5 were waited for; matrix products, arithmetic and copies ran while one was open for 21% of the time, Pallas kernels for 0%

profile of v9, /device:TPU:26, one launch (start us, length us, event | category | flops | bytes accessed | tf_op | source)
XLA Modules:
  0.0 245.0 jit_solution(436078694278491725)
XLA Ops:
  0.0 2.8 %broadcast_in_dim.174 = bf16[32,256,128]{2,1,0:T(8,128)(2,1)} broadcast(bf16[256,128]{1,0:T(8,128)(2,1)} %param.14), dimensions={1,2} | broadcast | bytes 2162688 | tf_op jit(solution)/shard_map/broadcast_in_dim | solution.py:131
  2.8 15.9 %all-to-all-start = ((bf16[32,256,128]{2,1,0:T(8,128)(2,1)}), bf16[32,256,128]{2,1,0:T(8,128)(2,1)S(1)}, u32[]{:S(2)}, u32[]{:S(2)}) async-start(bf16[32,256,128]{2,1,0:T(8,128)(2,1)} %broadcast_in_dim.174), calls=%async_computation | async-start | bytes 4194304 | tf_op jit(solution)/shard_map/all_to_all | solution.py:152
  20.1 3.8 %and_select_fusion.8 = (s32[256]{0:T(256)S(1)}, s32[256]{0:T(256)S(1)}, s32[256]{0:T(256)S(1)}) fusion(s32[4096]{0:T(1024)} %param.22, s32[]{:T(128)S(6)} %select_n.158, s32[]{:T(128)S(6)} %mul.231, s32[]{:T(128)S(6)} %select_n.164, s32[]{:T(128)S(6)} %mul.233, s32[]{:T(128)} %bitcast.17, s32[]{:T(128)} %bitcast.16, s32[]{:T(128)} %bitcast.15, s32[]{:T(128)} %bitcast.14, ...), kind=kLoop, calls=%fused_computation.192 | loop fusion | flops 26112 | bytes 4132 | tf_op jit(solution)/shard_map/jit(floor_divide)/jit(_where)/select_n | solution.py:42
  23.9 2.1 copy.95
  28.7 2.4 copy.96
  31.1 2.4 reshape.375
  33.5 2.0 copy.141
  35.5 2.0 reshape.377
  38.5 2.5 %broadcast_compare_fusion.3 = pred[1024]{0:T(1024)(128)(4,1)S(1)} fusion(s32[]{:T(128)} %bitcast.38, s32[]{:T(128)} %bitcast.37, s32[]{:T(128)} %bitcast.36, s32[]{:T(128)} %bitcast.35, s32[]{:T(128)S(6)} %mul.236, s32[]{:T(128)S(6)} %mul.273, pred[]{:T(512)S(6)} %gt.3), kind=kLoop, calls=%fused_computation.177 | loop fusion | flops 53248 | bytes 1049 | tf_op jit(solution)/shard_map/ge | solution.py:56
  41.0 2.5 %fusion.105 = s32[1024]{0:T(1024)S(1)} fusion(s32[]{:T(128)} %bitcast.38, s32[]{:T(128)} %bitcast.37, s32[]{:T(128)} %bitcast.36, s32[]{:T(128)} %bitcast.35, s32[]{:T(128)S(6)} %mul.273, s32[]{:T(128)S(6)} %mul.236, pred[]{:T(512)S(6)} %gt.3), kind=kLoop, calls=%fused_computation.154 | loop fusion | flops 52224 | bytes 4121 | tf_op jit(solution)/shard_map/jit(_where)/select_n | solution.py:228
  43.5 2.5 %add_select_fusion = s32[1024]{0:T(1024)S(1)} fusion(s32[]{:T(128)} %bitcast.38, s32[]{:T(128)} %bitcast.37, s32[]{:T(128)} %bitcast.36, s32[]{:T(128)} %bitcast.35, s32[]{:T(128)S(6)} %mul.236, s32[]{:T(128)S(6)} %mul.273, pred[]{:T(512)S(6)} %gt.3), kind=kLoop, calls=%fused_computation.121 | loop fusion | flops 67584 | bytes 4121 | tf_op jit(solution)/shard_map/jit(floor_divide)/jit(_where)/select_n | solution.py:42
  46.6 2.5 %add_select_fusion.1 = s32[1024]{0:T(1024)S(1)} fusion(s32[]{:T(128)} %bitcast.4, s32[]{:T(128)} %bitcast.3, s32[]{:T(128)} %bitcast.2, s32[]{:T(128)} %bitcast.1, s32[]{:T(128)S(6)} %mul.236, s32[]{:T(128)S(6)} %mul.231), kind=kLoop, calls=%fused_computation.125 | loop fusion | flops 66560 | bytes 4120 | tf_op jit(solution)/shard_map/jit(floor_divide)/jit(_where)/select_n | solution.py:42
  49.1 2.5 %fusion.107 = s32[1024]{0:T(1024)S(1)} fusion(s32[]{:T(128)} %bitcast.4, s32[]{:T(128)} %bitcast.3, s32[]{:T(128)} %bitcast.2, s32[]{:T(128)} %bitcast.1, s32[]{:T(128)S(6)} %mul.236, s32[]{:T(128)S(6)} %mul.231), kind=kLoop, calls=%fused_computation.158 | loop fusion | flops 51200 | bytes 4120 | tf_op jit(solution)/shard_map/add | solution.py:100
  51.6 23.9 %all-to-all-done = bf16[32,256,128]{2,1,0:T(8,128)(2,1)S(1)} async-done(((bf16[32,256,128]{2,1,0:T(8,128)(2,1)}), bf16[32,256,128]{2,1,0:T(8,128)(2,1)S(1)}, u32[]{:S(2)}, u32[]{:S(2)}) %all-to-all-start) | async-done | bytes 2097184 | tf_op jit(solution)/shard_map/all_to_all | solution.py:152
  75.5 2.3 pad_maximum_fusion
  77.8 11.5 %all-to-all-start.1 = ((bf16[32,128,128]{2,1,0:T(8,128)(2,1)}), bf16[32,128,128]{2,1,0:T(8,128)(2,1)}, u32[]{:S(2)}, u32[]{:S(2)}) async-start(bf16[32,128,128]{2,1,0:T(8,128)(2,1)} %pad_maximum_fusion), calls=%async_computation.1 | async-start | bytes 2097152 | tf_op jit(solution)/shard_map/all_to_all | solution.py:156
  89.3 2.5 %broadcast_compare_fusion.2 = pred[1024]{0:T(1024)(128)(4,1)S(1)} fusion(s32[]{:T(128)} %bitcast.4, s32[]{:T(128)} %bitcast.3, s32[]{:T(128)} %bitcast.2, s32[]{:T(128)} %bitcast.1, s32[]{:T(128)S(6)} %mul.236, s32[]{:T(128)S(6)} %mul.231), kind=kLoop, calls=%fused_computation.176 | loop fusion | flops 52224 | bytes 1048 | tf_op jit(solution)/shard_map/ge | solution.py:56
  92.4 2.5 %select_convert_fusion.1 = f32[1024]{0:T(1024)S(1)} fusion(s32[]{:T(128)} %bitcast.13, s32[]{:T(128)} %bitcast.12, s32[]{:T(128)} %bitcast.11, s32[]{:T(128)} %bitcast.10, s32[]{:T(128)S(6)} %mul.236), kind=kLoop, calls=%fused_computation.155 | loop fusion | flops 45056 | bytes 4116 | tf_op jit(solution)/shard_map/convert_element_type | solution.py:30
  95.2 2.2 fusion.46
  97.9 2.0 fusion.33
  100.2 17.6 %all-to-all-done.1 = bf16[32,128,128]{2,1,0:T(8,128)(2,1)} async-done(((bf16[32,128,128]{2,1,0:T(8,128)(2,1)}), bf16[32,128,128]{2,1,0:T(8,128)(2,1)}, u32[]{:S(2)}, u32[]{:S(2)}) %all-to-all-start.1) | async-done | bytes 1048608 | tf_op jit(solution)/shard_map/all_to_all | solution.py:156
  117.9 2.3 fusion.122
  120.2 2.4 reshape.381
  125.5 3.5 %all-to-all-start.2 = ((bf16[4,256,192]{1,2,0:T(8,128)(2,1)}), bf16[4,256,192]{1,2,0:T(8,128)(2,1)S(1)}, u32[]{:S(2)}, u32[]{:S(2)}) async-start(bf16[4,256,192]{1,2,0:T(8,128)(2,1)} %broadcast_in_dim.178), calls=%async_computation.2 | async-start | bytes 786432 | tf_op jit(solution)/shard_map/all_to_all | solution.py:84
  133.8 6.6 %all-to-all-done.2 = bf16[4,256,192]{1,2,0:T(8,128)(2,1)S(1)} async-done(((bf16[4,256,192]{1,2,0:T(8,128)(2,1)}), bf16[4,256,192]{1,2,0:T(8,128)(2,1)S(1)}, u32[]{:S(2)}, u32[]{:S(2)}) %all-to-all-start.2) | async-done | bytes 393248 | tf_op jit(solution)/shard_map/all_to_all | solution.py:84
  142.3 2.1 collective-permute-start
  146.5 6.4 %collective-permute-done = bf16[1024,256]{1,0:T(8,128)(2,1)} collective-permute-done((bf16[1024,256]{1,0:T(8,128)(2,1)S(1)}, bf16[1024,256]{1,0:T(8,128)(2,1)}, u32[]{:S(2)}, u32[]{:S(2)}) %collective-permute-start) | collective-permute-done | bytes 524320 | tf_op jit(solution)/shard_map/ppermute | solution.py:24
  157.0 2.0 fusion.24
  159.1 19.7 %all_to_all.25 = f32[4,256,130]{1,2,0:T(8,128)S(1)} all-to-all(f32[4,256,130]{1,2,0:T(8,128)S(1)} %pad_maximum_fusion.1), channel_id=1, replica_groups={{0,16,32,48},{64,80,96,112},{128,144,160,176},{192,208,224,240},{256,27..., dimensions={0} | all-to-all | bytes 1064960 | tf_op jit(solution)/shard_map/all_to_all | solution.py:89
  178.9 2.1 convert_bitcast_fusion
  181.0 5.6 %all-to-all-start.4 = ((bf16[32,256,128]{2,1,0:T(8,128)(2,1)}), bf16[32,256,128]{2,1,0:T(8,128)(2,1)S(1)}, u32[]{:S(2)}, u32[]{:S(2)}) async-start(bf16[32,256,128]{2,1,0:T(8,128)(2,1)} %convert_bitcast_fusion), calls=%async_computation.4 | async-start | bytes 4194304 | tf_op jit(solution)/shard_map/all_to_all | solution.py:258
  187.2 56.7 %all-to-all-done.4 = bf16[32,256,128]{2,1,0:T(8,128)(2,1)S(1)} async-done(((bf16[32,256,128]{2,1,0:T(8,128)(2,1)}), bf16[32,256,128]{2,1,0:T(8,128)(2,1)S(1)}, u32[]{:S(2)}, u32[]{:S(2)}) %all-to-all-start.4) | async-done | bytes 2097184 | tf_op jit(solution)/shard_map/all_to_all | solution.py:258
  (72 shorter events, 24.9 us)
Async XLA Ops:
  0.0 178.9 %copy-start = (bf16[128,4096]{1,0:T(8,128)(2,1)S(1)}, bf16[128,4096]{1,0:T(8,128)(2,1)}, u32[]{:S(2)}) copy-start(bf16[128,4096]{1,0:T(8,128)(2,1)} %param.18) | copy-start | bytes 3145732
  0.0 18.8 %copy-start.5 = (s32[16]{0:T(128)S(1)}, s32[16]{0:T(128)}, u32[]{:S(2)}) copy-start(s32[16]{0:T(128)} %param.23) | copy-start | bytes 196
  0.0 19.4 %copy-start.4 = (s32[64]{0:T(128)S(1)}, s32[64]{0:T(128)}, u32[]{:S(2)}) copy-start(s32[64]{0:T(128)} %param.20) | copy-start | bytes 772
  2.8 72.7 %all-to-all-start = ((bf16[32,256,128]{2,1,0:T(8,128)(2,1)}), bf16[32,256,128]{2,1,0:T(8,128)(2,1)S(1)}, u32[]{:S(2)}, u32[]{:S(2)}) async-start(bf16[32,256,128]{2,1,0:T(8,128)(2,1)} %broadcast_in_dim.174), calls=%async_computation | async-start | bytes 4194304 | tf_op jit(solution)/shard_map/all_to_all | solution.py:152
  23.9 13.6 %copy-start.6 = (s32[64]{0:T(128)S(1)}, s32[64]{0:T(128)}, u32[]{:S(2)}) copy-start(s32[64]{0:T(128)} %param.19) | copy-start | bytes 772
  31.1 63.8 %copy-start.3 = (s32[64]{0:T(128)S(1)}, s32[64]{0:T(128)}, u32[]{:S(2)}) copy-start(s32[64]{0:T(128)} %param.21) | copy-start | bytes 772
  31.1 64.1 %copy-start.2 = (bf16[4096]{0:T(1024)(128)(2,1)S(1)}, bf16[4096]{0:T(1024)(128)(2,1)}, u32[]{:S(2)}) copy-start(bf16[4096]{0:T(1024)(128)(2,1)} %param.15) | copy-start | bytes 24580
  77.8 40.1 %all-to-all-start.1 = ((bf16[32,128,128]{2,1,0:T(8,128)(2,1)}), bf16[32,128,128]{2,1,0:T(8,128)(2,1)}, u32[]{:S(2)}, u32[]{:S(2)}) async-start(bf16[32,128,128]{2,1,0:T(8,128)(2,1)} %pad_maximum_fusion), calls=%async_computation.1 | async-start | bytes 2097152 | tf_op jit(solution)/shard_map/all_to_all | solution.py:156
  125.5 14.9 %all-to-all-start.2 = ((bf16[4,256,192]{1,2,0:T(8,128)(2,1)}), bf16[4,256,192]{1,2,0:T(8,128)(2,1)S(1)}, u32[]{:S(2)}, u32[]{:S(2)}) async-start(bf16[4,256,192]{1,2,0:T(8,128)(2,1)} %broadcast_in_dim.178), calls=%async_computation.2 | async-start | bytes 786432 | tf_op jit(solution)/shard_map/all_to_all | solution.py:84
  130.9 13.7 %copy-start.1 = (pred[256,1024]{0,1:T(8,128)(4,1)S(1)}, pred[256,1024]{0,1:T(8,128)(4,1)}, u32[]{:S(2)}) copy-start(pred[256,1024]{0,1:T(8,128)(4,1)} %get-tuple-element.37) | copy-start | bytes 786436
  142.3 10.6 %collective-permute-start = (bf16[1024,256]{1,0:T(8,128)(2,1)S(1)}, bf16[1024,256]{1,0:T(8,128)(2,1)}, u32[]{:S(2)}, u32[]{:S(2)}) collective-permute-start(bf16[1024,256]{1,0:T(8,128)(2,1)S(1)} %scatter_fusion), channel_id=1, source_target_pairs={{0,1},{1,2},{2,3},{3,4},{4,5},{5,6},{6,7},{7,8},{8,9},{9,10},{10,1... | collective-permute-start | bytes 1572872 | tf_op jit(solution)/shard_map/ppermute | solution.py:24
  181.0 63.0 %all-to-all-start.4 = ((bf16[32,256,128]{2,1,0:T(8,128)(2,1)}), bf16[32,256,128]{2,1,0:T(8,128)(2,1)S(1)}, u32[]{:S(2)}, u32[]{:S(2)}) async-start(bf16[32,256,128]{2,1,0:T(8,128)(2,1)} %convert_bitcast_fusion), calls=%async_computation.4 | async-start | bytes 4194304 | tf_op jit(solution)/shard_map/all_to_all | solution.py:258

commit v10 on v9

--- a/solution.py
+++ b/solution.py
@@ -149,13 +149,9 @@
         .transpose(2, 0, 1, 3)
         .reshape(blk_count, rows_each * 2, HEAD_DIM)
     )
-    arrived = lax.all_to_all(x_part, "blk", 0, 0, tiled=True)
-    wide = arrived.astype(jnp.float32)
-    arrived, w_part, c_part = lax.optimization_barrier((arrived, w_part, c_part))
-    w_rows = w_part.shape[1]
-    moved = lax.all_to_all(jnp.concatenate([w_part, c_part], axis=1), "blk", 0, 0, tiled=True)
-    kv_cols = moved[:, :w_rows].reshape(blk_count, own_cols, pair_cols)
-    stored = moved[:, w_rows:].reshape(blk_count * rows_each, 2 * HEAD_DIM)
+    arrived = lax.all_to_all(jnp.concatenate([x_part, w_part], axis=1), "blk", 0, 0, tiled=True)
+    wide = arrived[:, :slots].astype(jnp.float32)
+    kv_cols = arrived[:, slots:].reshape(blk_count, own_cols, pair_cols)
 
     gains = norm_gain.astype(jnp.float32).reshape(blk_count, 1, own_cols)
     scaled = (wide * gains).astype(jnp.bfloat16)
@@ -187,7 +183,12 @@
     second = pair_piece[:, quarter:]
     turned = jnp.concatenate([first * cosine - second * sine, second * cosine + first * sine], axis=1)
     own_piece = jnp.where(member < key_members, turned, pair_piece).astype(jnp.bfloat16)
-    shared = group_gather(jnp.concatenate([own_query, own_piece], axis=1), "blk", group_size)
+    outgoing = jnp.concatenate([own_query, own_piece], axis=1)
+    outgoing, c_part = lax.optimization_barrier((outgoing, c_part))
+    stored = lax.all_to_all(c_part, "blk", 0, 0, tiled=True).reshape(
+        blk_count * rows_each, 2 * HEAD_DIM
+    )
+    shared = group_gather(outgoing, "blk", group_size)
     queries = shared[:, :, :HEAD_DIM].transpose(1, 0, 2)
     pieces = shared[:, :, HEAD_DIM:]
     fresh_keys = jnp.concatenate(

time: 246 us -> 247 us (level)
  the two profiles are of different devices: /device:TPU:26 before, /device:TPU:2 now
where the time goes in v10:
time: 247 us; the launch traced here: 246 us
  waiting for transfers between devices  128 us (52%)
  starting transfers between devices  42.4 us (17%)
  other arithmetic  32.7 us (13%)
  blocking collectives  19.2 us (8%)
  local copies, waits for them, and re-layouts  12.6 us (5%)
  matrix products  11 us (4%)
    all_to_all x1, waiting for transfers between devices, local(): lax.all_to_all(term.astype(jnp.bfloat16), 'blk', 0, 0, tiled=True)  53.1 us
    all_to_all x1, waiting for transfers between devices, local(): lax.all_to_all(jnp.concatenate([x_part, w_part], axis=1), 'blk', 0, 0, ti...  44 us
    all_to_all x1, blocking collectives, group_exchange(): lax.all_to_all(parts, axis, 0, 0, axis_index_groups=groups, tiled=True)  19.2 us
    all_to_all x1, starting transfers between devices, local(): lax.all_to_all(jnp.concatenate([x_part, w_part], axis=1), 'blk', 0, 0, ti...  16.2 us
    all_to_all x1, waiting for transfers between devices, local(): lax.all_to_all(c_part, 'blk', 0, 0, tiled=True)  15.6 us
    all_to_all x1, starting transfers between devices, local(): lax.all_to_all(c_part, 'blk', 0, 0, tiled=True)  13 us
    select_n x3, other arithmetic, tenant_lookup(): span_ids = positions // SPAN  8.92 us
    all_to_all x1, waiting for transfers between devices, group_gather(): lax.all_to_all(spread, axis, 0, 0, axis_index_groups=groups, tiled=True)  8.39 us
  transfers between devices with their start and end apart: 5, of which 5 were waited for; matrix products, arithmetic and copies ran while one was open for 12% of the time, Pallas kernels for 0%

profile of v10, /device:TPU:2, one launch (start us, length us, event | category | flops | bytes accessed | tf_op | source)
XLA Modules:
  0.0 246.0 jit_solution(7817517999627437416)
XLA Ops:
  0.0 1.4 copy.94
  3.1 1.7 pad_maximum_fusion
  4.9 16.2 %all-to-all-start = ((bf16[32,320,128]{2,1,0:T(8,128)(2,1)}), bf16[32,320,128]{2,1,0:T(8,128)(2,1)}, u32[]{:S(2)}, u32[]{:S(2)}) async-start(bf16[32,320,128]{2,1,0:T(8,128)(2,1)} %pad_maximum_fusion), calls=%async_computation | async-start | bytes 5242880 | tf_op jit(solution)/shard_map/all_to_all | solution.py:152
  22.5 4.1 %and_select_fusion.8 = (s32[256]{0:T(256)S(1)}, s32[256]{0:T(256)S(1)}, s32[256]{0:T(256)S(1)}) fusion(s32[4096]{0:T(1024)} %param.22, s32[]{:T(128)S(6)} %select_n.158, s32[]{:T(128)S(6)} %mul.231, s32[]{:T(128)S(6)} %select_n.164, s32[]{:T(128)S(6)} %mul.233, s32[]{:T(128)} %bitcast.24, s32[]{:T(128)} %bitcast.23, s32[]{:T(128)} %bitcast.22, s32[]{:T(128)} %bitcast.21, ...), kind=kLoop, calls=%fused_computation.192 | loop fusion | flops 26112 | bytes 4132 | tf_op jit(solution)/shard_map/jit(floor_divide)/jit(_where)/select_n | solution.py:42
  28.7 2.4 broadcast_compare_fusion.3
  31.1 2.4 fusion.105
  33.5 2.4 add_select_fusion
  36.6 2.4 add_select_fusion.1
  39.0 2.4 fusion.107
  42.1 2.5 %select_convert_fusion.1 = f32[1024]{0:T(1024)S(1)} fusion(s32[]{:T(128)} %bitcast.20, s32[]{:T(128)} %bitcast.19, s32[]{:T(128)} %bitcast.18, s32[]{:T(128)} %bitcast.17, s32[]{:T(128)S(6)} %mul.236), kind=kLoop, calls=%fused_computation.155 | loop fusion | flops 45056 | bytes 4116 | tf_op jit(solution)/shard_map/convert_element_type | solution.py:30
  44.7 44.0 %all-to-all-done = bf16[32,320,128]{2,1,0:T(8,128)(2,1)} async-done(((bf16[32,320,128]{2,1,0:T(8,128)(2,1)}), bf16[32,320,128]{2,1,0:T(8,128)(2,1)}, u32[]{:S(2)}, u32[]{:S(2)}) %all-to-all-start) | async-done | bytes 2621472 | tf_op jit(solution)/shard_map/all_to_all | solution.py:152
  88.7 2.1 fusion.1
  90.8 1.1 slice.160
  92.3 2.7 %fusion.33 = f32[256,1,128]{0,2,1:T(8,128)S(1)} fusion(bf16[32,128,128]{2,1,0:T(8,128)(2,1)} %bitcast.158, f32[32,128]{1,0:T(8,128)S(1)} %bitcast_convert_fusion, bf16[32,320,128]{2,1,0:T(8,128)(2,1)} %all-to-all-done, f32[256]{0:T(256)S(1)} %add_rsqrt_fusion), kind=kOutput, calls=%fused_computation.33 | convolution fusion | flops 271613952 | bytes 3294208 | tf_op jit(solution)/shard_map/ksc,kcd->sd/dot_general | solution.py:160
  95.3 2.3 fusion.39
  98.6 7.1 %all-to-all-start.2 = ((bf16[4,256,192]{1,2,0:T(8,128)(2,1)}), bf16[4,256,192]{1,2,0:T(8,128)(2,1)S(1)}, u32[]{:S(2)}, u32[]{:S(2)}) async-start(bf16[4,256,192]{1,2,0:T(8,128)(2,1)} %broadcast_in_dim.178), calls=%async_computation.2 | async-start | bytes 786432 | tf_op jit(solution)/shard_map/all_to_all | solution.py:84
  105.7 2.4 broadcast_compare_fusion.2
  108.4 1.3 fusion.46
  109.7 8.4 %all-to-all-done.2 = bf16[4,256,192]{1,2,0:T(8,128)(2,1)S(1)} async-done(((bf16[4,256,192]{1,2,0:T(8,128)(2,1)}), bf16[4,256,192]{1,2,0:T(8,128)(2,1)S(1)}, u32[]{:S(2)}, u32[]{:S(2)}) %all-to-all-start.2) | async-done | bytes 393248 | tf_op jit(solution)/shard_map/all_to_all | solution.py:84
  118.1 13.0 %all-to-all-start.1 = ((bf16[32,64,128]{2,1,0:T(8,128)(2,1)}), bf16[32,64,128]{2,1,0:T(8,128)(2,1)S(1)}, u32[]{:S(2)}, u32[]{:S(2)}) async-start(bf16[32,64,128]{2,1,0:T(8,128)(2,1)} %reshape.380), calls=%async_computation.1 | async-start | bytes 1048576 | tf_op jit(solution)/shard_map/all_to_all | solution.py:188
  131.5 15.6 %all-to-all-done.1 = bf16[32,64,128]{2,1,0:T(8,128)(2,1)S(1)} async-done(((bf16[32,64,128]{2,1,0:T(8,128)(2,1)}), bf16[32,64,128]{2,1,0:T(8,128)(2,1)S(1)}, u32[]{:S(2)}, u32[]{:S(2)}) %all-to-all-start.1) | async-done | bytes 524320 | tf_op jit(solution)/shard_map/all_to_all | solution.py:188
  147.4 1.2 fusion.56
  149.2 1.8 scatter_fusion
  151.0 2.1 collective-permute-start
  155.0 6.5 %collective-permute-done = bf16[1024,256]{1,0:T(8,128)(2,1)S(1)} collective-permute-done((bf16[1024,256]{1,0:T(8,128)(2,1)S(1)}, bf16[1024,256]{1,0:T(8,128)(2,1)S(1)}, u32[]{:S(2)}, u32[]{:S(2)}) %collective-permute-start) | collective-permute-done | bytes 524320 | tf_op jit(solution)/shard_map/ppermute | solution.py:24
  162.3 1.2 fusion.18
  163.6 1.0 fusion.6
  164.6 1.1 fusion.24
  165.8 19.2 %all_to_all.25 = f32[4,256,130]{1,2,0:T(8,128)S(1)} all-to-all(f32[4,256,130]{1,2,0:T(8,128)S(1)} %pad_maximum_fusion.1), channel_id=1, replica_groups={{0,16,32,48},{64,80,96,112},{128,144,160,176},{192,208,224,240},{256,27..., dimensions={0} | all-to-all | bytes 1064960 | tf_op jit(solution)/shard_map/all_to_all | solution.py:89
  185.1 2.1 convert_bitcast_fusion
  187.2 4.0 %all-to-all-start.4 = ((bf16[32,256,128]{2,1,0:T(8,128)(2,1)}), bf16[32,256,128]{2,1,0:T(8,128)(2,1)S(1)}, u32[]{:S(2)}, u32[]{:S(2)}) async-start(bf16[32,256,128]{2,1,0:T(8,128)(2,1)} %convert_bitcast_fusion), calls=%async_computation.4 | async-start | bytes 4194304 | tf_op jit(solution)/shard_map/all_to_all | solution.py:259
  191.9 53.1 %all-to-all-done.4 = bf16[32,256,128]{2,1,0:T(8,128)(2,1)S(1)} async-done(((bf16[32,256,128]{2,1,0:T(8,128)(2,1)}), bf16[32,256,128]{2,1,0:T(8,128)(2,1)S(1)}, u32[]{:S(2)}, u32[]{:S(2)}) %all-to-all-start.4) | async-done | bytes 2097184 | tf_op jit(solution)/shard_map/all_to_all | solution.py:259
  (74 shorter events, 14.3 us)
Async XLA Ops:
  0.0 185.1 %copy-start = (bf16[128,4096]{1,0:T(8,128)(2,1)S(1)}, bf16[128,4096]{1,0:T(8,128)(2,1)}, u32[]{:S(2)}) copy-start(bf16[128,4096]{1,0:T(8,128)(2,1)} %param.18) | copy-start | bytes 3145732
  0.0 2.6 %copy-start.2 = (bf16[256,128]{1,0:T(8,128)(2,1)S(1)}, bf16[256,128]{1,0:T(8,128)(2,1)}, u32[]{:S(2)}) copy-start(bf16[256,128]{1,0:T(8,128)(2,1)} %param.14) | copy-start | bytes 196612
  3.1 18.0 %copy-start.6 = (s32[16]{0:T(128)S(1)}, s32[16]{0:T(128)}, u32[]{:S(2)}) copy-start(s32[16]{0:T(128)} %param.23) | copy-start | bytes 196
  3.1 18.7 %copy-start.5 = (s32[64]{0:T(128)S(1)}, s32[64]{0:T(128)}, u32[]{:S(2)}) copy-start(s32[64]{0:T(128)} %param.20) | copy-start | bytes 772
  3.1 23.5 %copy-start.1 = (bf16[128,8,256]{2,1,0:T(8,128)(2,1)S(1)}, bf16[128,8,256]{2,1,0:T(8,128)(2,1)}, u32[]{:S(2)}) copy-start(bf16[128,8,256]{2,1,0:T(8,128)(2,1)} %param.13) | copy-start | bytes 1572868
  4.9 22.9 %copy-start.7 = (s32[64]{0:T(128)S(1)}, s32[64]{0:T(128)}, u32[]{:S(2)}) copy-start(s32[64]{0:T(128)} %param.19) | copy-start | bytes 772
  4.9 39.8 %copy-start.3 = (bf16[4096]{0:T(1024)(128)(2,1)S(1)}, bf16[4096]{0:T(1024)(128)(2,1)}, u32[]{:S(2)}) copy-start(bf16[4096]{0:T(1024)(128)(2,1)} %param.15) | copy-start | bytes 24580
  4.9 83.8 %all-to-all-start = ((bf16[32,320,128]{2,1,0:T(8,128)(2,1)}), bf16[32,320,128]{2,1,0:T(8,128)(2,1)}, u32[]{:S(2)}, u32[]{:S(2)}) async-start(bf16[32,320,128]{2,1,0:T(8,128)(2,1)} %pad_maximum_fusion), calls=%async_computation | async-start | bytes 5242880 | tf_op jit(solution)/shard_map/all_to_all | solution.py:152
  92.3 15.8 %copy-start.4 = (s32[64]{0:T(128)S(1)}, s32[64]{0:T(128)}, u32[]{:S(2)}) copy-start(s32[64]{0:T(128)} %param.21) | copy-start | bytes 772
  98.6 19.5 %all-to-all-start.2 = ((bf16[4,256,192]{1,2,0:T(8,128)(2,1)}), bf16[4,256,192]{1,2,0:T(8,128)(2,1)S(1)}, u32[]{:S(2)}, u32[]{:S(2)}) async-start(bf16[4,256,192]{1,2,0:T(8,128)(2,1)} %broadcast_in_dim.178), calls=%async_computation.2 | async-start | bytes 786432 | tf_op jit(solution)/shard_map/all_to_all | solution.py:84
  118.1 29.0 %all-to-all-start.1 = ((bf16[32,64,128]{2,1,0:T(8,128)(2,1)}), bf16[32,64,128]{2,1,0:T(8,128)(2,1)S(1)}, u32[]{:S(2)}, u32[]{:S(2)}) async-start(bf16[32,64,128]{2,1,0:T(8,128)(2,1)} %reshape.380), calls=%async_computation.1 | async-start | bytes 1048576 | tf_op jit(solution)/shard_map/all_to_all | solution.py:188
  151.0 10.5 %collective-permute-start = (bf16[1024,256]{1,0:T(8,128)(2,1)S(1)}, bf16[1024,256]{1,0:T(8,128)(2,1)S(1)}, u32[]{:S(2)}, u32[]{:S(2)}) collective-permute-start(bf16[1024,256]{1,0:T(8,128)(2,1)S(1)} %scatter_fusion), channel_id=1, source_target_pairs={{0,1},{1,2},{2,3},{3,4},{4,5},{5,6},{6,7},{7,8},{8,9},{9,10},{10,1... | collective-permute-start | bytes 1572872 | tf_op jit(solution)/shard_map/ppermute | solution.py:24
  187.2 57.9 %all-to-all-start.4 = ((bf16[32,256,128]{2,1,0:T(8,128)(2,1)}), bf16[32,256,128]{2,1,0:T(8,128)(2,1)S(1)}, u32[]{:S(2)}, u32[]{:S(2)}) async-start(bf16[32,256,128]{2,1,0:T(8,128)(2,1)} %convert_bitcast_fusion), calls=%async_computation.4 | async-start | bytes 4194304 | tf_op jit(solution)/shard_map/all_to_all | solution.py:259

commit v11 on v9

--- a/solution.py
+++ b/solution.py
@@ -149,13 +149,13 @@
         .transpose(2, 0, 1, 3)
         .reshape(blk_count, rows_each * 2, HEAD_DIM)
     )
-    arrived = lax.all_to_all(x_part, "blk", 0, 0, tiled=True)
-    wide = arrived.astype(jnp.float32)
-    arrived, w_part, c_part = lax.optimization_barrier((arrived, w_part, c_part))
     w_rows = w_part.shape[1]
-    moved = lax.all_to_all(jnp.concatenate([w_part, c_part], axis=1), "blk", 0, 0, tiled=True)
-    kv_cols = moved[:, :w_rows].reshape(blk_count, own_cols, pair_cols)
-    stored = moved[:, w_rows:].reshape(blk_count * rows_each, 2 * HEAD_DIM)
+    arrived = lax.all_to_all(
+        jnp.concatenate([x_part, w_part, c_part], axis=1), "blk", 0, 0, tiled=True
+    )
+    wide = arrived[:, :slots].astype(jnp.float32)
+    kv_cols = arrived[:, slots : slots + w_rows].reshape(blk_count, own_cols, pair_cols)
+    stored = arrived[:, slots + w_rows :].reshape(blk_count * rows_each, 2 * HEAD_DIM)
 
     gains = norm_gain.astype(jnp.float32).reshape(blk_count, 1, own_cols)
     scaled = (wide * gains).astype(jnp.bfloat16)

time: 246 us -> 250 us (1.016)
  waiting for transfers between devices: 111 us -> 143 us
  local copies, waits for them, and re-layouts: 28.8 us -> 12.8 us
  starting transfers between devices: 38.6 us -> 28.7 us
    all_to_all x2 -> x1, waiting for transfers between devices: 41.5 us -> 59.9 us  [local(): lax.all_to_all(jnp.concatenate([x_part, w_part, c_part], axis=1), 'blk',...]
    all_to_all x2 -> x1, starting transfers between devices: 27.4 us -> 16.1 us  [local(): lax.all_to_all(jnp.concatenate([x_part, w_part, c_part], axis=1), 'blk',...]
    all_to_all x1, waiting for transfers between devices: 56.7 us -> 67.1 us  [local(): lax.all_to_all(term.astype(jnp.bfloat16), 'blk', 0, 0, tiled=True)]
    reshape x3 -> x2, local copies, waits for them, and re-layouts: 5.57 us -> 1.57 us  [the longest x1 1.4 us: local(): arrived[:, slots:slots + w_rows].reshape(blk_count, own_cols, pair_cols)]
    all_to_all x1, waiting for transfers between devices: 6.56 us -> 9.43 us  [group_gather(): lax.all_to_all(spread, axis, 0, 0, axis_index_groups=groups, tiled=True)]
  transfers between devices with their start and end apart: 5 -> 4, of which waited for: 5 -> 4; matrix products, arithmetic and copies ran while one was open for 21% -> 13% of each run, Pallas kernels for 0% -> 0%
where the time goes in v11:
time: 250 us; the launch traced here: 249 us
  waiting for transfers between devices  143 us (57%)
  other arithmetic  33.4 us (13%)
  starting transfers between devices  28.7 us (11%)
  blocking collectives  19.9 us (8%)
  local copies, waits for them, and re-layouts  12.8 us (5%)
  matrix products  11.1 us (4%)
    all_to_all x1, waiting for transfers between devices, local(): lax.all_to_all(term.astype(jnp.bfloat16), 'blk', 0, 0, tiled=True)  67.1 us
    all_to_all x1, waiting for transfers between devices, local(): lax.all_to_all(jnp.concatenate([x_part, w_part, c_part], axis=1), 'blk',...  59.9 us
    all_to_all x1, blocking collectives, group_exchange(): lax.all_to_all(parts, axis, 0, 0, axis_index_groups=groups, tiled=True)  19.9 us
    all_to_all x1, starting transfers between devices, local(): lax.all_to_all(jnp.concatenate([x_part, w_part, c_part], axis=1), 'blk',...  16.1 us
    all_to_all x1, waiting for transfers between devices, group_gather(): lax.all_to_all(spread, axis, 0, 0, axis_index_groups=groups, tiled=True)  9.43 us
    select_n x3, other arithmetic, tenant_lookup(): span_ids = positions // SPAN  9.02 us
    ppermute x1, waiting for transfers between devices, shifted(): return lax.ppermute(shard, axis, pairs)  6.31 us
    all_to_all x1, starting transfers between devices, local(): lax.all_to_all(term.astype(jnp.bfloat16), 'blk', 0, 0, tiled=True)  5.34 us
  transfers between devices with their start and end apart: 4, of which 4 were waited for; matrix products, arithmetic and copies ran while one was open for 13% of the time, Pallas kernels for 0%

profile of v11, /device:TPU:26, one launch (start us, length us, event | category | flops | bytes accessed | tf_op | source)
XLA Modules:
  0.0 249.1 jit_solution(5811472070149277283)
XLA Ops:
  0.0 1.4 copy.95
  3.3 1.8 pad_maximum_fusion
  5.2 16.1 %all-to-all-start = ((bf16[32,384,128]{2,1,0:T(8,128)(2,1)}), bf16[32,384,128]{2,1,0:T(8,128)(2,1)}, u32[]{:S(2)}, u32[]{:S(2)}) async-start(bf16[32,384,128]{2,1,0:T(8,128)(2,1)} %pad_maximum_fusion), calls=%async_computation | async-start | bytes 6291456 | tf_op jit(solution)/shard_map/all_to_all | solution.py:153
  22.7 3.9 %and_select_fusion.8 = (s32[256]{0:T(256)S(1)}, s32[256]{0:T(256)S(1)}, s32[256]{0:T(256)S(1)}) fusion(s32[4096]{0:T(1024)} %param.22, s32[]{:T(128)S(6)} %select_n.158, s32[]{:T(128)S(6)} %mul.231, s32[]{:T(128)S(6)} %select_n.164, s32[]{:T(128)S(6)} %mul.233, s32[]{:T(128)} %bitcast.17, s32[]{:T(128)} %bitcast.16, s32[]{:T(128)} %bitcast.15, s32[]{:T(128)} %bitcast.14, ...), kind=kLoop, calls=%fused_computation.191 | loop fusion | flops 26112 | bytes 4132 | tf_op jit(solution)/shard_map/jit(floor_divide)/jit(_where)/select_n | solution.py:42
  27.6 2.6 %broadcast_compare_fusion.2 = pred[1024]{0:T(1024)(128)(4,1)S(1)} fusion(s32[]{:T(128)} %bitcast.4, s32[]{:T(128)} %bitcast.3, s32[]{:T(128)} %bitcast.2, s32[]{:T(128)} %bitcast.1, s32[]{:T(128)S(6)} %mul.236, s32[]{:T(128)S(6)} %mul.231), kind=kLoop, calls=%fused_computation.175 | loop fusion | flops 52224 | bytes 1048 | tf_op jit(solution)/shard_map/ge | solution.py:56
  30.9 2.5 %broadcast_compare_fusion.3 = pred[1024]{0:T(1024)(128)(4,1)S(1)} fusion(s32[]{:T(128)} %bitcast.38, s32[]{:T(128)} %bitcast.37, s32[]{:T(128)} %bitcast.36, s32[]{:T(128)} %bitcast.35, s32[]{:T(128)S(6)} %mul.236, s32[]{:T(128)S(6)} %mul.273, pred[]{:T(512)S(6)} %gt.3), kind=kLoop, calls=%fused_computation.176 | loop fusion | flops 53248 | bytes 1049 | tf_op jit(solution)/shard_map/ge | solution.py:56
  33.4 2.5 %fusion.105 = s32[1024]{0:T(1024)S(1)} fusion(s32[]{:T(128)} %bitcast.38, s32[]{:T(128)} %bitcast.37, s32[]{:T(128)} %bitcast.36, s32[]{:T(128)} %bitcast.35, s32[]{:T(128)S(6)} %mul.273, s32[]{:T(128)S(6)} %mul.236, pred[]{:T(512)S(6)} %gt.3), kind=kLoop, calls=%fused_computation.153 | loop fusion | flops 52224 | bytes 4121 | tf_op jit(solution)/shard_map/jit(_where)/select_n | solution.py:228
  35.9 2.5 %add_select_fusion = s32[1024]{0:T(1024)S(1)} fusion(s32[]{:T(128)} %bitcast.38, s32[]{:T(128)} %bitcast.37, s32[]{:T(128)} %bitcast.36, s32[]{:T(128)} %bitcast.35, s32[]{:T(128)S(6)} %mul.236, s32[]{:T(128)S(6)} %mul.273, pred[]{:T(512)S(6)} %gt.3), kind=kLoop, calls=%fused_computation.120 | loop fusion | flops 67584 | bytes 4121 | tf_op jit(solution)/shard_map/jit(floor_divide)/jit(_where)/select_n | solution.py:42
  38.5 2.6 %add_select_fusion.1 = s32[1024]{0:T(1024)S(1)} fusion(s32[]{:T(128)} %bitcast.4, s32[]{:T(128)} %bitcast.3, s32[]{:T(128)} %bitcast.2, s32[]{:T(128)} %bitcast.1, s32[]{:T(128)S(6)} %mul.236, s32[]{:T(128)S(6)} %mul.231), kind=kLoop, calls=%fused_computation.124 | loop fusion | flops 66560 | bytes 4120 | tf_op jit(solution)/shard_map/jit(floor_divide)/jit(_where)/select_n | solution.py:42
  41.0 2.6 %fusion.107 = s32[1024]{0:T(1024)S(1)} fusion(s32[]{:T(128)} %bitcast.4, s32[]{:T(128)} %bitcast.3, s32[]{:T(128)} %bitcast.2, s32[]{:T(128)} %bitcast.1, s32[]{:T(128)S(6)} %mul.236, s32[]{:T(128)S(6)} %mul.231), kind=kLoop, calls=%fused_computation.157 | loop fusion | flops 51200 | bytes 4120 | tf_op jit(solution)/shard_map/add | solution.py:100
  44.3 2.6 %select_convert_fusion.1 = f32[1024]{0:T(1024)S(1)} fusion(s32[]{:T(128)} %bitcast.13, s32[]{:T(128)} %bitcast.12, s32[]{:T(128)} %bitcast.11, s32[]{:T(128)} %bitcast.10, s32[]{:T(128)S(6)} %mul.236), kind=kLoop, calls=%fused_computation.154 | loop fusion | flops 45056 | bytes 4116 | tf_op jit(solution)/shard_map/convert_element_type | solution.py:30
  47.1 1.3 fusion.46
  48.4 59.9 %all-to-all-done = bf16[32,384,128]{2,1,0:T(8,128)(2,1)} async-done(((bf16[32,384,128]{2,1,0:T(8,128)(2,1)}), bf16[32,384,128]{2,1,0:T(8,128)(2,1)}, u32[]{:S(2)}, u32[]{:S(2)}) %all-to-all-start) | async-done | bytes 3145760 | tf_op jit(solution)/shard_map/all_to_all | solution.py:153
  108.4 2.1 fusion.1
  110.5 1.3 fusion.122
  111.7 1.4 reshape.381
  113.1 2.7 %fusion.33 = f32[256,1,128]{0,2,1:T(8,128)S(1)} fusion(bf16[32,128,128]{2,1,0:T(8,128)(2,1)} %bitcast.156, f32[32,128]{1,0:T(8,128)S(1)} %bitcast_convert_fusion, bf16[32,384,128]{2,1,0:T(8,128)(2,1)} %all-to-all-done, f32[256]{0:T(256)S(1)} %add_rsqrt_fusion), kind=kOutput, calls=%fused_computation.33 | convolution fusion | flops 271613952 | bytes 3294208 | tf_op jit(solution)/shard_map/ksc,kcd->sd/dot_general | solution.py:164
  116.2 2.3 fusion.39
  119.5 5.1 %all-to-all-start.1 = ((bf16[4,256,192]{1,2,0:T(8,128)(2,1)}), bf16[4,256,192]{1,2,0:T(8,128)(2,1)S(1)}, u32[]{:S(2)}, u32[]{:S(2)}) async-start(bf16[4,256,192]{1,2,0:T(8,128)(2,1)} %broadcast_in_dim.178), calls=%async_computation.1 | async-start | bytes 786432 | tf_op jit(solution)/shard_map/all_to_all | solution.py:84
  125.0 1.2 fusion.56
  126.8 9.4 %all-to-all-done.1 = bf16[4,256,192]{1,2,0:T(8,128)(2,1)S(1)} async-done(((bf16[4,256,192]{1,2,0:T(8,128)(2,1)}), bf16[4,256,192]{1,2,0:T(8,128)(2,1)S(1)}, u32[]{:S(2)}, u32[]{:S(2)}) %all-to-all-start.1) | async-done | bytes 393248 | tf_op jit(solution)/shard_map/all_to_all | solution.py:84
  136.4 1.8 scatter_fusion
  138.2 2.1 collective-permute-start
  141.3 1.1 fusion.4
  142.4 6.3 %collective-permute-done = bf16[1024,256]{1,0:T(8,128)(2,1)S(1)} collective-permute-done((bf16[1024,256]{1,0:T(8,128)(2,1)S(1)}, bf16[1024,256]{1,0:T(8,128)(2,1)S(1)}, u32[]{:S(2)}, u32[]{:S(2)}) %collective-permute-start) | collective-permute-done | bytes 524320 | tf_op jit(solution)/shard_map/ppermute | solution.py:24
  149.5 1.2 fusion.18
  150.7 1.0 fusion.6
  151.8 1.1 fusion.24
  153.0 19.9 %all_to_all.20 = f32[4,256,130]{1,2,0:T(8,128)S(1)} all-to-all(f32[4,256,130]{1,2,0:T(8,128)S(1)} %pad_maximum_fusion.1), channel_id=1, replica_groups={{0,16,32,48},{64,80,96,112},{128,144,160,176},{192,208,224,240},{256,27..., dimensions={0} | all-to-all | bytes 1064960 | tf_op jit(solution)/shard_map/all_to_all | solution.py:89
  173.0 2.1 convert_bitcast_fusion
  175.1 5.3 %all-to-all-start.3 = ((bf16[32,256,128]{2,1,0:T(8,128)(2,1)}), bf16[32,256,128]{2,1,0:T(8,128)(2,1)S(1)}, u32[]{:S(2)}, u32[]{:S(2)}) async-start(bf16[32,256,128]{2,1,0:T(8,128)(2,1)} %convert_bitcast_fusion), calls=%async_computation.3 | async-start | bytes 4194304 | tf_op jit(solution)/shard_map/all_to_all | solution.py:258
  181.0 67.1 %all-to-all-done.3 = bf16[32,256,128]{2,1,0:T(8,128)(2,1)S(1)} async-done(((bf16[32,256,128]{2,1,0:T(8,128)(2,1)}), bf16[32,256,128]{2,1,0:T(8,128)(2,1)S(1)}, u32[]{:S(2)}, u32[]{:S(2)}) %all-to-all-start.3) | async-done | bytes 2097184 | tf_op jit(solution)/shard_map/all_to_all | solution.py:258
  (74 shorter events, 11.7 us)
Async XLA Ops:
  0.0 173.0 %copy-start = (bf16[128,4096]{1,0:T(8,128)(2,1)S(1)}, bf16[128,4096]{1,0:T(8,128)(2,1)}, u32[]{:S(2)}) copy-start(bf16[128,4096]{1,0:T(8,128)(2,1)} %param.18) | copy-start | bytes 3145732
  0.0 2.5 %copy-start.2 = (bf16[128,8,256]{2,1,0:T(8,128)(2,1)S(1)}, bf16[128,8,256]{2,1,0:T(8,128)(2,1)}, u32[]{:S(2)}) copy-start(bf16[128,8,256]{2,1,0:T(8,128)(2,1)} %param.13) | copy-start | bytes 1572868
  0.0 2.8 %copy-start.3 = (bf16[256,128]{1,0:T(8,128)(2,1)S(1)}, bf16[256,128]{1,0:T(8,128)(2,1)}, u32[]{:S(2)}) copy-start(bf16[256,128]{1,0:T(8,128)(2,1)} %param.14) | copy-start | bytes 196612
  5.2 16.2 %copy-start.7 = (s32[16]{0:T(128)S(1)}, s32[16]{0:T(128)}, u32[]{:S(2)}) copy-start(s32[16]{0:T(128)} %param.23) | copy-start | bytes 196
  5.2 16.8 %copy-start.6 = (s32[64]{0:T(128)S(1)}, s32[64]{0:T(128)}, u32[]{:S(2)}) copy-start(s32[64]{0:T(128)} %param.20) | copy-start | bytes 772
  5.2 21.5 %copy-start.8 = (s32[64]{0:T(128)S(1)}, s32[64]{0:T(128)}, u32[]{:S(2)}) copy-start(s32[64]{0:T(128)} %param.19) | copy-start | bytes 772
  5.2 41.7 %copy-start.5 = (s32[64]{0:T(128)S(1)}, s32[64]{0:T(128)}, u32[]{:S(2)}) copy-start(s32[64]{0:T(128)} %param.21) | copy-start | bytes 772
  5.2 41.9 %copy-start.4 = (bf16[4096]{0:T(1024)(128)(2,1)S(1)}, bf16[4096]{0:T(1024)(128)(2,1)}, u32[]{:S(2)}) copy-start(bf16[4096]{0:T(1024)(128)(2,1)} %param.15) | copy-start | bytes 24580
  5.2 103.2 %all-to-all-start = ((bf16[32,384,128]{2,1,0:T(8,128)(2,1)}), bf16[32,384,128]{2,1,0:T(8,128)(2,1)}, u32[]{:S(2)}, u32[]{:S(2)}) async-start(bf16[32,384,128]{2,1,0:T(8,128)(2,1)} %pad_maximum_fusion), calls=%async_computation | async-start | bytes 6291456 | tf_op jit(solution)/shard_map/all_to_all | solution.py:153
  113.1 3.1 %copy-start.1 = (bf16[32,128,64]{2,1,0:T(8,128)(2,1)S(1)}, bf16[32,128,64]{2,1,0:T(8,128)(2,1)}, u32[]{:S(2)}) copy-start(bf16[32,128,64]{2,1,0:T(8,128)(2,1)} %reshape.381) | copy-start | bytes 1572868
  119.5 16.7 %all-to-all-start.1 = ((bf16[4,256,192]{1,2,0:T(8,128)(2,1)}), bf16[4,256,192]{1,2,0:T(8,128)(2,1)S(1)}, u32[]{:S(2)}, u32[]{:S(2)}) async-start(bf16[4,256,192]{1,2,0:T(8,128)(2,1)} %broadcast_in_dim.178), calls=%async_computation.1 | async-start | bytes 786432 | tf_op jit(solution)/shard_map/all_to_all | solution.py:84
  138.2 10.5 %collective-permute-start = (bf16[1024,256]{1,0:T(8,128)(2,1)S(1)}, bf16[1024,256]{1,0:T(8,128)(2,1)S(1)}, u32[]{:S(2)}, u32[]{:S(2)}) collective-permute-start(bf16[1024,256]{1,0:T(8,128)(2,1)S(1)} %scatter_fusion), channel_id=1, source_target_pairs={{0,1},{1,2},{2,3},{3,4},{4,5},{5,6},{6,7},{7,8},{8,9},{9,10},{10,1... | collective-permute-start | bytes 1572872 | tf_op jit(solution)/shard_map/ppermute | solution.py:24
  175.1 73.0 %all-to-all-start.3 = ((bf16[32,256,128]{2,1,0:T(8,128)(2,1)}), bf16[32,256,128]{2,1,0:T(8,128)(2,1)S(1)}, u32[]{:S(2)}, u32[]{:S(2)}) async-start(bf16[32,256,128]{2,1,0:T(8,128)(2,1)} %convert_bitcast_fusion), calls=%async_computation.3 | async-start | bytes 4194304 | tf_op jit(solution)/shard_map/all_to_all | solution.py:258

commit v12 on v9

--- a/solution.py
+++ b/solution.py
@@ -214,32 +214,20 @@
     )
     merged = stored.at[place].set(jnp.concatenate([fresh_keys, fresh_values], axis=1), mode="drop")
     query_tenant = tenant_lookup(query_pos, tenant_of_span)
-    own_part = attend_part(
+    prior = shifted(merged, "kv", 1)
+    prior_pos = joined_rows(span_order, jnp.maximum(kv_index - 1, 0), spans_here, stored_rows)
+    prior_pos = jnp.where(kv_index > 0, prior_pos, -1)
+    both = jnp.concatenate([merged, prior], axis=0)
+    both_pos = jnp.concatenate([key_pos, prior_pos], axis=0)
+    top, totals, summed = attend_part(
         queries,
         query_pos,
         query_tenant,
-        merged[:, :HEAD_DIM],
-        merged[:, HEAD_DIM:],
-        key_pos,
-        tenant_lookup(key_pos, tenant_of_span),
-    )
-    prior = shifted(merged, "kv", 1)
-    prior_pos = joined_rows(span_order, jnp.maximum(kv_index - 1, 0), spans_here, stored_rows)
-    prior_pos = jnp.where(kv_index > 0, prior_pos, -1)
-    prior_part = attend_part(
-        queries,
-        query_pos,
-        query_tenant,
-        prior[:, :HEAD_DIM],
-        prior[:, HEAD_DIM:],
-        prior_pos,
-        tenant_lookup(prior_pos, tenant_of_span),
-    )
-    top = jnp.maximum(own_part[0], prior_part[0])
-    scale_own = jnp.exp(own_part[0] - top)
-    scale_prior = jnp.exp(prior_part[0] - top)
-    totals = own_part[1] * scale_own + prior_part[1] * scale_prior
-    summed = own_part[2] * scale_own[..., None] + prior_part[2] * scale_prior[..., None]
+        both[:, :HEAD_DIM],
+        both[:, HEAD_DIM:],
+        both_pos,
+        tenant_lookup(both_pos, tenant_of_span),
+    )
     packed = jnp.concatenate([summed, top[..., None], totals[..., None]], axis=-1)
     gathered = group_exchange(packed, "blk", group_size)
     part_max = gathered[:, :, HEAD_DIM]

time: 246 us -> 247 us (level)
  waiting for transfers between devices: 111 us -> 125 us
  other arithmetic: 34.4 us -> 23 us
    all_to_all x1, waiting for transfers between devices: 23.9 us -> 34.1 us  [local(): arrived = lax.all_to_all(x_part, 'blk', 0, 0, tiled=True)]
    select_n x3 -> x2, other arithmetic: 8.8 us -> 3.83 us  [tenant_lookup(): span_ids = positions // SPAN]
    ge x2 -> x1, other arithmetic: 4.96 us -> 0.01 us  [attend_part(): key_pos[None, :] >= 0]
  transfers between devices with their start and end apart: 5 -> 5, of which waited for: 5 -> 5; matrix products, arithmetic and copies ran while one was open for 21% -> 15% of each run, Pallas kernels for 0% -> 0%
where the time goes in v12:
time: 247 us; the launch traced here: 246 us
  waiting for transfers between devices  125 us (51%)
  starting transfers between devices  38.6 us (16%)
  local copies, waits for them, and re-layouts  29.1 us (12%)
  other arithmetic  23 us (9%)
  blocking collectives  19.7 us (8%)
  matrix products  9.45 us (4%)
    all_to_all x1, waiting for transfers between devices, local(): lax.all_to_all(term.astype(jnp.bfloat16), 'blk', 0, 0, tiled=True)  57 us
    all_to_all x1, waiting for transfers between devices, local(): arrived = lax.all_to_all(x_part, 'blk', 0, 0, tiled=True)  34.1 us
    all_to_all x1, waiting for transfers between devices, local(): lax.all_to_all(jnp.concatenate([w_part, c_part], axis=1), 'blk', 0, 0, ti...  19.7 us
    all_to_all x1, blocking collectives, group_exchange(): lax.all_to_all(parts, axis, 0, 0, axis_index_groups=groups, tiled=True)  19.7 us
    all_to_all x1, starting transfers between devices, local(): arrived = lax.all_to_all(x_part, 'blk', 0, 0, tiled=True)  15.9 us
    all_to_all x1, starting transfers between devices, local(): lax.all_to_all(jnp.concatenate([w_part, c_part], axis=1), 'blk', 0, 0, ti...  11.5 us
    all_to_all x1, waiting for transfers between devices, group_gather(): lax.all_to_all(spread, axis, 0, 0, axis_index_groups=groups, tiled=True)  8.18 us
    ppermute x1, waiting for transfers between devices, shifted(): return lax.ppermute(shard, axis, pairs)  6.45 us
  transfers between devices with their start and end apart: 5, of which 5 were waited for; matrix products, arithmetic and copies ran while one was open for 15% of the time, Pallas kernels for 0%

profile of v12, /device:TPU:26, one launch (start us, length us, event | category | flops | bytes accessed | tf_op | source)
XLA Modules:
  0.0 245.8 jit_solution(15955411010823918322)
XLA Ops:
  0.0 2.8 %broadcast_in_dim.152 = bf16[32,256,128]{2,1,0:T(8,128)(2,1)} broadcast(bf16[256,128]{1,0:T(8,128)(2,1)} %param.14), dimensions={1,2} | broadcast | bytes 2162688 | tf_op jit(solution)/shard_map/broadcast_in_dim | solution.py:131
  2.8 15.9 %all-to-all-start = ((bf16[32,256,128]{2,1,0:T(8,128)(2,1)}), bf16[32,256,128]{2,1,0:T(8,128)(2,1)S(1)}, u32[]{:S(2)}, u32[]{:S(2)}) async-start(bf16[32,256,128]{2,1,0:T(8,128)(2,1)} %broadcast_in_dim.152), calls=%async_computation | async-start | bytes 4194304 | tf_op jit(solution)/shard_map/all_to_all | solution.py:152
  18.8 2.0 copy.111
  20.7 2.0 reshape.326
  22.7 2.0 copy.75
  27.6 2.4 copy.76
  29.9 2.5 reshape.324
  33.7 3.8 %and_select_fusion.8 = (s32[256]{0:T(256)S(1)}, s32[256]{0:T(256)S(1)}, s32[256]{0:T(256)S(1)}) fusion(s32[4096]{0:T(1024)} %param.22, s32[]{:T(128)S(6)} %select_n.152, s32[]{:T(128)S(6)} %mul.192, s32[]{:T(128)S(6)} %select_n.158, s32[]{:T(128)S(6)} %mul.194, s32[]{:T(128)} %bitcast.21, s32[]{:T(128)} %bitcast.20, s32[]{:T(128)} %bitcast.19, s32[]{:T(128)} %bitcast.18, ...), kind=kLoop, calls=%fused_computation.160 | loop fusion | flops 26112 | bytes 4132 | tf_op jit(solution)/shard_map/jit(floor_divide)/jit(_where)/select_n | solution.py:42
  38.3 2.4 fusion.81
  41.3 34.1 %all-to-all-done = bf16[32,256,128]{2,1,0:T(8,128)(2,1)S(1)} async-done(((bf16[32,256,128]{2,1,0:T(8,128)(2,1)}), bf16[32,256,128]{2,1,0:T(8,128)(2,1)S(1)}, u32[]{:S(2)}, u32[]{:S(2)}) %all-to-all-start) | async-done | bytes 2097184 | tf_op jit(solution)/shard_map/all_to_all | solution.py:152
  75.5 2.3 pad_maximum_fusion
  77.8 11.5 %all-to-all-start.1 = ((bf16[32,128,128]{2,1,0:T(8,128)(2,1)}), bf16[32,128,128]{2,1,0:T(8,128)(2,1)}, u32[]{:S(2)}, u32[]{:S(2)}) async-start(bf16[32,128,128]{2,1,0:T(8,128)(2,1)} %pad_maximum_fusion), calls=%async_computation.1 | async-start | bytes 2097152 | tf_op jit(solution)/shard_map/all_to_all | solution.py:156
  89.5 2.4 fusion.79
  92.6 2.4 select_convert_fusion.1
  95.8 2.0 fusion.21
  98.2 19.7 %all-to-all-done.1 = bf16[32,128,128]{2,1,0:T(8,128)(2,1)} async-done(((bf16[32,128,128]{2,1,0:T(8,128)(2,1)}), bf16[32,128,128]{2,1,0:T(8,128)(2,1)}, u32[]{:S(2)}, u32[]{:S(2)}) %all-to-all-start.1) | async-done | bytes 1048608 | tf_op jit(solution)/shard_map/all_to_all | solution.py:156
  117.9 2.3 fusion.91
  120.2 2.4 reshape.330
  122.5 1.9 fusion.27
  125.5 3.5 %all-to-all-start.2 = ((bf16[4,256,192]{1,2,0:T(8,128)(2,1)}), bf16[4,256,192]{1,2,0:T(8,128)(2,1)S(1)}, u32[]{:S(2)}, u32[]{:S(2)}) async-start(bf16[4,256,192]{1,2,0:T(8,128)(2,1)} %broadcast_in_dim.156), calls=%async_computation.2 | async-start | bytes 786432 | tf_op jit(solution)/shard_map/all_to_all | solution.py:84
  132.2 8.2 %all-to-all-done.2 = bf16[4,256,192]{1,2,0:T(8,128)(2,1)S(1)} async-done(((bf16[4,256,192]{1,2,0:T(8,128)(2,1)}), bf16[4,256,192]{1,2,0:T(8,128)(2,1)S(1)}, u32[]{:S(2)}, u32[]{:S(2)}) %all-to-all-start.2) | async-done | bytes 393248 | tf_op jit(solution)/shard_map/all_to_all | solution.py:84
  140.5 1.8 scatter_fusion
  142.3 2.1 collective-permute-start
  144.4 1.8 fusion.10
  146.5 6.4 %collective-permute-done = bf16[1024,256]{1,0:T(8,128)(2,1)} collective-permute-done((bf16[1024,256]{1,0:T(8,128)(2,1)S(1)}, bf16[1024,256]{1,0:T(8,128)(2,1)}, u32[]{:S(2)}, u32[]{:S(2)}) %collective-permute-start) | collective-permute-done | bytes 524320 | tf_op jit(solution)/shard_map/ppermute | solution.py:24
  154.0 1.5 fusion
  155.5 2.0 fusion.5
  157.4 2.1 fusion.1
  159.6 19.7 %all_to_all.25 = f32[4,256,130]{1,2,0:T(8,128)S(1)} all-to-all(f32[4,256,130]{1,2,0:T(8,128)S(1)} %pad_maximum_fusion.1), channel_id=1, replica_groups={{0,16,32,48},{64,80,96,112},{128,144,160,176},{192,208,224,240},{256,27..., dimensions={0} | all-to-all | bytes 1064960 | tf_op jit(solution)/shard_map/all_to_all | solution.py:89
  179.4 2.1 convert_bitcast_fusion
  181.5 5.6 %all-to-all-start.4 = ((bf16[32,256,128]{2,1,0:T(8,128)(2,1)}), bf16[32,256,128]{2,1,0:T(8,128)(2,1)S(1)}, u32[]{:S(2)}, u32[]{:S(2)}) async-start(bf16[32,256,128]{2,1,0:T(8,128)(2,1)} %convert_bitcast_fusion), calls=%async_computation.4 | async-start | bytes 4194304 | tf_op jit(solution)/shard_map/all_to_all | solution.py:246
  187.8 57.0 %all-to-all-done.4 = bf16[32,256,128]{2,1,0:T(8,128)(2,1)S(1)} async-done(((bf16[32,256,128]{2,1,0:T(8,128)(2,1)}), bf16[32,256,128]{2,1,0:T(8,128)(2,1)S(1)}, u32[]{:S(2)}, u32[]{:S(2)}) %all-to-all-start.4) | async-done | bytes 2097184 | tf_op jit(solution)/shard_map/all_to_all | solution.py:246
  (67 shorter events, 14.7 us)
Async XLA Ops:
  0.0 179.4 %copy-start = (bf16[128,4096]{1,0:T(8,128)(2,1)S(1)}, bf16[128,4096]{1,0:T(8,128)(2,1)}, u32[]{:S(2)}) copy-start(bf16[128,4096]{1,0:T(8,128)(2,1)} %param.18) | copy-start | bytes 3145732
  2.8 72.7 %all-to-all-start = ((bf16[32,256,128]{2,1,0:T(8,128)(2,1)}), bf16[32,256,128]{2,1,0:T(8,128)(2,1)S(1)}, u32[]{:S(2)}, u32[]{:S(2)}) async-start(bf16[32,256,128]{2,1,0:T(8,128)(2,1)} %broadcast_in_dim.152), calls=%async_computation | async-start | bytes 4194304 | tf_op jit(solution)/shard_map/all_to_all | solution.py:152
  18.7 13.7 %copy-start.4 = (s32[16]{0:T(128)S(1)}, s32[16]{0:T(128)}, u32[]{:S(2)}) copy-start(s32[16]{0:T(128)} %param.23) | copy-start | bytes 196
  18.7 14.3 %copy-start.3 = (s32[64]{0:T(128)S(1)}, s32[64]{0:T(128)}, u32[]{:S(2)}) copy-start(s32[64]{0:T(128)} %param.20) | copy-start | bytes 772
  26.7 62.6 %copy-start.5 = (s32[64]{0:T(128)S(1)}, s32[64]{0:T(128)}, u32[]{:S(2)}) copy-start(s32[64]{0:T(128)} %param.19) | copy-start | bytes 772
  26.7 68.3 %copy-start.2 = (s32[64]{0:T(128)S(1)}, s32[64]{0:T(128)}, u32[]{:S(2)}) copy-start(s32[64]{0:T(128)} %param.21) | copy-start | bytes 772
  26.7 68.6 %copy-start.1 = (bf16[4096]{0:T(1024)(128)(2,1)S(1)}, bf16[4096]{0:T(1024)(128)(2,1)}, u32[]{:S(2)}) copy-start(bf16[4096]{0:T(1024)(128)(2,1)} %param.15) | copy-start | bytes 24580
  77.8 40.1 %all-to-all-start.1 = ((bf16[32,128,128]{2,1,0:T(8,128)(2,1)}), bf16[32,128,128]{2,1,0:T(8,128)(2,1)}, u32[]{:S(2)}, u32[]{:S(2)}) async-start(bf16[32,128,128]{2,1,0:T(8,128)(2,1)} %pad_maximum_fusion), calls=%async_computation.1 | async-start | bytes 2097152 | tf_op jit(solution)/shard_map/all_to_all | solution.py:156
  125.5 14.9 %all-to-all-start.2 = ((bf16[4,256,192]{1,2,0:T(8,128)(2,1)}), bf16[4,256,192]{1,2,0:T(8,128)(2,1)S(1)}, u32[]{:S(2)}, u32[]{:S(2)}) async-start(bf16[4,256,192]{1,2,0:T(8,128)(2,1)} %broadcast_in_dim.156), calls=%async_computation.2 | async-start | bytes 786432 | tf_op jit(solution)/shard_map/all_to_all | solution.py:84
  142.3 10.6 %collective-permute-start = (bf16[1024,256]{1,0:T(8,128)(2,1)S(1)}, bf16[1024,256]{1,0:T(8,128)(2,1)}, u32[]{:S(2)}, u32[]{:S(2)}) collective-permute-start(bf16[1024,256]{1,0:T(8,128)(2,1)S(1)} %scatter_fusion), channel_id=1, source_target_pairs={{0,1},{1,2},{2,3},{3,4},{4,5},{5,6},{6,7},{7,8},{8,9},{9,10},{10,1... | collective-permute-start | bytes 1572872 | tf_op jit(solution)/shard_map/ppermute | solution.py:24
  181.5 63.2 %all-to-all-start.4 = ((bf16[32,256,128]{2,1,0:T(8,128)(2,1)}), bf16[32,256,128]{2,1,0:T(8,128)(2,1)S(1)}, u32[]{:S(2)}, u32[]{:S(2)}) async-start(bf16[32,256,128]{2,1,0:T(8,128)(2,1)} %convert_bitcast_fusion), calls=%async_computation.4 | async-start | bytes 4194304 | tf_op jit(solution)/shard_map/all_to_all | solution.py:246

commit v13 on v9

--- a/solution.py
+++ b/solution.py
@@ -138,11 +138,13 @@
         second = HEAD_DIM // 2 + m * quarter
         sorted_w.append(groups_w[:, :, second : second + quarter])
     sorted_w.append(groups_w[:, :, HEAD_DIM:])
+    half_rows = own_cols // 2
+    parity = kv_index % 2
     w_part = (
-        jnp.concatenate(sorted_w, axis=2)
-        .reshape(own_cols, blk_count, pair_cols)
+        lax.dynamic_slice_in_dim(jnp.concatenate(sorted_w, axis=2), parity * half_rows, half_rows, 0)
+        .reshape(half_rows, blk_count, pair_cols)
         .transpose(1, 0, 2)
-        .reshape(blk_count, own_cols * pair_cols // HEAD_DIM, HEAD_DIM)
+        .reshape(blk_count, half_rows * pair_cols // HEAD_DIM, HEAD_DIM)
     )
     c_part = (
         cache_entries.reshape(group_size, rows_each, KVH, 2 * HEAD_DIM)
@@ -154,7 +156,12 @@
     arrived, w_part, c_part = lax.optimization_barrier((arrived, w_part, c_part))
     w_rows = w_part.shape[1]
     moved = lax.all_to_all(jnp.concatenate([w_part, c_part], axis=1), "blk", 0, 0, tiled=True)
-    kv_cols = moved[:, :w_rows].reshape(blk_count, own_cols, pair_cols)
+    mine = moved[:, :w_rows].reshape(blk_count, half_rows, pair_cols)
+    kv_devices = lax.axis_size("kv")
+    other = lax.ppermute(mine, "kv", [(i, i ^ 1) for i in range(kv_devices)])
+    low_half = jnp.where(parity == 0, mine, other)
+    high_half = jnp.where(parity == 0, other, mine)
+    kv_cols = jnp.concatenate([low_half, high_half], axis=1)
     stored = moved[:, w_rows:].reshape(blk_count * rows_each, 2 * HEAD_DIM)
 
     gains = norm_gain.astype(jnp.float32).reshape(blk_count, 1, own_cols)

time: 246 us -> 247 us (level)
  the two profiles are of different devices: /device:TPU:26 before, /device:TPU:42 now
where the time goes in v13:
time: 247 us; the launch traced here: 246 us
  waiting for transfers between devices  109 us (44%)
  starting transfers between devices  41 us (17%)
  other arithmetic  35.3 us (14%)
  local copies, waits for them, and re-layouts  33.1 us (13%)
  blocking collectives  18.5 us (7%)
  matrix products  8.8 us (4%)
    all_to_all x1, waiting for transfers between devices, local(): lax.all_to_all(term.astype(jnp.bfloat16), 'blk', 0, 0, tiled=True)  54.5 us
    all_to_all x1, waiting for transfers between devices, local(): arrived = lax.all_to_all(x_part, 'blk', 0, 0, tiled=True)  24.7 us
    all_to_all x1, blocking collectives, group_exchange(): lax.all_to_all(parts, axis, 0, 0, axis_index_groups=groups, tiled=True)  18.5 us
    all_to_all x1, starting transfers between devices, local(): arrived = lax.all_to_all(x_part, 'blk', 0, 0, tiled=True)  15.7 us
    all_to_all x1, waiting for transfers between devices, local(): lax.all_to_all(jnp.concatenate([w_part, c_part], axis=1), 'blk', 0, 0, ti...  13.5 us
    all_to_all x1, starting transfers between devices, local(): lax.all_to_all(jnp.concatenate([w_part, c_part], axis=1), 'blk', 0, 0, ti...  9.74 us
    all_to_all x1, waiting for transfers between devices, group_gather(): lax.all_to_all(spread, axis, 0, 0, axis_index_groups=groups, tiled=True)  9.72 us
    select_n x3, other arithmetic, tenant_lookup(): span_ids = positions // SPAN  8.99 us
  transfers between devices with their start and end apart: 6, of which 5 were waited for; matrix products, arithmetic and copies ran while one was open for 22% of the time, Pallas kernels for 0%

profile of v13, /device:TPU:42, one launch (start us, length us, event | category | flops | bytes accessed | tf_op | source)
XLA Modules:
  0.0 245.8 jit_solution(147377745300094830)
XLA Ops:
  0.0 2.8 %broadcast_in_dim.174 = bf16[32,256,128]{2,1,0:T(8,128)(2,1)} broadcast(bf16[256,128]{1,0:T(8,128)(2,1)} %param.14), dimensions={1,2} | broadcast | bytes 2162688 | tf_op jit(solution)/shard_map/broadcast_in_dim | solution.py:131
  2.8 15.7 %all-to-all-start = ((bf16[32,256,128]{2,1,0:T(8,128)(2,1)}), bf16[32,256,128]{2,1,0:T(8,128)(2,1)S(1)}, u32[]{:S(2)}, u32[]{:S(2)}) async-start(bf16[32,256,128]{2,1,0:T(8,128)(2,1)} %broadcast_in_dim.174), calls=%async_computation | async-start | bytes 4194304 | tf_op jit(solution)/shard_map/all_to_all | solution.py:154
  25.4 2.1 copy.112
  28.8 2.0 copy.113
  30.7 2.0 reshape.377
  34.1 3.9 %and_select_fusion.8 = (s32[256]{0:T(256)S(1)}, s32[256]{0:T(256)S(1)}, s32[256]{0:T(256)S(1)}) fusion(s32[4096]{0:T(1024)} %param.22, s32[]{:T(128)S(6)} %select_n.177, s32[]{:T(128)S(6)} %mul.234, s32[]{:T(128)S(6)} %select_n.183, s32[]{:T(128)S(6)} %mul.236, s32[]{:T(128)} %bitcast.15, s32[]{:T(128)} %bitcast.14, s32[]{:T(128)} %bitcast.13, s32[]{:T(128)} %bitcast.12, ...), kind=kLoop, calls=%fused_computation.202 | loop fusion | flops 26112 | bytes 4132 | tf_op jit(solution)/shard_map/jit(floor_divide)/jit(_where)/select_n | solution.py:42
  39.0 2.5 %broadcast_compare_fusion.3 = pred[1024]{0:T(1024)(128)(4,1)S(1)} fusion(s32[]{:T(128)} %bitcast.36, s32[]{:T(128)} %bitcast.35, s32[]{:T(128)} %bitcast.34, s32[]{:T(128)} %bitcast.33, s32[]{:T(128)S(6)} %mul.239, s32[]{:T(128)S(6)} %mul.277, pred[]{:T(512)S(6)} %gt.3), kind=kLoop, calls=%fused_computation.187 | loop fusion | flops 53248 | bytes 1049 | tf_op jit(solution)/shard_map/ge | solution.py:56
  41.5 2.5 %fusion.111 = s32[1024]{0:T(1024)S(1)} fusion(s32[]{:T(128)} %bitcast.36, s32[]{:T(128)} %bitcast.35, s32[]{:T(128)} %bitcast.34, s32[]{:T(128)} %bitcast.33, s32[]{:T(128)S(6)} %mul.277, s32[]{:T(128)S(6)} %mul.239, pred[]{:T(512)S(6)} %gt.3), kind=kLoop, calls=%fused_computation.164 | loop fusion | flops 52224 | bytes 4121 | tf_op jit(solution)/shard_map/jit(_where)/select_n | solution.py:235
  44.0 2.5 %add_select_fusion = s32[1024]{0:T(1024)S(1)} fusion(s32[]{:T(128)} %bitcast.36, s32[]{:T(128)} %bitcast.35, s32[]{:T(128)} %bitcast.34, s32[]{:T(128)} %bitcast.33, s32[]{:T(128)S(6)} %mul.239, s32[]{:T(128)S(6)} %mul.277, pred[]{:T(512)S(6)} %gt.3), kind=kLoop, calls=%fused_computation.131 | loop fusion | flops 67584 | bytes 4121 | tf_op jit(solution)/shard_map/jit(floor_divide)/jit(_where)/select_n | solution.py:42
  47.2 2.5 %add_select_fusion.1 = s32[1024]{0:T(1024)S(1)} fusion(s32[]{:T(128)} %bitcast.4, s32[]{:T(128)} %bitcast.3, s32[]{:T(128)} %bitcast.2, s32[]{:T(128)} %bitcast.1, s32[]{:T(128)S(6)} %mul.239, s32[]{:T(128)S(6)} %mul.234), kind=kLoop, calls=%fused_computation.135 | loop fusion | flops 66560 | bytes 4120 | tf_op jit(solution)/shard_map/jit(floor_divide)/jit(_where)/select_n | solution.py:42
  49.8 2.5 %fusion.113 = s32[1024]{0:T(1024)S(1)} fusion(s32[]{:T(128)} %bitcast.4, s32[]{:T(128)} %bitcast.3, s32[]{:T(128)} %bitcast.2, s32[]{:T(128)} %bitcast.1, s32[]{:T(128)S(6)} %mul.239, s32[]{:T(128)S(6)} %mul.234), kind=kLoop, calls=%fused_computation.168 | loop fusion | flops 51200 | bytes 4120 | tf_op jit(solution)/shard_map/add | solution.py:100
  52.3 24.7 %all-to-all-done = bf16[32,256,128]{2,1,0:T(8,128)(2,1)S(1)} async-done(((bf16[32,256,128]{2,1,0:T(8,128)(2,1)}), bf16[32,256,128]{2,1,0:T(8,128)(2,1)S(1)}, u32[]{:S(2)}, u32[]{:S(2)}) %all-to-all-start) | async-done | bytes 2097184 | tf_op jit(solution)/shard_map/all_to_all | solution.py:154
  77.0 2.0 pad_maximum_fusion
  79.0 9.7 %all-to-all-start.1 = ((bf16[32,96,128]{2,1,0:T(8,128)(2,1)}), bf16[32,96,128]{2,1,0:T(8,128)(2,1)}, u32[]{:S(2)}, u32[]{:S(2)}) async-start(bf16[32,96,128]{2,1,0:T(8,128)(2,1)} %pad_maximum_fusion), calls=%async_computation.1 | async-start | bytes 1572864 | tf_op jit(solution)/shard_map/all_to_all | solution.py:158
  88.7 2.5 %broadcast_compare_fusion.2 = pred[1024]{0:T(1024)(128)(4,1)S(1)} fusion(s32[]{:T(128)} %bitcast.4, s32[]{:T(128)} %bitcast.3, s32[]{:T(128)} %bitcast.2, s32[]{:T(128)} %bitcast.1, s32[]{:T(128)S(6)} %mul.239, s32[]{:T(128)S(6)} %mul.234), kind=kLoop, calls=%fused_computation.186 | loop fusion | flops 52224 | bytes 1048 | tf_op jit(solution)/shard_map/ge | solution.py:56
  91.9 2.5 %select_convert_fusion.1 = f32[1024]{0:T(1024)S(1)} fusion(s32[]{:T(128)} %bitcast.11, s32[]{:T(128)} %bitcast.10, s32[]{:T(128)} %bitcast.9, s32[]{:T(128)} %bitcast.8, s32[]{:T(128)S(6)} %mul.239), kind=kLoop, calls=%fused_computation.165 | loop fusion | flops 45056 | bytes 4116 | tf_op jit(solution)/shard_map/convert_element_type | solution.py:30
  94.8 2.2 fusion.46
  97.5 13.5 %all-to-all-done.1 = bf16[32,96,128]{2,1,0:T(8,128)(2,1)} async-done(((bf16[32,96,128]{2,1,0:T(8,128)(2,1)}), bf16[32,96,128]{2,1,0:T(8,128)(2,1)}, u32[]{:S(2)}, u32[]{:S(2)}) %all-to-all-start.1) | async-done | bytes 786464 | tf_op jit(solution)/shard_map/all_to_all | solution.py:158
  112.7 2.0 reshape.381
  114.7 2.0 copy.119
  116.8 1.9 collective-permute-start
  118.7 2.0 fusion.33
  121.0 1.9 slice.157
  122.9 2.0 reshape.378
  128.0 3.5 %all-to-all-start.2 = ((bf16[4,256,192]{1,2,0:T(8,128)(2,1)}), bf16[4,256,192]{1,2,0:T(8,128)(2,1)S(1)}, u32[]{:S(2)}, u32[]{:S(2)}) async-start(bf16[4,256,192]{1,2,0:T(8,128)(2,1)} %broadcast_in_dim.178), calls=%async_computation.2 | async-start | bytes 786432 | tf_op jit(solution)/shard_map/all_to_all | solution.py:84
  134.5 9.7 %all-to-all-done.2 = bf16[4,256,192]{1,2,0:T(8,128)(2,1)S(1)} async-done(((bf16[4,256,192]{1,2,0:T(8,128)(2,1)}), bf16[4,256,192]{1,2,0:T(8,128)(2,1)S(1)}, u32[]{:S(2)}, u32[]{:S(2)}) %all-to-all-start.2) | async-done | bytes 393248 | tf_op jit(solution)/shard_map/all_to_all | solution.py:84
  146.2 2.1 collective-permute-start.1
  150.4 6.3 %collective-permute-done.1 = bf16[1024,256]{1,0:T(8,128)(2,1)S(1)} collective-permute-done((bf16[1024,256]{1,0:T(8,128)(2,1)S(1)}, bf16[1024,256]{1,0:T(8,128)(2,1)S(1)}, u32[]{:S(2)}, u32[]{:S(2)}) %collective-permute-start.1) | collective-permute-done | bytes 524320 | tf_op jit(solution)/shard_map/ppermute | solution.py:24
  161.0 18.5 %all_to_all.25 = f32[4,256,130]{1,2,0:T(8,128)S(1)} all-to-all(f32[4,256,130]{1,2,0:T(8,128)S(1)} %pad_maximum_fusion.1), channel_id=1, replica_groups={{0,16,32,48},{64,80,96,112},{128,144,160,176},{192,208,224,240},{256,27..., dimensions={0} | all-to-all | bytes 1064960 | tf_op jit(solution)/shard_map/all_to_all | solution.py:89
  179.5 2.1 convert_bitcast_fusion
  181.6 8.0 %all-to-all-start.4 = ((bf16[32,256,128]{2,1,0:T(8,128)(2,1)}), bf16[32,256,128]{2,1,0:T(8,128)(2,1)S(1)}, u32[]{:S(2)}, u32[]{:S(2)}) async-start(bf16[32,256,128]{2,1,0:T(8,128)(2,1)} %convert_bitcast_fusion), calls=%async_computation.4 | async-start | bytes 4194304 | tf_op jit(solution)/shard_map/all_to_all | solution.py:265
  190.3 54.5 %all-to-all-done.4 = bf16[32,256,128]{2,1,0:T(8,128)(2,1)S(1)} async-done(((bf16[32,256,128]{2,1,0:T(8,128)(2,1)}), bf16[32,256,128]{2,1,0:T(8,128)(2,1)S(1)}, u32[]{:S(2)}, u32[]{:S(2)}) %all-to-all-start.4) | async-done | bytes 2097184 | tf_op jit(solution)/shard_map/all_to_all | solution.py:265
  (80 shorter events, 30.4 us)
Async XLA Ops:
  0.0 179.5 %copy-start = (bf16[128,4096]{1,0:T(8,128)(2,1)S(1)}, bf16[128,4096]{1,0:T(8,128)(2,1)}, u32[]{:S(2)}) copy-start(bf16[128,4096]{1,0:T(8,128)(2,1)} %param.18) | copy-start | bytes 3145732
  2.8 74.2 %all-to-all-start = ((bf16[32,256,128]{2,1,0:T(8,128)(2,1)}), bf16[32,256,128]{2,1,0:T(8,128)(2,1)S(1)}, u32[]{:S(2)}, u32[]{:S(2)}) async-start(bf16[32,256,128]{2,1,0:T(8,128)(2,1)} %broadcast_in_dim.174), calls=%async_computation | async-start | bytes 4194304 | tf_op jit(solution)/shard_map/all_to_all | solution.py:154
  19.7 0.8 copy-start.1
  21.6 11.2 %copy-start.6 = (s32[16]{0:T(128)S(1)}, s32[16]{0:T(128)}, u32[]{:S(2)}) copy-start(s32[16]{0:T(128)} %param.23) | copy-start | bytes 196
  21.6 11.8 %copy-start.5 = (s32[64]{0:T(128)S(1)}, s32[64]{0:T(128)}, u32[]{:S(2)}) copy-start(s32[64]{0:T(128)} %param.20) | copy-start | bytes 772
  21.6 16.4 %copy-start.7 = (s32[64]{0:T(128)S(1)}, s32[64]{0:T(128)}, u32[]{:S(2)}) copy-start(s32[64]{0:T(128)} %param.19) | copy-start | bytes 772
  24.3 70.2 %copy-start.4 = (s32[64]{0:T(128)S(1)}, s32[64]{0:T(128)}, u32[]{:S(2)}) copy-start(s32[64]{0:T(128)} %param.21) | copy-start | bytes 772
  24.3 70.4 %copy-start.3 = (bf16[4096]{0:T(1024)(128)(2,1)S(1)}, bf16[4096]{0:T(1024)(128)(2,1)}, u32[]{:S(2)}) copy-start(bf16[4096]{0:T(1024)(128)(2,1)} %param.15) | copy-start | bytes 24580
  79.0 32.0 %all-to-all-start.1 = ((bf16[32,96,128]{2,1,0:T(8,128)(2,1)}), bf16[32,96,128]{2,1,0:T(8,128)(2,1)}, u32[]{:S(2)}, u32[]{:S(2)}) async-start(bf16[32,96,128]{2,1,0:T(8,128)(2,1)} %pad_maximum_fusion), calls=%async_computation.1 | async-start | bytes 1572864 | tf_op jit(solution)/shard_map/all_to_all | solution.py:158
  116.8 8.2 %collective-permute-start = (bf16[32,64,64]{1,2,0:T(8,128)(2,1)}, bf16[32,64,64]{1,2,0:T(8,128)(2,1)}, u32[]{:S(2)}, u32[]{:S(2)}) collective-permute-start(bf16[32,64,64]{1,2,0:T(8,128)(2,1)} %copy.119), channel_id=1, source_target_pairs={{0,1},{1,0},{2,3},{3,2},{4,5},{5,4},{6,7},{7,6},{8,9},{9,8},{10,11... | collective-permute-start | bytes 786440 | tf_op jit(solution)/shard_map/ppermute | solution.py:161
  128.0 16.2 %all-to-all-start.2 = ((bf16[4,256,192]{1,2,0:T(8,128)(2,1)}), bf16[4,256,192]{1,2,0:T(8,128)(2,1)S(1)}, u32[]{:S(2)}, u32[]{:S(2)}) async-start(bf16[4,256,192]{1,2,0:T(8,128)(2,1)} %broadcast_in_dim.178), calls=%async_computation.2 | async-start | bytes 786432 | tf_op jit(solution)/shard_map/all_to_all | solution.py:84
  132.5 16.0 %copy-start.2 = (pred[256,1024]{0,1:T(8,128)(4,1)S(1)}, pred[256,1024]{0,1:T(8,128)(4,1)}, u32[]{:S(2)}) copy-start(pred[256,1024]{0,1:T(8,128)(4,1)} %get-tuple-element.37) | copy-start | bytes 786436
  146.2 10.5 %collective-permute-start.1 = (bf16[1024,256]{1,0:T(8,128)(2,1)S(1)}, bf16[1024,256]{1,0:T(8,128)(2,1)S(1)}, u32[]{:S(2)}, u32[]{:S(2)}) collective-permute-start(bf16[1024,256]{1,0:T(8,128)(2,1)S(1)} %scatter_fusion), channel_id=1, source_target_pairs={{0,1},{1,2},{2,3},{3,4},{4,5},{5,6},{6,7},{7,8},{8,9},{9,10},{10,1... | collective-permute-start | bytes 1572872 | tf_op jit(solution)/shard_map/ppermute | solution.py:24
  181.6 63.1 %all-to-all-start.4 = ((bf16[32,256,128]{2,1,0:T(8,128)(2,1)}), bf16[32,256,128]{2,1,0:T(8,128)(2,1)S(1)}, u32[]{:S(2)}, u32[]{:S(2)}) async-start(bf16[32,256,128]{2,1,0:T(8,128)(2,1)} %convert_bitcast_fusion), calls=%async_computation.4 | async-start | bytes 4194304 | tf_op jit(solution)/shard_map/all_to_all | solution.py:265

commit v14 on v8

--- a/solution.py
+++ b/solution.py
@@ -246,15 +246,16 @@
     scale_prior = jnp.exp(prior_part[0] - top)
     totals = own_part[1] * scale_own + prior_part[1] * scale_prior
     summed = own_part[2] * scale_own[..., None] + prior_part[2] * scale_prior[..., None]
-    top_hi, top_lo = split_wide(top)
+    top_hi = top.astype(jnp.bfloat16)
+    top_mid, top_lo = split_wide(top - top_hi.astype(jnp.float32))
     total_hi, total_lo = split_wide(totals)
+    pieces = (top_hi, top_mid, top_lo, total_hi, total_lo)
     packed = jnp.concatenate(
-        [summed.astype(jnp.bfloat16)] + [v[..., None] for v in (top_hi, top_lo, total_hi, total_lo)],
-        axis=-1,
+        [summed.astype(jnp.bfloat16)] + [v[..., None] for v in pieces], axis=-1
     )
     gathered = group_exchange(packed, "blk", group_size).astype(jnp.float32)
-    part_max = gathered[:, :, HEAD_DIM] + gathered[:, :, HEAD_DIM + 1]
-    part_total = gathered[:, :, HEAD_DIM + 2] + gathered[:, :, HEAD_DIM + 3]
+    part_max = gathered[:, :, HEAD_DIM] + (gathered[:, :, HEAD_DIM + 1] + gathered[:, :, HEAD_DIM + 2])
+    part_total = gathered[:, :, HEAD_DIM + 3] + gathered[:, :, HEAD_DIM + 4]
     best = jnp.max(part_max, axis=0)
     weight = jnp.exp(part_max - best[None])
     total = jnp.sum(part_total * weight, axis=0)

time: 236 us -> 236 us (level)
  transfers between devices with their start and end apart: 5 -> 5, of which waited for: 5 -> 5; matrix products, arithmetic and copies ran while one was open for 21% -> 22% of each run, Pallas kernels for 0% -> 0%
where the time goes in v14:
time: 236 us; the launch traced here: 235 us
  waiting for transfers between devices  110 us (47%)
  starting transfers between devices  37.6 us (16%)
  other arithmetic  34.8 us (15%)
  local copies, waits for them, and re-layouts  29 us (12%)
  blocking collectives  13.3 us (6%)
  matrix products  9.97 us (4%)
    all_to_all x1, waiting for transfers between devices, local(): lax.all_to_all(term.astype(jnp.bfloat16), 'blk', 0, 0, tiled=True)  53.7 us
    all_to_all x1, waiting for transfers between devices, local(): arrived = lax.all_to_all(x_part, 'blk', 0, 0, tiled=True)  27.5 us
    all_to_all x1, waiting for transfers between devices, local(): lax.all_to_all(jnp.concatenate([w_part, c_part], axis=1), 'blk', 0, 0, ti...  16 us
    all_to_all x1, starting transfers between devices, local(): arrived = lax.all_to_all(x_part, 'blk', 0, 0, tiled=True)  15.8 us
    all_to_all x1, blocking collectives, group_exchange(): lax.all_to_all(parts, axis, 0, 0, axis_index_groups=groups, tiled=True)  13.3 us
    select_n x3, other arithmetic, tenant_lookup(): span_ids = positions // SPAN  8.99 us
    all_to_all x1, starting transfers between devices, local(): lax.all_to_all(term.astype(jnp.bfloat16), 'blk', 0, 0, tiled=True)  8.73 us
    all_to_all x1, starting transfers between devices, local(): lax.all_to_all(jnp.concatenate([w_part, c_part], axis=1), 'blk', 0, 0, ti...  7.43 us
  transfers between devices with their start and end apart: 5, of which 5 were waited for; matrix products, arithmetic and copies ran while one was open for 22% of the time, Pallas kernels for 0%

profile of v14, /device:TPU:34, one launch (start us, length us, event | category | flops | bytes accessed | tf_op | source)
XLA Modules:
  0.0 234.7 jit_solution(14689680994531186764)
XLA Ops:
  0.0 2.8 %broadcast_in_dim.177 = bf16[32,256,128]{2,1,0:T(8,128)(2,1)} broadcast(bf16[256,128]{1,0:T(8,128)(2,1)} %param.14), dimensions={1,2} | broadcast | bytes 2162688 | tf_op jit(solution)/shard_map/broadcast_in_dim | solution.py:137
  2.8 15.8 %all-to-all-start = ((bf16[32,256,128]{2,1,0:T(8,128)(2,1)}), bf16[32,256,128]{2,1,0:T(8,128)(2,1)S(1)}, u32[]{:S(2)}, u32[]{:S(2)}) async-start(bf16[32,256,128]{2,1,0:T(8,128)(2,1)} %broadcast_in_dim.177), calls=%async_computation | async-start | bytes 4194304 | tf_op jit(solution)/shard_map/all_to_all | solution.py:158
  18.7 2.1 copy.108
  23.5 2.4 %copy.109 = bf16[32,128,64]{2,1,0:T(8,128)(2,1)} copy(bf16[32,128,64]{1,2,0:T(8,128)(2,1)} %bitcast.191) | data formatting | bytes 1048576 | tf_op jit(solution)/shard_map/transpose | solution.py:150
  25.9 2.4 %reshape.443 = bf16[32,64,128]{2,1,0:T(8,128)(2,1)} reshape(bf16[32,128,64]{2,1,0:T(8,128)(2,1)} %copy.109) | data formatting | bytes 1048576 | tf_op jit(solution)/shard_map/reshape | solution.py:151
  28.3 2.0 copy.162
  30.3 2.0 reshape.445
  33.6 3.9 %and_select_fusion.8 = (s32[256]{0:T(256)S(1)}, s32[256]{0:T(256)S(1)}, s32[256]{0:T(256)S(1)}) fusion(s32[4096]{0:T(1024)} %param.22, s32[]{:T(128)S(6)} %select_n.158, s32[]{:T(128)S(6)} %mul.239, s32[]{:T(128)S(6)} %select_n.164, s32[]{:T(128)S(6)} %mul.241, s32[]{:T(128)} %bitcast.17, s32[]{:T(128)} %bitcast.16, s32[]{:T(128)} %bitcast.15, s32[]{:T(128)} %bitcast.14, ...), kind=kLoop, calls=%fused_computation.205 | loop fusion | flops 26112 | bytes 4132 | tf_op jit(solution)/shard_map/jit(floor_divide)/jit(_where)/select_n | solution.py:42
  38.5 2.5 %broadcast_compare_fusion.3 = pred[1024]{0:T(1024)(128)(4,1)S(1)} fusion(s32[]{:T(128)} %bitcast.38, s32[]{:T(128)} %bitcast.37, s32[]{:T(128)} %bitcast.36, s32[]{:T(128)} %bitcast.35, s32[]{:T(128)S(6)} %mul.244, s32[]{:T(128)S(6)} %mul.281, pred[]{:T(512)S(6)} %gt.3), kind=kLoop, calls=%fused_computation.190 | loop fusion | flops 53248 | bytes 1049 | tf_op jit(solution)/shard_map/ge | solution.py:56
  41.1 2.5 %fusion.112 = s32[1024]{0:T(1024)S(1)} fusion(s32[]{:T(128)} %bitcast.38, s32[]{:T(128)} %bitcast.37, s32[]{:T(128)} %bitcast.36, s32[]{:T(128)} %bitcast.35, s32[]{:T(128)S(6)} %mul.281, s32[]{:T(128)S(6)} %mul.244, pred[]{:T(512)S(6)} %gt.3), kind=kLoop, calls=%fused_computation.165 | loop fusion | flops 52224 | bytes 4121 | tf_op jit(solution)/shard_map/jit(_where)/select_n | solution.py:234
  43.6 2.5 %add_select_fusion = s32[1024]{0:T(1024)S(1)} fusion(s32[]{:T(128)} %bitcast.38, s32[]{:T(128)} %bitcast.37, s32[]{:T(128)} %bitcast.36, s32[]{:T(128)} %bitcast.35, s32[]{:T(128)S(6)} %mul.244, s32[]{:T(128)S(6)} %mul.281, pred[]{:T(512)S(6)} %gt.3), kind=kLoop, calls=%fused_computation.121 | loop fusion | flops 67584 | bytes 4121 | tf_op jit(solution)/shard_map/jit(floor_divide)/jit(_where)/select_n | solution.py:42
  46.8 2.5 %add_select_fusion.1 = s32[1024]{0:T(1024)S(1)} fusion(s32[]{:T(128)} %bitcast.4, s32[]{:T(128)} %bitcast.3, s32[]{:T(128)} %bitcast.2, s32[]{:T(128)} %bitcast.1, s32[]{:T(128)S(6)} %mul.244, s32[]{:T(128)S(6)} %mul.239), kind=kLoop, calls=%fused_computation.125 | loop fusion | flops 66560 | bytes 4120 | tf_op jit(solution)/shard_map/jit(floor_divide)/jit(_where)/select_n | solution.py:42
  49.3 2.5 %fusion.114 = s32[1024]{0:T(1024)S(1)} fusion(s32[]{:T(128)} %bitcast.4, s32[]{:T(128)} %bitcast.3, s32[]{:T(128)} %bitcast.2, s32[]{:T(128)} %bitcast.1, s32[]{:T(128)S(6)} %mul.244, s32[]{:T(128)S(6)} %mul.239), kind=kLoop, calls=%fused_computation.169 | loop fusion | flops 51200 | bytes 4120 | tf_op jit(solution)/shard_map/add | solution.py:106
  51.9 27.5 %all-to-all-done = bf16[32,256,128]{2,1,0:T(8,128)(2,1)S(1)} async-done(((bf16[32,256,128]{2,1,0:T(8,128)(2,1)}), bf16[32,256,128]{2,1,0:T(8,128)(2,1)S(1)}, u32[]{:S(2)}, u32[]{:S(2)}) %all-to-all-start) | async-done | bytes 2097184 | tf_op jit(solution)/shard_map/all_to_all | solution.py:158
  79.4 2.3 pad_maximum_fusion
  81.7 7.4 %all-to-all-start.1 = ((bf16[32,128,128]{2,1,0:T(8,128)(2,1)}), bf16[32,128,128]{2,1,0:T(8,128)(2,1)}, u32[]{:S(2)}, u32[]{:S(2)}) async-start(bf16[32,128,128]{2,1,0:T(8,128)(2,1)} %pad_maximum_fusion), calls=%async_computation.1 | async-start | bytes 2097152 | tf_op jit(solution)/shard_map/all_to_all | solution.py:162
  89.2 2.5 %broadcast_compare_fusion.2 = pred[1024]{0:T(1024)(128)(4,1)S(1)} fusion(s32[]{:T(128)} %bitcast.4, s32[]{:T(128)} %bitcast.3, s32[]{:T(128)} %bitcast.2, s32[]{:T(128)} %bitcast.1, s32[]{:T(128)S(6)} %mul.244, s32[]{:T(128)S(6)} %mul.239), kind=kLoop, calls=%fused_computation.189 | loop fusion | flops 52224 | bytes 1048 | tf_op jit(solution)/shard_map/ge | solution.py:56
  92.3 2.5 %select_convert_fusion.1 = f32[1024]{0:T(1024)S(1)} fusion(s32[]{:T(128)} %bitcast.13, s32[]{:T(128)} %bitcast.12, s32[]{:T(128)} %bitcast.11, s32[]{:T(128)} %bitcast.10, s32[]{:T(128)S(6)} %mul.244), kind=kLoop, calls=%fused_computation.166 | loop fusion | flops 45056 | bytes 4116 | tf_op jit(solution)/shard_map/convert_element_type | solution.py:30
  95.1 2.2 fusion.52
  97.8 2.0 fusion.36
  100.2 16.0 %all-to-all-done.1 = bf16[32,128,128]{2,1,0:T(8,128)(2,1)} async-done(((bf16[32,128,128]{2,1,0:T(8,128)(2,1)}), bf16[32,128,128]{2,1,0:T(8,128)(2,1)}, u32[]{:S(2)}, u32[]{:S(2)}) %all-to-all-start.1) | async-done | bytes 1048608 | tf_op jit(solution)/shard_map/all_to_all | solution.py:162
  116.1 2.3 fusion.133
  118.4 2.4 %reshape.449 = bf16[32,128,64]{2,1,0:T(8,128)(2,1)} reshape(bf16[32,64,128]{2,1,0:T(8,128)(2,1)} %get-tuple-element.20) | data formatting | bytes 1048576 | tf_op jit(solution)/shard_map/reshape | solution.py:163
  120.8 1.9 fusion.42
  123.7 3.5 %all-to-all-start.2 = ((bf16[4,256,192]{1,2,0:T(8,128)(2,1)}), bf16[4,256,192]{1,2,0:T(8,128)(2,1)S(1)}, u32[]{:S(2)}, u32[]{:S(2)}) async-start(bf16[4,256,192]{1,2,0:T(8,128)(2,1)} %broadcast_in_dim.181), calls=%async_computation.2 | async-start | bytes 786432 | tf_op jit(solution)/shard_map/all_to_all | solution.py:90
  132.1 5.8 %all-to-all-done.2 = bf16[4,256,192]{1,2,0:T(8,128)(2,1)S(1)} async-done(((bf16[4,256,192]{1,2,0:T(8,128)(2,1)}), bf16[4,256,192]{1,2,0:T(8,128)(2,1)S(1)}, u32[]{:S(2)}, u32[]{:S(2)}) %all-to-all-start.2) | async-done | bytes 393248 | tf_op jit(solution)/shard_map/all_to_all | solution.py:90
  140.1 2.1 collective-permute-start
  144.1 6.5 %collective-permute-done = bf16[1024,256]{1,0:T(8,128)(2,1)S(1)} collective-permute-done((bf16[1024,256]{1,0:T(8,128)(2,1)S(1)}, bf16[1024,256]{1,0:T(8,128)(2,1)S(1)}, u32[]{:S(2)}, u32[]{:S(2)}) %collective-permute-start) | collective-permute-done | bytes 524320 | tf_op jit(solution)/shard_map/ppermute | solution.py:24
  155.0 13.3 %all_to_all.25 = bf16[4,256,133]{1,2,0:T(8,128)(2,1)S(1)} all-to-all(bf16[4,256,133]{1,2,0:T(8,128)(2,1)S(1)} %concatenate.43), channel_id=1, replica_groups={{0,16,32,48},{64,80,96,112},{128,144,160,176},{192,208,224,240},{256,27..., dimensions={0} | all-to-all | bytes 544768 | tf_op jit(solution)/shard_map/all_to_all | solution.py:95
  168.5 2.1 convert_bitcast_fusion
  170.6 8.7 %all-to-all-start.4 = ((bf16[32,256,128]{2,1,0:T(8,128)(2,1)}), bf16[32,256,128]{2,1,0:T(8,128)(2,1)S(1)}, u32[]{:S(2)}, u32[]{:S(2)}) async-start(bf16[32,256,128]{2,1,0:T(8,128)(2,1)} %convert_bitcast_fusion), calls=%async_computation.4 | async-start | bytes 4194304 | tf_op jit(solution)/shard_map/all_to_all | solution.py:270
  180.0 53.7 %all-to-all-done.4 = bf16[32,256,128]{2,1,0:T(8,128)(2,1)S(1)} async-done(((bf16[32,256,128]{2,1,0:T(8,128)(2,1)}), bf16[32,256,128]{2,1,0:T(8,128)(2,1)S(1)}, u32[]{:S(2)}, u32[]{:S(2)}) %all-to-all-start.4) | async-done | bytes 2097184 | tf_op jit(solution)/shard_map/all_to_all | solution.py:270
  (82 shorter events, 23.4 us)
Async XLA Ops:
  0.0 168.5 %copy-start = (bf16[128,4096]{1,0:T(8,128)(2,1)S(1)}, bf16[128,4096]{1,0:T(8,128)(2,1)}, u32[]{:S(2)}) copy-start(bf16[128,4096]{1,0:T(8,128)(2,1)} %param.18) | copy-start | bytes 3145732
  2.8 76.6 %all-to-all-start = ((bf16[32,256,128]{2,1,0:T(8,128)(2,1)}), bf16[32,256,128]{2,1,0:T(8,128)(2,1)S(1)}, u32[]{:S(2)}, u32[]{:S(2)}) async-start(bf16[32,256,128]{2,1,0:T(8,128)(2,1)} %broadcast_in_dim.177), calls=%async_computation | async-start | bytes 4194304 | tf_op jit(solution)/shard_map/all_to_all | solution.py:158
  18.6 13.7 %copy-start.5 = (s32[16]{0:T(128)S(1)}, s32[16]{0:T(128)}, u32[]{:S(2)}) copy-start(s32[16]{0:T(128)} %param.23) | copy-start | bytes 196
  18.7 14.2 %copy-start.4 = (s32[64]{0:T(128)S(1)}, s32[64]{0:T(128)}, u32[]{:S(2)}) copy-start(s32[64]{0:T(128)} %param.20) | copy-start | bytes 772
  18.7 18.9 %copy-start.6 = (s32[64]{0:T(128)S(1)}, s32[64]{0:T(128)}, u32[]{:S(2)}) copy-start(s32[64]{0:T(128)} %param.19) | copy-start | bytes 772
  25.9 69.0 %copy-start.3 = (s32[64]{0:T(128)S(1)}, s32[64]{0:T(128)}, u32[]{:S(2)}) copy-start(s32[64]{0:T(128)} %param.21) | copy-start | bytes 772
  25.9 69.2 %copy-start.2 = (bf16[4096]{0:T(1024)(128)(2,1)S(1)}, bf16[4096]{0:T(1024)(128)(2,1)}, u32[]{:S(2)}) copy-start(bf16[4096]{0:T(1024)(128)(2,1)} %param.15) | copy-start | bytes 24580
  81.7 34.4 %all-to-all-start.1 = ((bf16[32,128,128]{2,1,0:T(8,128)(2,1)}), bf16[32,128,128]{2,1,0:T(8,128)(2,1)}, u32[]{:S(2)}, u32[]{:S(2)}) async-start(bf16[32,128,128]{2,1,0:T(8,128)(2,1)} %pad_maximum_fusion), calls=%async_computation.1 | async-start | bytes 2097152 | tf_op jit(solution)/shard_map/all_to_all | solution.py:162
  123.7 14.2 %all-to-all-start.2 = ((bf16[4,256,192]{1,2,0:T(8,128)(2,1)}), bf16[4,256,192]{1,2,0:T(8,128)(2,1)S(1)}, u32[]{:S(2)}, u32[]{:S(2)}) async-start(bf16[4,256,192]{1,2,0:T(8,128)(2,1)} %broadcast_in_dim.181), calls=%async_computation.2 | async-start | bytes 786432 | tf_op jit(solution)/shard_map/all_to_all | solution.py:90
  129.2 13.0 %copy-start.1 = (pred[256,1024]{0,1:T(8,128)(4,1)S(1)}, pred[256,1024]{0,1:T(8,128)(4,1)}, u32[]{:S(2)}) copy-start(pred[256,1024]{0,1:T(8,128)(4,1)} %get-tuple-element.43) | copy-start | bytes 786436
  140.1 10.5 %collective-permute-start = (bf16[1024,256]{1,0:T(8,128)(2,1)S(1)}, bf16[1024,256]{1,0:T(8,128)(2,1)S(1)}, u32[]{:S(2)}, u32[]{:S(2)}) collective-permute-start(bf16[1024,256]{1,0:T(8,128)(2,1)S(1)} %scatter_fusion), channel_id=1, source_target_pairs={{0,1},{1,2},{2,3},{3,4},{4,5},{5,6},{6,7},{7,8},{8,9},{9,10},{10,1... | collective-permute-start | bytes 1572872 | tf_op jit(solution)/shard_map/ppermute | solution.py:24
  170.6 63.0 %all-to-all-start.4 = ((bf16[32,256,128]{2,1,0:T(8,128)(2,1)}), bf16[32,256,128]{2,1,0:T(8,128)(2,1)S(1)}, u32[]{:S(2)}, u32[]{:S(2)}) async-start(bf16[32,256,128]{2,1,0:T(8,128)(2,1)} %convert_bitcast_fusion), calls=%async_computation.4 | async-start | bytes 4194304 | tf_op jit(solution)/shard_map/all_to_all | solution.py:270

commit v15 on v9

--- a/solution.py
+++ b/solution.py
@@ -187,9 +187,11 @@
     second = pair_piece[:, quarter:]
     turned = jnp.concatenate([first * cosine - second * sine, second * cosine + first * sine], axis=1)
     own_piece = jnp.where(member < key_members, turned, pair_piece).astype(jnp.bfloat16)
-    shared = group_gather(jnp.concatenate([own_query, own_piece], axis=1), "blk", group_size)
-    queries = shared[:, :, :HEAD_DIM].transpose(1, 0, 2)
-    pieces = shared[:, :, HEAD_DIM:]
+    piece_rows = slots * pair_cols // HEAD_DIM
+    outgoing = jnp.concatenate([own_query, own_piece.reshape(piece_rows, HEAD_DIM)], axis=0)
+    shared = group_gather(outgoing, "blk", group_size)
+    queries = shared[:, :slots].transpose(1, 0, 2)
+    pieces = shared[:, slots:].reshape(group_size, slots, pair_cols)
     fresh_keys = jnp.concatenate(
         [pieces[m, :, :quarter] for m in range(key_members)]
         + [pieces[m, :, quarter:] for m in range(key_members)],
@@ -240,14 +242,22 @@
     scale_prior = jnp.exp(prior_part[0] - top)
     totals = own_part[1] * scale_own + prior_part[1] * scale_prior
     summed = own_part[2] * scale_own[..., None] + prior_part[2] * scale_prior[..., None]
-    packed = jnp.concatenate([summed, top[..., None], totals[..., None]], axis=-1)
+    stat_rows = slots // HEAD_DIM
+    packed = jnp.concatenate(
+        [
+            summed,
+            top.reshape(group_size, stat_rows, HEAD_DIM),
+            totals.reshape(group_size, stat_rows, HEAD_DIM),
+        ],
+        axis=1,
+    )
     gathered = group_exchange(packed, "blk", group_size)
-    part_max = gathered[:, :, HEAD_DIM]
-    part_total = gathered[:, :, HEAD_DIM + 1]
+    part_max = gathered[:, slots : slots + stat_rows].reshape(group_size, slots)
+    part_total = gathered[:, slots + stat_rows :].reshape(group_size, slots)
     best = jnp.max(part_max, axis=0)
     weight = jnp.exp(part_max - best[None])
     total = jnp.sum(part_total * weight, axis=0)
-    heads_sum = jnp.sum(gathered[:, :, :HEAD_DIM] * weight[..., None], axis=0)
+    heads_sum = jnp.sum(gathered[:, :slots] * weight[..., None], axis=0)
     heads_out = (heads_sum / total[:, None]).astype(jnp.bfloat16)
     term = jnp.einsum(
         "ch,hkd->kcd",

time: 246 us -> 256 us (1.041)
  matrix products: 11.8 us -> 18.7 us
    ppermute x1, waiting for transfers between devices: 6.41 us -> 2.35 us  [shifted(): return lax.ppermute(shard, axis, pairs)]
    dot_general x2, matrix products: 3.24 us -> 7.19 us  [attend_part(): jnp.einsum('gcs,sh->gch', weights.astype(jnp.bfloat16), values, preferred...]
    all_to_all x1, waiting for transfers between devices: 56.7 us -> 60.1 us  [local(): lax.all_to_all(term.astype(jnp.bfloat16), 'blk', 0, 0, tiled=True)]
    dot_general x2, matrix products: 2.57 us -> 5.5 us  [attend_part(): jnp.einsum('cgh,sh->gcs', queries, keys, preferred_element_type=jnp.float32)]
where the time goes in v15:
time: 256 us; the launch traced here: 254 us
  waiting for transfers between devices  112 us (44%)
  starting transfers between devices  38.7 us (15%)
  other arithmetic  35.8 us (14%)
  local copies, waits for them, and re-layouts  28.9 us (11%)
  blocking collectives  19.5 us (8%)
  matrix products  18.7 us (7%)
    all_to_all x1, waiting for transfers between devices, local(): lax.all_to_all(term.astype(jnp.bfloat16), 'blk', 0, 0, tiled=True)  60.1 us
    all_to_all x1, waiting for transfers between devices, local(): arrived = lax.all_to_all(x_part, 'blk', 0, 0, tiled=True)  23.9 us
    all_to_all x1, blocking collectives, group_exchange(): lax.all_to_all(parts, axis, 0, 0, axis_index_groups=groups, tiled=True)  19.5 us
    all_to_all x1, waiting for transfers between devices, local(): lax.all_to_all(jnp.concatenate([w_part, c_part], axis=1), 'blk', 0, 0, ti...  17.6 us
    all_to_all x1, starting transfers between devices, local(): arrived = lax.all_to_all(x_part, 'blk', 0, 0, tiled=True)  15.9 us
    all_to_all x1, starting transfers between devices, local(): lax.all_to_all(jnp.concatenate([w_part, c_part], axis=1), 'blk', 0, 0, ti...  11.5 us
    select_n x3, other arithmetic, tenant_lookup(): span_ids = positions // SPAN  8.81 us
    all_to_all x1, waiting for transfers between devices, group_gather(): lax.all_to_all(spread, axis, 0, 0, axis_index_groups=groups, tiled=True)  8.17 us
  transfers between devices with their start and end apart: 5, of which 5 were waited for; matrix products, arithmetic and copies ran while one was open for 21% of the time, Pallas kernels for 0%

profile of v15, /device:TPU:26, one launch (start us, length us, event | category | flops | bytes accessed | tf_op | source)
XLA Modules:
  0.0 254.2 jit_solution(6226303904464014228)
XLA Ops:
  0.0 2.8 %broadcast_in_dim.172 = bf16[32,256,128]{2,1,0:T(8,128)(2,1)} broadcast(bf16[256,128]{1,0:T(8,128)(2,1)} %param.14), dimensions={1,2} | broadcast | bytes 2162688 | tf_op jit(solution)/shard_map/broadcast_in_dim | solution.py:131
  2.8 15.9 %all-to-all-start = ((bf16[32,256,128]{2,1,0:T(8,128)(2,1)}), bf16[32,256,128]{2,1,0:T(8,128)(2,1)S(1)}, u32[]{:S(2)}, u32[]{:S(2)}) async-start(bf16[32,256,128]{2,1,0:T(8,128)(2,1)} %broadcast_in_dim.172), calls=%async_computation | async-start | bytes 4194304 | tf_op jit(solution)/shard_map/all_to_all | solution.py:152
  20.0 3.8 %and_select_fusion.8 = (s32[256]{0:T(256)S(1)}, s32[256]{0:T(256)S(1)}, s32[256]{0:T(256)S(1)}) fusion(s32[4096]{0:T(1024)} %param.22, s32[]{:T(128)S(6)} %select_n.158, s32[]{:T(128)S(6)} %mul.218, s32[]{:T(128)S(6)} %select_n.164, s32[]{:T(128)S(6)} %mul.220, s32[]{:T(128)} %bitcast.17, s32[]{:T(128)} %bitcast.16, s32[]{:T(128)} %bitcast.15, s32[]{:T(128)} %bitcast.14, ...), kind=kLoop, calls=%fused_computation.183 | loop fusion | flops 26112 | bytes 4132 | tf_op jit(solution)/shard_map/jit(floor_divide)/jit(_where)/select_n | solution.py:42
  28.7 2.4 copy.63
  31.1 2.4 reshape.377
  38.5 2.5 broadcast_compare_fusion.3
  41.0 2.5 fusion.97
  43.4 2.5 add_select_fusion
  46.6 2.5 add_select_fusion.1
  49.1 2.5 fusion.99
  51.6 23.9 %all-to-all-done = bf16[32,256,128]{2,1,0:T(8,128)(2,1)S(1)} async-done(((bf16[32,256,128]{2,1,0:T(8,128)(2,1)}), bf16[32,256,128]{2,1,0:T(8,128)(2,1)S(1)}, u32[]{:S(2)}, u32[]{:S(2)}) %all-to-all-start) | async-done | bytes 2097184 | tf_op jit(solution)/shard_map/all_to_all | solution.py:152
  75.5 2.3 pad_maximum_fusion
  77.8 11.5 %all-to-all-start.1 = ((bf16[32,128,128]{2,1,0:T(8,128)(2,1)}), bf16[32,128,128]{2,1,0:T(8,128)(2,1)}, u32[]{:S(2)}, u32[]{:S(2)}) async-start(bf16[32,128,128]{2,1,0:T(8,128)(2,1)} %pad_maximum_fusion), calls=%async_computation.1 | async-start | bytes 2097152 | tf_op jit(solution)/shard_map/all_to_all | solution.py:156
  89.3 2.5 broadcast_compare_fusion.2
  92.4 2.5 select_convert_fusion.1
  95.2 2.2 fusion.46
  100.2 17.6 %all-to-all-done.1 = bf16[32,128,128]{2,1,0:T(8,128)(2,1)} async-done(((bf16[32,128,128]{2,1,0:T(8,128)(2,1)}), bf16[32,128,128]{2,1,0:T(8,128)(2,1)}, u32[]{:S(2)}, u32[]{:S(2)}) %all-to-all-start.1) | async-done | bytes 1048608 | tf_op jit(solution)/shard_map/all_to_all | solution.py:156
  117.9 2.3 fusion.114
  120.2 2.4 reshape.383
  126.0 3.5 %all-to-all-start.2 = ((bf16[4,384,128]{2,1,0:T(8,128)(2,1)}), bf16[4,384,128]{2,1,0:T(8,128)(2,1)S(1)}, u32[]{:S(2)}, u32[]{:S(2)}) async-start(bf16[4,384,128]{2,1,0:T(8,128)(2,1)} %broadcast_in_dim.176), calls=%async_computation.2 | async-start | bytes 786432 | tf_op jit(solution)/shard_map/all_to_all | solution.py:84
  132.7 8.2 %all-to-all-done.2 = bf16[4,384,128]{2,1,0:T(8,128)(2,1)S(1)} async-done(((bf16[4,384,128]{2,1,0:T(8,128)(2,1)}), bf16[4,384,128]{2,1,0:T(8,128)(2,1)S(1)}, u32[]{:S(2)}, u32[]{:S(2)}) %all-to-all-start.2) | async-done | bytes 393248 | tf_op jit(solution)/shard_map/all_to_all | solution.py:84
  143.3 2.1 collective-permute-start
  145.4 2.8 %fusion.2 = (f32[4,256]{1,0:T(4,128)S(1)}, f32[1024,256,4]{1,0,2:T(8,128)}) fusion(pred[256,1024]{0,1:T(8,128)(4,1)S(1)} %copy-done.2, bf16[4,384,128]{2,1,0:T(8,128)(2,1)S(1)} %all-to-all-done.2, bf16[1024,256]{1,0:T(8,128)(2,1)S(1)} %scatter_fusion), kind=kOutput, calls=%fused_computation.10 | convolution fusion | flops 271580160 | bytes 4984832 | tf_op jit(solution)/shard_map/cgh,sh->gcs/dot_general | solution.py:50
  148.2 3.2 %fusion.4 = f32[4,256]{1,0:T(4,128)S(1)} fusion(f32[1024,256,4]{1,0,2:T(8,128)} %get-tuple-element.64, f32[4,256]{1,0:T(4,128)S(1)} %get-tuple-element.63, pred[256,1024]{0,1:T(8,128)(4,1)S(1)} %copy-done.2), kind=kLoop, calls=%fused_computation.12 | loop fusion | flops 5241856 | bytes 4464640 | tf_op jit(solution)/shard_map/reduce_sum | solution.py:61
  151.5 2.4 collective-permute-done
  153.8 2.7 %fusion.3 = (f32[4,256]{1,0:T(4,128)S(1)}, f32[1024,256,4]{1,0,2:T(8,128)}) fusion(pred[256,1024]{0,1:T(8,128)(4,1)S(1)} %get-tuple-element.43, bf16[4,384,128]{2,1,0:T(8,128)(2,1)S(1)} %all-to-all-done.2, bf16[1024,256]{1,0:T(8,128)(2,1)S(1)} %collective-permute-done), kind=kOutput, calls=%fused_computation.11 | convolution fusion | flops 271580160 | bytes 4984832 | tf_op jit(solution)/shard_map/cgh,sh->gcs/dot_general | solution.py:50
  156.6 3.7 %fusion.18 = f32[4,256,128]{2,1,0:T(8,128)S(1)} fusion(f32[1024,256,4]{1,0,2:T(8,128)} %get-tuple-element.64, f32[4,256]{1,0:T(4,128)S(1)} %get-tuple-element.63, pred[256,1024]{0,1:T(8,128)(4,1)S(1)} %copy-done.2, bf16[1024,256]{1,0:T(8,128)(2,1)S(1)} %scatter_fusion, f32[4,256]{1,0:T(4,128)S(1)} %get-tuple-element.41), kind=kOutput, calls=%fused_computation.27 | convolution fusion | flops 273809408 | bytes 5251072 | tf_op jit(solution)/shard_map/gcs,sh->gch/dot_general | solution.py:62
  161.3 3.5 %fusion.24 = f32[4,256,128]{2,1,0:T(8,128)S(1)} fusion(f32[4,256,128]{2,1,0:T(8,128)S(1)} %fusion.18, f32[1024,256,4]{1,0,2:T(8,128)} %get-tuple-element.62, f32[4,256]{1,0:T(4,128)S(1)} %get-tuple-element.61, pred[256,1024]{0,1:T(8,128)(4,1)S(1)} %get-tuple-element.43, bf16[1024,256]{1,0:T(8,128)(2,1)S(1)} %collective-permute-done, ...), kind=kOutput, calls=%fused_computation.29 | convolution fusion | flops 273940480 | bytes 5775360 | tf_op jit(solution)/shard_map/gcs,sh->gch/dot_general | solution.py:62
  164.9 19.5 %all_to_all.25 = f32[4,260,128]{2,1,0:T(8,128)S(1)} all-to-all(f32[4,260,128]{2,1,0:T(8,128)S(1)} %pad_maximum_fusion.1), channel_id=1, replica_groups={{0,16,32,48},{64,80,96,112},{128,144,160,176},{192,208,224,240},{256,27..., dimensions={0} | all-to-all | bytes 1064960 | tf_op jit(solution)/shard_map/all_to_all | solution.py:89
  184.7 2.1 convert_bitcast_fusion
  186.8 5.7 %all-to-all-start.4 = ((bf16[32,256,128]{2,1,0:T(8,128)(2,1)}), bf16[32,256,128]{2,1,0:T(8,128)(2,1)S(1)}, u32[]{:S(2)}, u32[]{:S(2)}) async-start(bf16[32,256,128]{2,1,0:T(8,128)(2,1)} %convert_bitcast_fusion), calls=%async_computation.4 | async-start | bytes 4194304 | tf_op jit(solution)/shard_map/all_to_all | solution.py:268
  193.1 60.1 %all-to-all-done.4 = bf16[32,256,128]{2,1,0:T(8,128)(2,1)S(1)} async-done(((bf16[32,256,128]{2,1,0:T(8,128)(2,1)}), bf16[32,256,128]{2,1,0:T(8,128)(2,1)S(1)}, u32[]{:S(2)}, u32[]{:S(2)}) %all-to-all-start.4) | async-done | bytes 2097184 | tf_op jit(solution)/shard_map/all_to_all | solution.py:268
  (80 shorter events, 27.4 us)
Async XLA Ops:
  0.0 184.7 %copy-start = (bf16[128,4096]{1,0:T(8,128)(2,1)S(1)}, bf16[128,4096]{1,0:T(8,128)(2,1)}, u32[]{:S(2)}) copy-start(bf16[128,4096]{1,0:T(8,128)(2,1)} %param.18) | copy-start | bytes 3145732
  0.0 18.8 %copy-start.6 = (s32[16]{0:T(128)S(1)}, s32[16]{0:T(128)}, u32[]{:S(2)}) copy-start(s32[16]{0:T(128)} %param.23) | copy-start | bytes 196
  0.0 19.3 %copy-start.5 = (s32[64]{0:T(128)S(1)}, s32[64]{0:T(128)}, u32[]{:S(2)}) copy-start(s32[64]{0:T(128)} %param.20) | copy-start | bytes 772
  2.8 72.7 %all-to-all-start = ((bf16[32,256,128]{2,1,0:T(8,128)(2,1)}), bf16[32,256,128]{2,1,0:T(8,128)(2,1)S(1)}, u32[]{:S(2)}, u32[]{:S(2)}) async-start(bf16[32,256,128]{2,1,0:T(8,128)(2,1)} %broadcast_in_dim.172), calls=%async_computation | async-start | bytes 4194304 | tf_op jit(solution)/shard_map/all_to_all | solution.py:152
  23.9 13.6 %copy-start.7 = (s32[64]{0:T(128)S(1)}, s32[64]{0:T(128)}, u32[]{:S(2)}) copy-start(s32[64]{0:T(128)} %param.19) | copy-start | bytes 772
  31.1 63.8 %copy-start.4 = (s32[64]{0:T(128)S(1)}, s32[64]{0:T(128)}, u32[]{:S(2)}) copy-start(s32[64]{0:T(128)} %param.21) | copy-start | bytes 772
  31.1 64.1 %copy-start.3 = (bf16[4096]{0:T(1024)(128)(2,1)S(1)}, bf16[4096]{0:T(1024)(128)(2,1)}, u32[]{:S(2)}) copy-start(bf16[4096]{0:T(1024)(128)(2,1)} %param.15) | copy-start | bytes 24580
  77.8 40.1 %all-to-all-start.1 = ((bf16[32,128,128]{2,1,0:T(8,128)(2,1)}), bf16[32,128,128]{2,1,0:T(8,128)(2,1)}, u32[]{:S(2)}, u32[]{:S(2)}) async-start(bf16[32,128,128]{2,1,0:T(8,128)(2,1)} %pad_maximum_fusion), calls=%async_computation.1 | async-start | bytes 2097152 | tf_op jit(solution)/shard_map/all_to_all | solution.py:156
  126.0 14.9 %all-to-all-start.2 = ((bf16[4,384,128]{2,1,0:T(8,128)(2,1)}), bf16[4,384,128]{2,1,0:T(8,128)(2,1)S(1)}, u32[]{:S(2)}, u32[]{:S(2)}) async-start(bf16[4,384,128]{2,1,0:T(8,128)(2,1)} %broadcast_in_dim.176), calls=%async_computation.2 | async-start | bytes 786432 | tf_op jit(solution)/shard_map/all_to_all | solution.py:84
  130.7 14.7 %copy-start.2 = (pred[256,1024]{0,1:T(8,128)(4,1)S(1)}, pred[256,1024]{0,1:T(8,128)(4,1)}, u32[]{:S(2)}) copy-start(pred[256,1024]{0,1:T(8,128)(4,1)} %get-tuple-element.42) | copy-start | bytes 786436
  143.3 10.5 %collective-permute-start = (bf16[1024,256]{1,0:T(8,128)(2,1)S(1)}, bf16[1024,256]{1,0:T(8,128)(2,1)S(1)}, u32[]{:S(2)}, u32[]{:S(2)}) collective-permute-start(bf16[1024,256]{1,0:T(8,128)(2,1)S(1)} %scatter_fusion), channel_id=1, source_target_pairs={{0,1},{1,2},{2,3},{3,4},{4,5},{5,6},{6,7},{7,8},{8,9},{9,10},{10,1... | collective-permute-start | bytes 1572872 | tf_op jit(solution)/shard_map/ppermute | solution.py:24
  156.6 3.7 %copy-start.1 = (f32[1024,256,4]{1,0,2:T(8,128)S(1)}, f32[1024,256,4]{1,0,2:T(8,128)}, u32[]{:S(2)}) copy-start(f32[1024,256,4]{1,0,2:T(8,128)} %get-tuple-element.62) | copy-start | bytes 12582916
  186.8 66.3 %all-to-all-start.4 = ((bf16[32,256,128]{2,1,0:T(8,128)(2,1)}), bf16[32,256,128]{2,1,0:T(8,128)(2,1)S(1)}, u32[]{:S(2)}, u32[]{:S(2)}) async-start(bf16[32,256,128]{2,1,0:T(8,128)(2,1)} %convert_bitcast_fusion), calls=%async_computation.4 | async-start | bytes 4194304 | tf_op jit(solution)/shard_map/all_to_all | solution.py:268

commit v16 on v15

--- a/solution.py
+++ b/solution.py
@@ -187,11 +187,9 @@
     second = pair_piece[:, quarter:]
     turned = jnp.concatenate([first * cosine - second * sine, second * cosine + first * sine], axis=1)
     own_piece = jnp.where(member < key_members, turned, pair_piece).astype(jnp.bfloat16)
-    piece_rows = slots * pair_cols // HEAD_DIM
-    outgoing = jnp.concatenate([own_query, own_piece.reshape(piece_rows, HEAD_DIM)], axis=0)
-    shared = group_gather(outgoing, "blk", group_size)
-    queries = shared[:, :slots].transpose(1, 0, 2)
-    pieces = shared[:, slots:].reshape(group_size, slots, pair_cols)
+    shared = group_gather(jnp.concatenate([own_query, own_piece], axis=1), "blk", group_size)
+    queries = shared[:, :, :HEAD_DIM].transpose(1, 0, 2)
+    pieces = shared[:, :, HEAD_DIM:]
     fresh_keys = jnp.concatenate(
         [pieces[m, :, :quarter] for m in range(key_members)]
         + [pieces[m, :, quarter:] for m in range(key_members)],

time: 256 us -> 256 us (level)
  the two profiles are of different devices: /device:TPU:26 before, /device:TPU:145 now
where the time goes in v16:
time: 256 us; the launch traced here: 255 us
  waiting for transfers between devices  106 us (41%)
  starting transfers between devices  48.4 us (19%)
  other arithmetic  35.9 us (14%)
  local copies, waits for them, and re-layouts  28.2 us (11%)
  matrix products  19.6 us (8%)
  blocking collectives  16.8 us (7%)
    all_to_all x1, waiting for transfers between devices, local(): lax.all_to_all(term.astype(jnp.bfloat16), 'blk', 0, 0, tiled=True)  64.2 us
    all_to_all x1, waiting for transfers between devices, local(): arrived = lax.all_to_all(x_part, 'blk', 0, 0, tiled=True)  20.1 us
    all_to_all x1, blocking collectives, group_exchange(): lax.all_to_all(parts, axis, 0, 0, axis_index_groups=groups, tiled=True)  16.8 us
    all_to_all x1, waiting for transfers between devices, local(): lax.all_to_all(jnp.concatenate([w_part, c_part], axis=1), 'blk', 0, 0, ti...  15.4 us
    all_to_all x1, starting transfers between devices, local(): lax.all_to_all(jnp.concatenate([w_part, c_part], axis=1), 'blk', 0, 0, ti...  15.3 us
    all_to_all x1, starting transfers between devices, local(): arrived = lax.all_to_all(x_part, 'blk', 0, 0, tiled=True)  13.7 us
    select_n x3, other arithmetic, tenant_lookup(): span_ids = positions // SPAN  8.88 us
    dot_general x2, matrix products, attend_part(): jnp.einsum('gcs,sh->gch', weights.astype(jnp.bfloat16), values, preferred...  8.04 us
  transfers between devices with their start and end apart: 5, of which 4 were waited for; matrix products, arithmetic and copies ran while one was open for 21% of the time, Pallas kernels for 0%

profile of v16, /device:TPU:145, one launch (start us, length us, event | category | flops | bytes accessed | tf_op | source)
XLA Modules:
  0.0 255.1 jit_solution(6434797175433303918)
XLA Ops:
  0.0 2.8 %broadcast_in_dim.172 = bf16[32,256,128]{2,1,0:T(8,128)(2,1)} broadcast(bf16[256,128]{1,0:T(8,128)(2,1)} %param.14), dimensions={1,2} | broadcast | bytes 2162688 | tf_op jit(solution)/shard_map/broadcast_in_dim | solution.py:131
  2.8 13.7 %all-to-all-start = ((bf16[32,256,128]{2,1,0:T(8,128)(2,1)}), bf16[32,256,128]{2,1,0:T(8,128)(2,1)S(1)}, u32[]{:S(2)}, u32[]{:S(2)}) async-start(bf16[32,256,128]{2,1,0:T(8,128)(2,1)} %broadcast_in_dim.172), calls=%async_computation | async-start | bytes 4194304 | tf_op jit(solution)/shard_map/all_to_all | solution.py:152
  17.8 3.9 %and_select_fusion.8 = (s32[256]{0:T(256)S(1)}, s32[256]{0:T(256)S(1)}, s32[256]{0:T(256)S(1)}) fusion(s32[4096]{0:T(1024)} %param.22, s32[]{:T(128)S(6)} %select_n.158, s32[]{:T(128)S(6)} %mul.218, s32[]{:T(128)S(6)} %select_n.164, s32[]{:T(128)S(6)} %mul.220, s32[]{:T(128)} %bitcast.17, s32[]{:T(128)} %bitcast.16, s32[]{:T(128)} %bitcast.15, s32[]{:T(128)} %bitcast.14, ...), kind=kLoop, calls=%fused_computation.192 | loop fusion | flops 26112 | bytes 4132 | tf_op jit(solution)/shard_map/jit(floor_divide)/jit(_where)/select_n | solution.py:42
  21.8 2.1 copy.71
  26.6 2.4 copy.72
  28.9 2.4 reshape.367
  36.3 2.5 broadcast_compare_fusion.3
  38.8 2.5 fusion.105
  41.3 2.5 add_select_fusion
  44.4 2.5 add_select_fusion.1
  46.9 2.5 fusion.107
  49.4 20.1 %all-to-all-done = bf16[32,256,128]{2,1,0:T(8,128)(2,1)S(1)} async-done(((bf16[32,256,128]{2,1,0:T(8,128)(2,1)}), bf16[32,256,128]{2,1,0:T(8,128)(2,1)S(1)}, u32[]{:S(2)}, u32[]{:S(2)}) %all-to-all-start) | async-done | bytes 2097184 | tf_op jit(solution)/shard_map/all_to_all | solution.py:152
  69.5 2.3 pad_maximum_fusion
  71.8 15.3 %all-to-all-start.1 = ((bf16[32,128,128]{2,1,0:T(8,128)(2,1)}), bf16[32,128,128]{2,1,0:T(8,128)(2,1)}, u32[]{:S(2)}, u32[]{:S(2)}) async-start(bf16[32,128,128]{2,1,0:T(8,128)(2,1)} %pad_maximum_fusion), calls=%async_computation.1 | async-start | bytes 2097152 | tf_op jit(solution)/shard_map/all_to_all | solution.py:156
  87.2 2.5 broadcast_compare_fusion.2
  90.3 2.5 select_convert_fusion.1
  93.1 2.2 fusion.46
  98.1 15.4 %all-to-all-done.1 = bf16[32,128,128]{2,1,0:T(8,128)(2,1)} async-done(((bf16[32,128,128]{2,1,0:T(8,128)(2,1)}), bf16[32,128,128]{2,1,0:T(8,128)(2,1)}, u32[]{:S(2)}, u32[]{:S(2)}) %all-to-all-start.1) | async-done | bytes 1048608 | tf_op jit(solution)/shard_map/all_to_all | solution.py:156
  113.6 2.3 fusion.122
  115.9 2.4 reshape.373
  121.2 5.7 %all-to-all-start.2 = ((bf16[4,256,192]{1,2,0:T(8,128)(2,1)}), bf16[4,256,192]{1,2,0:T(8,128)(2,1)S(1)}, u32[]{:S(2)}, u32[]{:S(2)}) async-start(bf16[4,256,192]{1,2,0:T(8,128)(2,1)} %broadcast_in_dim.176), calls=%async_computation.2 | async-start | bytes 786432 | tf_op jit(solution)/shard_map/all_to_all | solution.py:84
  130.2 6.1 %all-to-all-done.2 = bf16[4,256,192]{1,2,0:T(8,128)(2,1)S(1)} async-done(((bf16[4,256,192]{1,2,0:T(8,128)(2,1)}), bf16[4,256,192]{1,2,0:T(8,128)(2,1)S(1)}, u32[]{:S(2)}, u32[]{:S(2)}) %all-to-all-start.2) | async-done | bytes 393248 | tf_op jit(solution)/shard_map/all_to_all | solution.py:84
  138.5 6.3 %collective-permute-start = (bf16[1024,256]{1,0:T(8,128)(2,1)S(1)}, bf16[1024,256]{1,0:T(8,128)(2,1)S(1)}, u32[]{:S(2)}, u32[]{:S(2)}) collective-permute-start(bf16[1024,256]{1,0:T(8,128)(2,1)S(1)} %scatter_fusion), channel_id=1, source_target_pairs={{0,1},{1,2},{2,3},{3,4},{4,5},{5,6},{6,7},{7,8},{8,9},{9,10},{10,1... | collective-permute-start | bytes 1572872 | tf_op jit(solution)/shard_map/ppermute | solution.py:24
  144.8 2.8 %fusion.2 = (f32[4,256]{1,0:T(4,128)S(1)}, f32[1024,256,4]{1,0,2:T(8,128)}) fusion(pred[256,1024]{0,1:T(8,128)(4,1)S(1)} %copy-done.2, bf16[4,256,128]{2,1,0:T(8,128)(2,1)S(1)} %copy.89, bf16[1024,256]{1,0:T(8,128)(2,1)S(1)} %scatter_fusion), kind=kOutput, calls=%fused_computation.10 | convolution fusion | flops 271580160 | bytes 4984832 | tf_op jit(solution)/shard_map/cgh,sh->gcs/dot_general | solution.py:50
  147.6 3.2 %fusion.4 = f32[4,256]{1,0:T(4,128)S(1)} fusion(f32[1024,256,4]{1,0,2:T(8,128)} %get-tuple-element.58, f32[4,256]{1,0:T(4,128)S(1)} %get-tuple-element.57, pred[256,1024]{0,1:T(8,128)(4,1)S(1)} %copy-done.2), kind=kLoop, calls=%fused_computation.12 | loop fusion | flops 5241856 | bytes 4464640 | tf_op jit(solution)/shard_map/reduce_sum | solution.py:61
  150.8 2.7 %fusion.3 = (f32[4,256]{1,0:T(4,128)S(1)}, f32[1024,256,4]{1,0,2:T(8,128)}) fusion(pred[256,1024]{0,1:T(8,128)(4,1)S(1)} %get-tuple-element.37, bf16[4,256,128]{2,1,0:T(8,128)(2,1)S(1)} %copy.89, bf16[1024,256]{1,0:T(8,128)(2,1)S(1)} %collective-permute-done), kind=kOutput, calls=%fused_computation.11 | convolution fusion | flops 271580160 | bytes 4984832 | tf_op jit(solution)/shard_map/cgh,sh->gcs/dot_general | solution.py:50
  153.6 4.5 %fusion.18 = f32[4,256,128]{2,1,0:T(8,128)} fusion(f32[1024,256,4]{1,0,2:T(8,128)} %get-tuple-element.58, f32[4,256]{1,0:T(4,128)S(1)} %get-tuple-element.57, pred[256,1024]{0,1:T(8,128)(4,1)S(1)} %copy-done.2, bf16[1024,256]{1,0:T(8,128)(2,1)S(1)} %scatter_fusion, f32[4,256]{1,0:T(4,128)S(1)} %get-tuple-element.35), kind=kOutput, calls=%fused_computation.27 | convolution fusion | flops 273809408 | bytes 5251072 | tf_op jit(solution)/shard_map/gcs,sh->gch/dot_general | solution.py:62
  159.2 3.5 %fusion.24 = f32[4,256,128]{2,1,0:T(8,128)S(1)} fusion(f32[4,256,128]{2,1,0:T(8,128)S(1)} %copy-done.8, f32[1024,256,4]{1,0,2:T(8,128)} %get-tuple-element.56, f32[4,256]{1,0:T(4,128)S(1)} %get-tuple-element.55, pred[256,1024]{0,1:T(8,128)(4,1)S(1)} %get-tuple-element.37, bf16[1024,256]{1,0:T(8,128)(2,1)S(1)} %collective-permute-done, ...), kind=kOutput, calls=%fused_computation.29 | convolution fusion | flops 273940480 | bytes 5775360 | tf_op jit(solution)/shard_map/gcs,sh->gch/dot_general | solution.py:62
  162.8 16.8 %all_to_all.25 = f32[4,260,128]{2,1,0:T(8,128)S(1)} all-to-all(f32[4,260,128]{2,1,0:T(8,128)S(1)} %pad_maximum_fusion.1), channel_id=1, replica_groups={{0,16,32,48},{64,80,96,112},{128,144,160,176},{192,208,224,240},{256,27..., dimensions={0} | all-to-all | bytes 1064960 | tf_op jit(solution)/shard_map/all_to_all | solution.py:89
  179.9 2.1 convert_bitcast_fusion
  182.0 7.3 %all-to-all-start.4 = ((bf16[32,256,128]{2,1,0:T(8,128)(2,1)}), bf16[32,256,128]{2,1,0:T(8,128)(2,1)S(1)}, u32[]{:S(2)}, u32[]{:S(2)}) async-start(bf16[32,256,128]{2,1,0:T(8,128)(2,1)} %convert_bitcast_fusion), calls=%async_computation.4 | async-start | bytes 4194304 | tf_op jit(solution)/shard_map/all_to_all | solution.py:266
  189.9 64.2 %all-to-all-done.4 = bf16[32,256,128]{2,1,0:T(8,128)(2,1)S(1)} async-done(((bf16[32,256,128]{2,1,0:T(8,128)(2,1)}), bf16[32,256,128]{2,1,0:T(8,128)(2,1)S(1)}, u32[]{:S(2)}, u32[]{:S(2)}) %all-to-all-start.4) | async-done | bytes 2097184 | tf_op jit(solution)/shard_map/all_to_all | solution.py:266
  (80 shorter events, 24.7 us)
Async XLA Ops:
  0.0 179.8 %copy-start = (bf16[128,4096]{1,0:T(8,128)(2,1)S(1)}, bf16[128,4096]{1,0:T(8,128)(2,1)}, u32[]{:S(2)}) copy-start(bf16[128,4096]{1,0:T(8,128)(2,1)} %param.18) | copy-start | bytes 3145732
  0.0 16.5 %copy-start.6 = (s32[16]{0:T(128)S(1)}, s32[16]{0:T(128)}, u32[]{:S(2)}) copy-start(s32[16]{0:T(128)} %param.23) | copy-start | bytes 196
  0.0 17.1 %copy-start.5 = (s32[64]{0:T(128)S(1)}, s32[64]{0:T(128)}, u32[]{:S(2)}) copy-start(s32[64]{0:T(128)} %param.20) | copy-start | bytes 772
  2.8 66.7 %all-to-all-start = ((bf16[32,256,128]{2,1,0:T(8,128)(2,1)}), bf16[32,256,128]{2,1,0:T(8,128)(2,1)S(1)}, u32[]{:S(2)}, u32[]{:S(2)}) async-start(bf16[32,256,128]{2,1,0:T(8,128)(2,1)} %broadcast_in_dim.172), calls=%async_computation | async-start | bytes 4194304 | tf_op jit(solution)/shard_map/all_to_all | solution.py:152
  21.7 13.6 %copy-start.7 = (s32[64]{0:T(128)S(1)}, s32[64]{0:T(128)}, u32[]{:S(2)}) copy-start(s32[64]{0:T(128)} %param.19) | copy-start | bytes 772
  28.9 63.9 %copy-start.4 = (s32[64]{0:T(128)S(1)}, s32[64]{0:T(128)}, u32[]{:S(2)}) copy-start(s32[64]{0:T(128)} %param.21) | copy-start | bytes 772
  28.9 64.1 %copy-start.3 = (bf16[4096]{0:T(1024)(128)(2,1)S(1)}, bf16[4096]{0:T(1024)(128)(2,1)}, u32[]{:S(2)}) copy-start(bf16[4096]{0:T(1024)(128)(2,1)} %param.15) | copy-start | bytes 24580
  71.8 41.7 %all-to-all-start.1 = ((bf16[32,128,128]{2,1,0:T(8,128)(2,1)}), bf16[32,128,128]{2,1,0:T(8,128)(2,1)}, u32[]{:S(2)}, u32[]{:S(2)}) async-start(bf16[32,128,128]{2,1,0:T(8,128)(2,1)} %pad_maximum_fusion), calls=%async_computation.1 | async-start | bytes 2097152 | tf_op jit(solution)/shard_map/all_to_all | solution.py:156
  121.2 15.1 %all-to-all-start.2 = ((bf16[4,256,192]{1,2,0:T(8,128)(2,1)}), bf16[4,256,192]{1,2,0:T(8,128)(2,1)S(1)}, u32[]{:S(2)}, u32[]{:S(2)}) async-start(bf16[4,256,192]{1,2,0:T(8,128)(2,1)} %broadcast_in_dim.176), calls=%async_computation.2 | async-start | bytes 786432 | tf_op jit(solution)/shard_map/all_to_all | solution.py:84
  128.2 16.6 %copy-start.2 = (pred[256,1024]{0,1:T(8,128)(4,1)S(1)}, pred[256,1024]{0,1:T(8,128)(4,1)}, u32[]{:S(2)}) copy-start(pred[256,1024]{0,1:T(8,128)(4,1)} %get-tuple-element.36) | copy-start | bytes 786436
  138.5 12.4 %collective-permute-start = (bf16[1024,256]{1,0:T(8,128)(2,1)S(1)}, bf16[1024,256]{1,0:T(8,128)(2,1)S(1)}, u32[]{:S(2)}, u32[]{:S(2)}) collective-permute-start(bf16[1024,256]{1,0:T(8,128)(2,1)S(1)} %scatter_fusion), channel_id=1, source_target_pairs={{0,1},{1,2},{2,3},{3,4},{4,5},{5,6},{6,7},{7,8},{8,9},{9,10},{10,1... | collective-permute-start | bytes 1572872 | tf_op jit(solution)/shard_map/ppermute | solution.py:24
  153.6 4.5 %copy-start.1 = (f32[1024,256,4]{1,0,2:T(8,128)S(1)}, f32[1024,256,4]{1,0,2:T(8,128)}, u32[]{:S(2)}) copy-start(f32[1024,256,4]{1,0,2:T(8,128)} %get-tuple-element.56) | copy-start | bytes 12582916
  158.1 1.1 copy-start.8
  182.0 72.1 %all-to-all-start.4 = ((bf16[32,256,128]{2,1,0:T(8,128)(2,1)}), bf16[32,256,128]{2,1,0:T(8,128)(2,1)S(1)}, u32[]{:S(2)}, u32[]{:S(2)}) async-start(bf16[32,256,128]{2,1,0:T(8,128)(2,1)} %convert_bitcast_fusion), calls=%async_computation.4 | async-start | bytes 4194304 | tf_op jit(solution)/shard_map/all_to_all | solution.py:266
